TPU v7x, 256 devices: a whole 4x4x8 slice. The times are simulated.
256 devices in a mesh: dp: 16 (over x, y_hi, core), mp: 16 (over y_lo, z).
Axes of the slice: x: 4, y: 4 (y_hi: 2, y_lo: 2; y = y_hi * 2 + y_lo), z: 8, core: 2. Of those that a mesh axis runs over, the one named last changes fastest.
Arguments:
- tokens: bfloat16 [4096, 4096], P('dp'), may hold values from -32 to 32
- weights: bfloat16 [4096, 2, 3, 4096], P('dp', None, None, 'mp'), may hold values from -1 to 1
- block_modality: int32 [32], replicated, may hold values from 0 to 1
- doc_ids: int32 [4096], replicated, may hold values from 0 to 31, never falling along the last dimension, each value on 1 to 1024 neighbouring positions
- grad_out: bfloat16 [4096, 4096], P('dp', 'mp'), may hold values from -6 to 6
Outputs:
- attended: bfloat16 [4096, 4096], P('dp', 'mp')
- grad_tokens: bfloat16 [4096, 4096], P('dp', 'mp')
- grad_weights: bfloat16 [4096, 2, 3, 4096], P('dp', None, None, 'mp')
Inputs may be any that keep to these rules, and one draw needn't show every extreme that they name: doc_ids never falls along the sequence; a document is a run of equal ids of at most 1024 tokens, and one document has exactly 1024.
All inputs are finite; a program needn't handle non-finite values.
Results may differ from a plain program's by a relative error of at most 0.025.
Values may be sent and summed in bfloat16 or wider, within the bound.
No kernel may reach another device: no remote copies, remote signals or barrier semaphores. Data moves between devices by JAX's collectives and lax.ppermute only.
A program may use at most 128 MiB of HBM per device.

v0:
```python
import jax
import jax.numpy as jnp
from jax import lax
from jax.sharding import PartitionSpec as P

HD = 128
BLOCK = 128
SPAN = 4


def shifted(block, axis, distance):
    devices = range(lax.axis_size(axis))
    route = [(i - distance, i) for i in devices if i - distance in devices]
    return lax.ppermute(block, axis, route)


def select_product(block_rows, modality, text_mat, image_mat, contract):
    contraction = (((1,), (contract,)), ((), ()))
    return lax.cond(
        modality == 0,
        lambda: lax.dot_general(
            block_rows, text_mat, contraction, preferred_element_type=jnp.float32
        ),
        lambda: lax.dot_general(
            block_rows, image_mat, contraction, preferred_element_type=jnp.float32
        ),
    )


def blockwise(row_data, modalities, text_mat, image_mat, contract):
    blocks = row_data.reshape(modalities.shape[0], BLOCK, row_data.shape[1])

    def one_block(block_pair):
        return select_product(block_pair[0], block_pair[1], text_mat, image_mat, contract)

    result = lax.map(one_block, (blocks, modalities))
    return result.reshape(row_data.shape[0], result.shape[2])


def on_device(tokens, weights, block_modality, doc_ids, grad_out):
    local_rows = tokens.shape[0]
    width_rows = weights.shape[0]
    head_width = weights.shape[3]
    head_count = head_width // HD
    dp_devices = lax.axis_size("dp")
    local_blocks = local_rows // BLOCK
    front_pad = SPAN * local_rows
    window_len = front_pad + local_rows
    my_index = lax.axis_index("dp")
    scale_factor = HD ** (-0.5)
    my_mods = lax.dynamic_slice_in_dim(block_modality, my_index * local_blocks, local_blocks, 0)
    flat_weights = weights.reshape(width_rows, 2, 3 * head_width)
    text_local = flat_weights[:, 0]
    image_local = flat_weights[:, 1]
    columns = lax.all_to_all(tokens, "dp", split_axis=1, concat_axis=0, tiled=True)
    text_whole, image_whole = (
        lax.all_gather(text_local, "dp", axis=0, tiled=True),
        lax.all_gather(image_local, "dp", axis=0, tiled=True),
    )
    summed = blockwise(tokens, my_mods, text_whole, image_whole, 0)
    qkv = summed.astype(jnp.bfloat16).reshape(local_rows, 3, head_count, HD)
    queries = qkv[:, 0]
    key_values = qkv[:, 1:]
    received = []
    for distance in range(SPAN, 0, -1):
        received.append(shifted(key_values, "dp", distance))
    window = jnp.concatenate(received + [key_values], 0)
    key_rows = window[:, 0]
    value_rows = window[:, 1]
    docs_pad = jnp.concatenate([jnp.full((front_pad,), -1, jnp.int32), doc_ids], 0)
    key_docs = lax.dynamic_slice_in_dim(docs_pad, my_index * local_rows, window_len, 0)
    query_docs = lax.dynamic_slice_in_dim(doc_ids, my_index * local_rows, local_rows, 0)
    offsets = jnp.arange(window_len, dtype=jnp.int32) - front_pad
    allowed = (key_docs[None, :] == query_docs[:, None]) & (
        offsets[None, :] <= jnp.arange(local_rows, dtype=jnp.int32)[:, None]
    )
    scores = (
        jnp.einsum("qhd,khd->hqk", queries, key_rows, preferred_element_type=jnp.float32)
        * scale_factor
    )
    scores = jnp.where(allowed[None], scores, -1e30)
    top_score = jnp.max(scores, axis=-1, keepdims=True)
    expos = jnp.where(allowed[None], jnp.exp(scores - top_score), 0.0)
    probs_f = expos / jnp.sum(expos, axis=-1, keepdims=True)
    probs = probs_f.astype(jnp.bfloat16)
    attended = jnp.einsum("hqk,khd->qhd", probs, value_rows, preferred_element_type=jnp.float32)
    attended = attended.astype(jnp.bfloat16).reshape(local_rows, head_width)
    upstream = grad_out.reshape(local_rows, head_count, HD)
    dprob = jnp.einsum("qhd,khd->hqk", upstream, value_rows, preferred_element_type=jnp.float32)
    row_delta = jnp.sum(probs_f * dprob, axis=-1, keepdims=True)
    dscore = (probs_f * (dprob - row_delta)).astype(jnp.bfloat16)
    grad_q = (
        jnp.einsum("hqk,khd->qhd", dscore, key_rows, preferred_element_type=jnp.float32)
        * scale_factor
    )
    grad_k = (
        jnp.einsum("hqk,qhd->khd", dscore, queries, preferred_element_type=jnp.float32)
        * scale_factor
    )
    grad_v = jnp.einsum("hqk,qhd->khd", probs, upstream, preferred_element_type=jnp.float32)
    window_grads = jnp.stack([grad_k, grad_v], 1)
    own_grads = window_grads[front_pad:]
    for distance in range(1, SPAN + 1):
        lower_edge = front_pad - distance * local_rows
        sent_block = window_grads[lower_edge : lower_edge + local_rows]
        own_grads = own_grads + shifted(sent_block.astype(jnp.bfloat16), "dp", -distance).astype(
            sent_block.dtype
        )
    dqkv = (
        jnp.concatenate([grad_q[:, None], own_grads], 1)
        .astype(jnp.bfloat16)
        .reshape(local_rows, 3 * head_width)
    )
    gathered = lax.all_gather(dqkv, "dp", axis=0, tiled=True)
    column_groups = columns.reshape(dp_devices, local_blocks, BLOCK, width_rows)
    grad_groups = gathered.reshape(dp_devices, local_blocks, BLOCK, 3 * head_width)
    modality_groups = block_modality.reshape(dp_devices, local_blocks)
    modality_range = jnp.arange(2, dtype=jnp.int32)

    def accumulate(running, triple):
        column_group, grad_group, group_mods = triple
        per_block = jnp.einsum(
            "bnf,bnc->bfc", column_group, grad_group, preferred_element_type=jnp.float32
        )
        selector = (group_mods[:, None] == modality_range[None, :]).astype(jnp.float32)
        return (running + jnp.sum(selector[:, :, None, None] * per_block[:, None], axis=0), None)

    weight_sum, unused = lax.scan(
        accumulate,
        jnp.zeros((2, width_rows, 3 * head_width), jnp.float32),
        (column_groups, grad_groups, modality_groups),
    )
    grad_weights = (
        jnp.transpose(weight_sum, (1, 0, 2))
        .astype(jnp.bfloat16)
        .reshape(width_rows, 2, 3, head_width)
    )
    input_terms = blockwise(dqkv, my_mods, text_whole, image_whole, 1)
    grad_tokens = lax.psum_scatter(
        input_terms.astype(jnp.bfloat16), "mp", scatter_dimension=1, tiled=True
    )
    return (attended, grad_tokens, grad_weights)


def solution(mesh):
    return jax.shard_map(
        on_device,
        mesh=mesh,
        in_specs=(P("dp", None), P("dp", None, None, "mp"), P(), P(), P("dp", "mp")),
        out_specs=(P("dp", "mp"), P("dp", "mp"), P("dp", None, None, "mp")),
        check_vma=False,
    )
```

profile of v0, /device:TPU:6, one launch (start us, length us, event | category | flops | bytes accessed | tf_op | source)
XLA Modules:
  0.0 415.7 jit_solution(13535835044259661621)
XLA Ops:
  11.5 76.0 %all-gather.8.cloned.1.call-done = bf16[4096,1,768]{0,2,1:T(8,128)(2,1)} async-done(((bf16[256,1,768]{0,2,1:T(8,128)(2,1)}), bf16[4096,1,768]{0,2,1:T(8,128)(2,1)}) %all-gather.8.cloned.1.call-update) | async-done | bytes 6291472 | tf_op jit(solution)/shard_map/all_gather | solution.py:58
  87.6 8.6 %copy.59 = bf16[4096,768]{1,0:T(8,128)(2,1)} copy(bf16[4096,768]{0,1:T(8,128)(2,1)} %bitcast.114) | data formatting | bytes 12582912 | tf_op jit(solution)/shard_map/while | solution.py:36
  96.2 67.1 %all-gather.10.cloned.1.call-done = bf16[4096,1,768]{0,2,1:T(8,128)(2,1)} async-done(((bf16[256,1,768]{0,2,1:T(8,128)(2,1)}), bf16[4096,1,768]{0,2,1:T(8,128)(2,1)}) %all-gather.10.cloned.1.call-update) | async-done | bytes 6291472 | tf_op jit(solution)/shard_map/all_gather | solution.py:57
  163.3 8.8 %copy.60 = bf16[4096,768]{1,0:T(8,128)(2,1)} copy(bf16[4096,768]{0,1:T(8,128)(2,1)} %bitcast.115) | data formatting | bytes 12582912 | tf_op jit(solution)/shard_map/while | solution.py:36
  172.1 11.7 %while.31 = (s32[]{:T(128)}, bf16[2,128,768]{2,1,0:T(8,128)(2,1)}, s32[2]{0:T(128)S(1)}, bf16[2,128,4096]{2,1,0:T(8,128)(2,1)S(1)}, bf16[4096,768]{1,0:T(8,128)(...) while((s32[]{:T(128)}, bf16[2,128,768]{2,1,0:T(8,128)(2,1)}, s32[2]{0:T(128)S(1)}, ...), condition=%wide.region_3.4_spmd, body=%wide.region_0.3_spmd.sunk | while | flops 805306368 | bytes 10027175 | solution.py:36
  173.4 3.8 conditional.4
  173.4 3.8 convolution_bitcast_fusion.1
  179.3 3.8 conditional.4
  179.3 3.8 convolution_bitcast_fusion.1
  186.4 2.3 collective-permute-start.1
  193.8 2.5 collective-permute-done
  200.2 7.3 %collective-permute-done.2 = bf16[256,2,2,128]{3,0,2,1:T(8,128)(2,1)} collective-permute-done((bf16[256,2,2,128]{3,0,2,1:T(8,128)(2,1)S(1)}, bf16[256,2,2,128]{3,0,2,1:T(8,128)(2,1)}, u32[]{:S(2)}, u32[]{:S(2)}) %collective-permute-start.2) | collective-permute-done | bytes 262176 | tf_op jit(solution)/shard_map/ppermute | solution.py:14
  211.0 4.0 fusion.30
  215.0 2.7 multiply_reduce_fusion.1
  223.3 2.4 collective-permute-start.5
  225.6 5.6 %collective-permute-start.4 = (bf16[256,2,2,128]{0,3,2,1:T(8,128)(2,1)S(1)}, bf16[256,2,2,128]{0,3,2,1:T(8,128)(2,1)S(1)}, u32[]{:S(2)}, u32[]{:S(2)}) collective-permute-start(bf16[256,2,2,128]{0,3,2,1:T(8,128)(2,1)S(1)} %get-tuple-element.257), channel_id=1, source_target_pairs={{16,0},{32,16},{48,32},{64,48},{80,64},{96,80},{112,96},{128,112},... | collective-permute-start | bytes 786440 | tf_op jit(solution)/shard_map/ppermute | solution.py:14
  233.0 3.5 collective-permute-done.5
  236.4 2.8 collective-permute-done.4
  240.2 2.5 copy.72
  242.7 8.3 %all-to-all-start = ((bf16[256,16,256]{0,2,1:T(8,128)(2,1)}), bf16[256,16,256]{0,2,1:T(8,128)(2,1)}, u32[]{:S(2)}, u32[]{:S(2)}) async-start(bf16[256,16,256]{0,2,1:T(8,128)(2,1)} %bitcast.113), calls=%async_computation.1 | async-start | bytes 4194304 | tf_op jit(solution)/shard_map/all_to_all | solution.py:55
  251.3 33.1 %all-to-all-done = bf16[256,16,256]{0,2,1:T(8,128)(2,1)} async-done(((bf16[256,16,256]{0,2,1:T(8,128)(2,1)}), bf16[256,16,256]{0,2,1:T(8,128)(2,1)}, u32[]{:S(2)}, u32[]{:S(2)}) %all-to-all-start) | async-done | bytes 2097184 | tf_op jit(solution)/shard_map/all_to_all | solution.py:55
  284.4 3.9 copy.73
  288.4 2.6 convolution_convert_fusion
  292.3 14.6 %while.32 = (s32[]{:T(128)}, bf16[2,128,4096]{2,1,0:T(8,128)(2,1)}, s32[2]{0:T(128)S(1)}, bf16[2,128,768]{2,1,0:T(8,128)(2,1)S(1)}, bf16[4096,768]{1,0:T(8,128)(...) while((s32[]{:T(128)}, bf16[2,128,4096]{2,1,0:T(8,128)(2,1)}, s32[2]{0:T(128)S(1)}, ...), condition=%wide.region_10.11_spmd, body=%wide.region_7.10_spmd.sunk | while | flops 805306368 | bytes 10027175 | solution.py:36
  293.6 4.9 %conditional.5 = (bf16[1,128,4096]{2,1,0:T(8,128)(2,1)S(1)}) conditional(s32[]{:T(128)} %bitcast.106, (bf16[128,768]{1,0:T(8,128)(2,1)S(1)}, bf16[4096,768]{1,0:T(8,128)(2,1)}) %tuple.94, (bf16[128,768]{1,0:T(8,128)(2,1)S(1)}, bf16[4096,768]{1,0:T(8,128)(2,1)}) %tuple.95), branch_computations={%region_8.8_spmd, %region_9.9_spmd} | conditional | flops 805306368 | bytes 7536648 | solution.py:19
  293.6 4.9 %convolution_bitcast_fusion.3 = bf16[1,128,4096]{2,1,0:T(8,128)(2,1)S(1)} fusion(bf16[128,768]{1,0:T(8,128)(2,1)S(1)} %get-tuple-element.109, bf16[4096,768]{1,0:T(8,128)(2,1)} %get-tuple-element.110), kind=kOutput, calls=%fused_computation.6 | convolution fusion | flops 805306368 | bytes 7536640 | tf_op jit(solution)/shard_map/while/body/eval_jaxpr/cond/branch_1_fun/dot_general | solution.py:21
  300.8 4.9 %conditional.5 = (bf16[1,128,4096]{2,1,0:T(8,128)(2,1)S(1)}) conditional(s32[]{:T(128)} %bitcast.106, (bf16[128,768]{1,0:T(8,128)(2,1)S(1)}, bf16[4096,768]{1,0:T(8,128)(2,1)}) %tuple.94, (bf16[128,768]{1,0:T(8,128)(2,1)S(1)}, bf16[4096,768]{1,0:T(8,128)(2,1)}) %tuple.95), branch_computations={%region_8.8_spmd, %region_9.9_spmd} | conditional | flops 805306368 | bytes 7536648 | solution.py:19
  300.8 4.9 %convolution_bitcast_fusion.3 = bf16[1,128,4096]{2,1,0:T(8,128)(2,1)S(1)} fusion(bf16[128,768]{1,0:T(8,128)(2,1)S(1)} %get-tuple-element.109, bf16[4096,768]{1,0:T(8,128)(2,1)} %get-tuple-element.110), kind=kOutput, calls=%fused_computation.6 | convolution fusion | flops 805306368 | bytes 7536640 | tf_op jit(solution)/shard_map/while/body/eval_jaxpr/cond/branch_1_fun/dot_general | solution.py:21
  306.9 25.7 %all-gather.6.cloned.1.call-done = bf16[4096,768]{0,1:T(8,128)(2,1)} async-done(((bf16[256,768]{0,1:T(8,128)(2,1)}), bf16[4096,768]{0,1:T(8,128)(2,1)}) %all-gather.6.cloned.1.call-update) | async-done | bytes 6291472 | tf_op jit(solution)/shard_map/all_gather | solution.py:114
  332.7 8.6 %copy.74 = bf16[4096,768]{1,0:T(8,128)(2,1)} copy(bf16[4096,768]{0,1:T(8,128)(2,1)} %all-gather.6.cloned.1.call-done) | data formatting | bytes 12582912 | tf_op jit(solution)/shard_map/all_gather | solution.py:114
  341.3 39.1 %while.33 = (s32[]{:T(128)}, f32[2,256,768]{2,1,0:T(8,128)S(1)}, s32[16,2]{1,0:T(8,128)S(1)}, bf16[16,2,128,256]{3,2,1,0:T(8,128)(2,1)}, bf16[16,2,128,768]{3,2,1,0:T(8,128)(2,1)}, /*index=5*/s32[]{:T(128)}, s32[]{:T(128)}) while((s32[]{:T(128)}, f32[2,256,768]{2,1,0:T(8,128)S(1)}, s32[16,2]{1,0:T(8,128)S(1)}, ...), condition=%wide.region_14.15_spmd.clone, body=%wide.region_12.14_spmd.clone.sunk | while | flops 102629384 | bytes 9962651 | solution.py:128
  382.4 26.8 %reduce-scatter.2.cloned.1.call-done = bf16[256,256]{1,0:T(8,128)(2,1)} async-done(((bf16[256,4096]{1,0:T(8,128)(2,1)}), bf16[256,256]{1,0:T(8,128)(2,1)}) %reduce-scatter.2.cloned.1.call-update) | async-done | bytes 131088 | tf_op jit(solution)/shard_map/reduce_scatter | solution.py:139
  (156 shorter events, 75.6 us)
Async XLA Ops:
  7.2 4.1 copy-start.6
  7.2 4.2 %copy-start.5 = (s32[4096]{0:T(1024)S(1)}, s32[4096]{0:T(1024)}, u32[]{:S(2)}) copy-start(s32[4096]{0:T(1024)} %param.18) | copy-start | bytes 49156
  7.2 80.4 %all-gather.8.cloned.1.call-start = ((), (), s32[]{:S(2)}) async-start(), calls=%async_computation.4 | async-start | bytes 6684672 | tf_op jit(solution)/shard_map/all_gather | solution.py:58
  10.5 152.8 %all-gather.10.cloned.1.call-start = ((), (), s32[]{:S(2)}) async-start(), calls=%async_computation.5 | async-start | bytes 6684672 | tf_op jit(solution)/shard_map/all_gather | solution.py:57
  11.2 321.4 %all-gather.6.cloned.1.call-start = ((), (), s32[]{:S(2)}) async-start(), calls=%async_computation.3 | async-start | bytes 6684672 | tf_op jit(solution)/shard_map/all_gather | solution.py:114
  163.3 8.8 %copy-start = (bf16[256,4096]{1,0:T(8,128)(2,1)S(1)}, bf16[256,4096]{1,0:T(8,128)(2,1)}, u32[]{:S(2)}) copy-start(bf16[256,4096]{1,0:T(8,128)(2,1)} %param.15) | copy-start | bytes 6291460
  183.8 7.2 %copy-start.3 = (bf16[256,256]{1,0:T(8,128)(2,1)S(1)}, bf16[256,256]{1,0:T(8,128)(2,1)}, u32[]{:S(2)}) copy-start(bf16[256,256]{1,0:T(8,128)(2,1)} %param.19) | copy-start | bytes 393220
  185.1 11.1 %collective-permute-start = (bf16[256,2,2,128]{3,0,2,1:T(8,128)(2,1)S(1)}, bf16[256,2,2,128]{3,0,2,1:T(8,128)(2,1)}, u32[]{:S(2)}, u32[]{:S(2)}) collective-permute-start(bf16[256,2,2,128]{3,0,2,1:T(8,128)(2,1)S(1)} %copy.84), channel_id=1, source_target_pairs={{0,64},{16,80},{32,96},{48,112},{64,128},{80,144},{96,160},{112,17... | collective-permute-start | bytes 786440 | tf_op jit(solution)/shard_map/ppermute | solution.py:14
  186.4 12.0 %collective-permute-start.1 = (bf16[256,2,2,128]{3,0,2,1:T(8,128)(2,1)S(1)}, bf16[256,2,2,128]{3,0,2,1:T(8,128)(2,1)}, u32[]{:S(2)}, u32[]{:S(2)}) collective-permute-start(bf16[256,2,2,128]{3,0,2,1:T(8,128)(2,1)S(1)} %copy.84), channel_id=1, source_target_pairs={{0,48},{16,64},{32,80},{48,96},{64,112},{80,128},{96,144},{112,160... | collective-permute-start | bytes 786440 | tf_op jit(solution)/shard_map/ppermute | solution.py:14
  188.7 18.7 %collective-permute-start.2 = (bf16[256,2,2,128]{3,0,2,1:T(8,128)(2,1)S(1)}, bf16[256,2,2,128]{3,0,2,1:T(8,128)(2,1)}, u32[]{:S(2)}, u32[]{:S(2)}) collective-permute-start(bf16[256,2,2,128]{3,0,2,1:T(8,128)(2,1)S(1)} %copy.84), channel_id=1, source_target_pairs={{0,32},{16,48},{32,64},{48,80},{64,96},{80,112},{96,128},{112,144}... | collective-permute-start | bytes 786440 | tf_op jit(solution)/shard_map/ppermute | solution.py:14
  191.7 17.8 %collective-permute-start.3 = (bf16[256,2,2,128]{3,0,2,1:T(8,128)(2,1)S(1)}, bf16[256,2,2,128]{3,0,2,1:T(8,128)(2,1)S(1)}, u32[]{:S(2)}, u32[]{:S(2)}) collective-permute-start(bf16[256,2,2,128]{3,0,2,1:T(8,128)(2,1)S(1)} %copy.84), channel_id=1, source_target_pairs={{0,16},{16,32},{32,48},{48,64},{64,80},{80,96},{96,112},{112,128},... | collective-permute-start | bytes 786440 | tf_op jit(solution)/shard_map/ppermute | solution.py:14
  211.0 4.0 copy-start.4
  215.0 2.7 copy-start.2
  219.3 13.7 %collective-permute-start.7 = (bf16[256,2,2,128]{0,3,2,1:T(8,128)(2,1)S(1)}, bf16[256,2,2,128]{0,3,2,1:T(8,128)(2,1)S(1)}, u32[]{:S(2)}, u32[]{:S(2)}) collective-permute-start(bf16[256,2,2,128]{0,3,2,1:T(8,128)(2,1)S(1)} %get-tuple-element.258), channel_id=1, source_target_pairs={{64,0},{80,16},{96,32},{112,48},{128,64},{144,80},{160,96},{176,11... | collective-permute-start | bytes 786440 | tf_op jit(solution)/shard_map/ppermute | solution.py:14
  221.3 11.6 %collective-permute-start.6 = (bf16[256,2,2,128]{0,3,2,1:T(8,128)(2,1)S(1)}, bf16[256,2,2,128]{0,3,2,1:T(8,128)(2,1)S(1)}, u32[]{:S(2)}, u32[]{:S(2)}) collective-permute-start(bf16[256,2,2,128]{0,3,2,1:T(8,128)(2,1)S(1)} %get-tuple-element.259), channel_id=1, source_target_pairs={{48,0},{64,16},{80,32},{96,48},{112,64},{128,80},{144,96},{160,112... | collective-permute-start | bytes 786440 | tf_op jit(solution)/shard_map/ppermute | solution.py:14
  223.3 13.2 %collective-permute-start.5 = (bf16[256,2,2,128]{0,3,2,1:T(8,128)(2,1)S(1)}, bf16[256,2,2,128]{0,3,2,1:T(8,128)(2,1)S(1)}, u32[]{:S(2)}, u32[]{:S(2)}) collective-permute-start(bf16[256,2,2,128]{0,3,2,1:T(8,128)(2,1)S(1)} %get-tuple-element.260), channel_id=1, source_target_pairs={{32,0},{48,16},{64,32},{80,48},{96,64},{112,80},{128,96},{144,112}... | collective-permute-start | bytes 786440 | tf_op jit(solution)/shard_map/ppermute | solution.py:14
  225.6 13.6 %collective-permute-start.4 = (bf16[256,2,2,128]{0,3,2,1:T(8,128)(2,1)S(1)}, bf16[256,2,2,128]{0,3,2,1:T(8,128)(2,1)S(1)}, u32[]{:S(2)}, u32[]{:S(2)}) collective-permute-start(bf16[256,2,2,128]{0,3,2,1:T(8,128)(2,1)S(1)} %get-tuple-element.257), channel_id=1, source_target_pairs={{16,0},{32,16},{48,32},{64,48},{80,64},{96,80},{112,96},{128,112},... | collective-permute-start | bytes 786440 | tf_op jit(solution)/shard_map/ppermute | solution.py:14
  242.7 41.7 %all-to-all-start = ((bf16[256,16,256]{0,2,1:T(8,128)(2,1)}), bf16[256,16,256]{0,2,1:T(8,128)(2,1)}, u32[]{:S(2)}, u32[]{:S(2)}) async-start(bf16[256,16,256]{0,2,1:T(8,128)(2,1)} %bitcast.113), calls=%async_computation.1 | async-start | bytes 4194304 | tf_op jit(solution)/shard_map/all_to_all | solution.py:55
  251.0 158.2 %reduce-scatter.2.cloned.1.call-start = ((), (), s32[]{:S(2)}) async-start(), calls=%async_computation.2 | async-start | bytes 2228224 | tf_op jit(solution)/shard_map/reduce_scatter | solution.py:139
  288.4 3.4 copy-start.1
Sparse Core Ops, SparseCore 0:
  10.6 76.9 all-gather.7
  90.1 73.1 all-gather.9
  240.4 92.2 all-gather.5
  335.6 73.5 reduce-scatter.1
where the time goes:
time: 417 us; the launch traced here: 416 us
  waiting for transfers between devices  246 us (59%)
  local copies, waits for them, and re-layouts  54.6 us (13%)
  matrix products  52.8 us (13%)
  starting transfers between devices  28 us (7%)
  other arithmetic  16.4 us (4%)
  between operations  14 us (3%)
    all_gather x1, waiting for transfers between devices, on_device(): lax.all_gather(image_local, 'dp', axis=0, tiled=True)  76 us
    all_gather x1, waiting for transfers between devices, on_device(): lax.all_gather(text_local, 'dp', axis=0, tiled=True)  67.1 us
    all_to_all x1, waiting for transfers between devices, on_device(): lax.all_to_all(tokens, 'dp', split_axis=1, concat_axis=0, tiled=True)  33.1 us
    reduce_scatter x1, waiting for transfers between devices, on_device(): lax.psum_scatter(input_terms.astype(jnp.bfloat16), 'mp', scatter_dimensio...  26.8 us
    all_gather x1, waiting for transfers between devices, on_device(): gathered = lax.all_gather(dqkv, 'dp', axis=0, tiled=True)  25.7 us
    dot_general x16, matrix products, accumulate(): jnp.einsum('bnf,bnc->bfc', column_group, grad_group, preferred_element_ty...  23.6 us
    ppermute x8, starting transfers between devices, shifted(): return lax.ppermute(block, axis, route)  19.4 us
    while x3, local copies, waits for them, and re-layouts, blockwise(): result = lax.map(one_block, (blocks, modalities))  17.9 us
  transfers between devices with their start and end apart: 13, of which 11 were waited for; matrix products, arithmetic and copies ran while one was open for 22% of the time, Pallas kernels for 0%

commit v1 on v0

--- a/solution.py
+++ b/solution.py
@@ -14,27 +14,18 @@
     return lax.ppermute(block, axis, route)
 
 
-def select_product(block_rows, modality, text_mat, image_mat, contract):
-    contraction = (((1,), (contract,)), ((), ()))
-    return lax.cond(
-        modality == 0,
-        lambda: lax.dot_general(
-            block_rows, text_mat, contraction, preferred_element_type=jnp.float32
-        ),
-        lambda: lax.dot_general(
-            block_rows, image_mat, contraction, preferred_element_type=jnp.float32
-        ),
-    )
+def split_by_modality(rows, is_image):
+    zeros = jnp.zeros_like(rows)
+    text = jnp.where(is_image[:, None], zeros, rows)
+    image = jnp.where(is_image[:, None], rows, zeros)
+    return jnp.stack([text, image], axis=2).reshape(rows.shape[0], 2 * rows.shape[1])
 
 
-def blockwise(row_data, modalities, text_mat, image_mat, contract):
-    blocks = row_data.reshape(modalities.shape[0], BLOCK, row_data.shape[1])
-
-    def one_block(block_pair):
-        return select_product(block_pair[0], block_pair[1], text_mat, image_mat, contract)
-
-    result = lax.map(one_block, (blocks, modalities))
-    return result.reshape(row_data.shape[0], result.shape[2])
+def split_by_modality_major(rows, is_image):
+    zeros = jnp.zeros_like(rows)
+    text = jnp.where(is_image[:, None], zeros, rows)
+    image = jnp.where(is_image[:, None], rows, zeros)
+    return jnp.concatenate([text, image], axis=1)
 
 
 def on_device(tokens, weights, block_modality, doc_ids, grad_out):
@@ -43,21 +34,24 @@
     head_width = weights.shape[3]
     head_count = head_width // HD
     dp_devices = lax.axis_size("dp")
+    mp_devices = lax.axis_size("mp")
     local_blocks = local_rows // BLOCK
     front_pad = SPAN * local_rows
     window_len = front_pad + local_rows
     my_index = lax.axis_index("dp")
     scale_factor = HD ** (-0.5)
-    my_mods = lax.dynamic_slice_in_dim(block_modality, my_index * local_blocks, local_blocks, 0)
+    token_image = jnp.repeat(block_modality, BLOCK) == 1
+    my_image = lax.dynamic_slice_in_dim(token_image, my_index * local_rows, local_rows, 0)
+
     flat_weights = weights.reshape(width_rows, 2, 3 * head_width)
-    text_local = flat_weights[:, 0]
-    image_local = flat_weights[:, 1]
+    whole_weights = lax.all_gather(flat_weights, "dp", axis=0, tiled=True)
     columns = lax.all_to_all(tokens, "dp", split_axis=1, concat_axis=0, tiled=True)
-    text_whole, image_whole = (
-        lax.all_gather(text_local, "dp", axis=0, tiled=True),
-        lax.all_gather(image_local, "dp", axis=0, tiled=True),
+    whole_weights, columns = lax.optimization_barrier((whole_weights, columns))
+    stacked_weights = whole_weights.reshape(-1, 3 * head_width)
+
+    summed = jnp.dot(
+        split_by_modality(tokens, my_image), stacked_weights, preferred_element_type=jnp.float32
     )
-    summed = blockwise(tokens, my_mods, text_whole, image_whole, 0)
     qkv = summed.astype(jnp.bfloat16).reshape(local_rows, 3, head_count, HD)
     queries = qkv[:, 0]
     key_values = qkv[:, 1:]
@@ -111,34 +105,26 @@
         .astype(jnp.bfloat16)
         .reshape(local_rows, 3 * head_width)
     )
+
+    parts = lax.dot_general(
+        split_by_modality_major(dqkv, my_image),
+        whole_weights.reshape(whole_weights.shape[0], -1),
+        (((1,), (1,)), ((), ())),
+        preferred_element_type=jnp.float32,
+    ).astype(jnp.bfloat16)
+    group_parts = lax.all_to_all(
+        parts.reshape(local_rows, mp_devices, -1), "mp", split_axis=1, concat_axis=1, tiled=True
+    )
+    grad_tokens = jnp.sum(group_parts.astype(jnp.float32), axis=1).astype(jnp.bfloat16)
+
     gathered = lax.all_gather(dqkv, "dp", axis=0, tiled=True)
-    column_groups = columns.reshape(dp_devices, local_blocks, BLOCK, width_rows)
-    grad_groups = gathered.reshape(dp_devices, local_blocks, BLOCK, 3 * head_width)
-    modality_groups = block_modality.reshape(dp_devices, local_blocks)
-    modality_range = jnp.arange(2, dtype=jnp.int32)
-
-    def accumulate(running, triple):
-        column_group, grad_group, group_mods = triple
-        per_block = jnp.einsum(
-            "bnf,bnc->bfc", column_group, grad_group, preferred_element_type=jnp.float32
-        )
-        selector = (group_mods[:, None] == modality_range[None, :]).astype(jnp.float32)
-        return (running + jnp.sum(selector[:, :, None, None] * per_block[:, None], axis=0), None)
-
-    weight_sum, unused = lax.scan(
-        accumulate,
-        jnp.zeros((2, width_rows, 3 * head_width), jnp.float32),
-        (column_groups, grad_groups, modality_groups),
+    weight_sum = lax.dot_general(
+        columns,
+        split_by_modality_major(gathered, token_image),
+        (((0,), (0,)), ((), ())),
+        preferred_element_type=jnp.float32,
     )
-    grad_weights = (
-        jnp.transpose(weight_sum, (1, 0, 2))
-        .astype(jnp.bfloat16)
-        .reshape(width_rows, 2, 3, head_width)
-    )
-    input_terms = blockwise(dqkv, my_mods, text_whole, image_whole, 1)
-    grad_tokens = lax.psum_scatter(
-        input_terms.astype(jnp.bfloat16), "mp", scatter_dimension=1, tiled=True
-    )
+    grad_weights = weight_sum.astype(jnp.bfloat16).reshape(width_rows, 2, 3, head_width)
     return (attended, grad_tokens, grad_weights)
 
 

time: 417 us -> 318 us (0.76)
  the two profiles are of different devices: /device:TPU:6 before, /device:TPU:97 now
where the time goes in v1:
time: 318 us; the launch traced here: 316 us
  waiting for transfers between devices  199 us (63%)
  matrix products  36.8 us (12%)
  starting transfers between devices  33.5 us (11%)
  local copies, waits for them, and re-layouts  19.8 us (6%)
  between operations  14.3 us (4%)
  other arithmetic  12.6 us (4%)
    all_gather x1, waiting for transfers between devices, on_device(): whole_weights = lax.all_gather(flat_weights, 'dp', axis=0, tiled=True)  75.2 us
    all_to_all x1, waiting for transfers between devices, on_device(): lax.all_to_all(parts.reshape(local_rows, mp_devices, -1), 'mp', split_axi...  41.7 us
    all_to_all x1, waiting for transfers between devices, on_device(): lax.all_to_all(tokens, 'dp', split_axis=1, concat_axis=0, tiled=True)  33.3 us
    all_gather x1, waiting for transfers between devices, on_device(): gathered = lax.all_gather(dqkv, 'dp', axis=0, tiled=True)  32 us
    ppermute x8, starting transfers between devices, shifted(): return lax.ppermute(block, axis, route)  18 us
    ppermute x8, waiting for transfers between devices, shifted(): return lax.ppermute(block, axis, route)  16.8 us
    unnamed x21, local copies, waits for them, and re-layouts  11.2 us
    dot_general x1, matrix products, on_device(): lax.dot_general(columns, split_by_modality_major(gathered, token_image),...  9.92 us
  transfers between devices with their start and end apart: 12, of which 7 were waited for; matrix products, arithmetic and copies ran while one was open for 9% of the time, Pallas kernels for 0%

profile of v1, /device:TPU:97, one launch (start us, length us, event | category | flops | bytes accessed | tf_op | source)
XLA Modules:
  0.0 316.0 jit_solution(15968421403756851934)
XLA Ops:
  7.2 3.2 copy.46
  10.4 2.5 copy.47
  12.9 7.7 %all-to-all-start = ((bf16[256,16,256]{0,2,1:T(8,128)(2,1)}), bf16[256,16,256]{0,2,1:T(8,128)(2,1)}, u32[]{:S(2)}, u32[]{:S(2)}) async-start(bf16[256,16,256]{0,2,1:T(8,128)(2,1)} %bitcast.76), calls=%async_computation | async-start | bytes 4194304 | tf_op jit(solution)/shard_map/all_to_all | solution.py:48
  21.0 2.3 select_bitcast_fusion.1
  23.3 33.3 %all-to-all-done = bf16[256,16,256]{0,2,1:T(8,128)(2,1)} async-done(((bf16[256,16,256]{0,2,1:T(8,128)(2,1)}), bf16[256,16,256]{0,2,1:T(8,128)(2,1)}, u32[]{:S(2)}, u32[]{:S(2)}) %all-to-all-start) | async-done | bytes 2097184 | tf_op jit(solution)/shard_map/all_to_all | solution.py:48
  56.6 4.1 %copy.48 = bf16[16,256,256]{2,1,0:T(8,128)(2,1)} copy(bf16[16,256,256]{1,2,0:T(8,128)(2,1)} %bitcast.5) | data formatting | bytes 4194304 | tf_op jit(solution)/shard_map/all_to_all | solution.py:48
  60.7 75.2 %all-gather.3.cloned.1.call-done = bf16[4096,2,768]{0,2,1:T(8,128)(2,1)} async-done(((bf16[256,2,768]{0,2,1:T(8,128)(2,1)}), bf16[4096,2,768]{0,2,1:T(8,128)(2,1)}) %all-gather.3.cloned.1.call-update) | async-done | bytes 12582928 | tf_op jit(solution)/shard_map/all_gather | solution.py:47
  135.9 8.6 %fusion.22 = bf16[256,768]{1,0:T(8,128)(2,1)S(1)} fusion(bf16[4096,2,768]{0,2,1:T(8,128)(2,1)} %all-gather.3.cloned.1.call-done, bf16[256,4096,1]{1,0,2:T(8,128)(2,1)} %get-tuple-element.22, bf16[256,4096,1]{1,0,2:T(8,128)(2,1)S(1)} %copy-done.2), kind=kOutput, calls=%fused_computation.35 | convolution fusion | flops 3223519232 | bytes 17170432 | tf_op jit(solution)/shard_map/dot_general | solution.py:52
  144.9 2.8 collective-permute-start
  147.7 2.1 collective-permute-start.1
  149.7 2.1 collective-permute-start.2
  152.3 5.0 %collective-permute-start.3 = (bf16[256,2,2,128]{3,0,2,1:T(8,128)(2,1)S(1)}, bf16[256,2,2,128]{3,0,2,1:T(8,128)(2,1)S(1)}, u32[]{:S(2)}, u32[]{:S(2)}) collective-permute-start(bf16[256,2,2,128]{3,0,2,1:T(8,128)(2,1)S(1)} %copy.67), channel_id=1, source_target_pairs={{0,16},{16,32},{32,48},{48,64},{64,80},{80,96},{96,112},{112,128},... | collective-permute-start | bytes 786440 | tf_op jit(solution)/shard_map/ppermute | solution.py:14
  159.7 2.4 collective-permute-done.3
  163.6 2.5 fusion.45
  166.2 2.2 multiply_reduce_fusion
  169.9 1.3 collective-permute-start.7
  171.2 1.3 collective-permute-start.6
  172.5 1.3 collective-permute-start.5
  173.8 2.1 collective-permute-start.4
  175.9 1.7 fusion.26
  177.6 3.4 %collective-permute-done.7 = bf16[256,2,2,128]{0,3,2,1:T(8,128)(2,1)S(1)} collective-permute-done((bf16[256,2,2,128]{0,3,2,1:T(8,128)(2,1)S(1)}, bf16[256,2,2,128]{0,3,2,1:T(8,128)(2,1)S(1)}, u32[]{:S(2)}, u32[]{:S(2)}) %collective-permute-start.7) | collective-permute-done | bytes 262176 | tf_op jit(solution)/shard_map/ppermute | solution.py:14
  181.0 10.9 %collective-permute-done.6 = bf16[256,2,2,128]{0,3,2,1:T(8,128)(2,1)S(1)} collective-permute-done((bf16[256,2,2,128]{0,3,2,1:T(8,128)(2,1)S(1)}, bf16[256,2,2,128]{0,3,2,1:T(8,128)(2,1)S(1)}, u32[]{:S(2)}, u32[]{:S(2)}) %collective-permute-start.6) | collective-permute-done | bytes 262176 | tf_op jit(solution)/shard_map/ppermute | solution.py:14
  194.0 8.3 %convolution_convert_fusion = bf16[256,4096]{1,0:T(8,128)(2,1)S(1)} fusion(bf16[4096,1536]{0,1:T(8,128)(2,1)} %bitcast.74, bf16[256,768]{0,1:T(8,128)(2,1)S(1)} %get-tuple-element.28, bf16[256,768]{0,1:T(8,128)(2,1)S(1)} %get-tuple-element.27), kind=kOutput, calls=%fused_computation.7 | convolution fusion | flops 3223846912 | bytes 15466496 | tf_op jit(solution)/shard_map/dot_general | solution.py:109
  202.3 1.6 copy.82
  203.9 7.7 %all-to-all-start.1 = ((bf16[256,16,256]{2,0,1:T(8,128)(2,1)}), bf16[256,16,256]{2,0,1:T(8,128)(2,1)S(1)}, u32[]{:S(2)}, u32[]{:S(2)}) async-start(bf16[256,16,256]{2,0,1:T(8,128)(2,1)} %bitcast.77), calls=%async_computation.1 | async-start | bytes 4194304 | tf_op jit(solution)/shard_map/all_to_all | solution.py:115
  211.6 2.8 convolution_convert_fusion.1
  215.1 41.7 %all-to-all-done.1 = bf16[256,16,256]{2,0,1:T(8,128)(2,1)S(1)} async-done(((bf16[256,16,256]{2,0,1:T(8,128)(2,1)}), bf16[256,16,256]{2,0,1:T(8,128)(2,1)S(1)}, u32[]{:S(2)}, u32[]{:S(2)}) %all-to-all-start.1) | async-done | bytes 2097184 | tf_op jit(solution)/shard_map/all_to_all | solution.py:115
  257.8 32.0 %all-gather.5.cloned.1.call-done = bf16[4096,768]{0,1:T(8,128)(2,1)} async-done(((bf16[256,768]{0,1:T(8,128)(2,1)}), bf16[4096,768]{0,1:T(8,128)(2,1)}) %all-gather.5.cloned.1.call-update) | async-done | bytes 6291472 | tf_op jit(solution)/shard_map/all_gather | solution.py:120
  289.8 6.3 %broadcast_select_fusion.1 = (bf16[4096,768]{0,1:T(8,128)(2,1)S(1)}, bf16[4096,768]{0,1:T(8,128)(2,1)}) fusion(bf16[4096,768]{0,1:T(8,128)(2,1)} %all-gather.5.cloned.1.call-done, pred[4096]{0:T(1024)(128)(4,1)S(1)} %broadcast_bitcast_fusion), kind=kLoop, calls=%fused_computation.6 | loop fusion | flops 6291456 | bytes 18878464 | tf_op jit(solution)/shard_map/jit(_where)/select_n | solution.py:26
  296.1 9.9 %fusion.15 = bf16[256,1536]{1,0:T(8,128)(2,1)} fusion(bf16[4096,256]{1,0:T(8,128)(2,1)} %bitcast.81, bf16[4096,768]{0,1:T(8,128)(2,1)} %get-tuple-element.20, bf16[4096,768]{0,1:T(8,128)(2,1)S(1)} %get-tuple-element.19), kind=kOutput, calls=%fused_computation.27 | convolution fusion | flops 3246784512 | bytes 15466496 | tf_op jit(solution)/shard_map/dot_general | solution.py:121
  306.0 1.4 copy.59
  307.4 1.8 copy.61
  (47 shorter events, 10.3 us)
Async XLA Ops:
  7.2 3.2 %copy-start = (bf16[256,4096]{1,0:T(8,128)(2,1)S(1)}, bf16[256,4096]{1,0:T(8,128)(2,1)}, u32[]{:S(2)}) copy-start(bf16[256,4096]{1,0:T(8,128)(2,1)} %param.5) | copy-start | bytes 6291460
  7.2 128.7 %all-gather.3.cloned.1.call-start = ((), (), s32[]{:S(2)}) async-start(), calls=%async_computation.2 | async-start | bytes 13369344 | tf_op jit(solution)/shard_map/all_gather | solution.py:47
  12.9 7.8 %copy-start.5 = (s32[32]{0:T(128)S(1)}, s32[32]{0:T(128)}, u32[]{:S(2)}) copy-start(s32[32]{0:T(128)} %param.7) | copy-start | bytes 388
  12.9 8.0 %copy-start.4 = (s32[4096]{0:T(1024)S(1)}, s32[4096]{0:T(1024)}, u32[]{:S(2)}) copy-start(s32[4096]{0:T(1024)} %param.8) | copy-start | bytes 49156
  12.9 43.7 %all-to-all-start = ((bf16[256,16,256]{0,2,1:T(8,128)(2,1)}), bf16[256,16,256]{0,2,1:T(8,128)(2,1)}, u32[]{:S(2)}, u32[]{:S(2)}) async-start(bf16[256,16,256]{0,2,1:T(8,128)(2,1)} %bitcast.76), calls=%async_computation | async-start | bytes 4194304 | tf_op jit(solution)/shard_map/all_to_all | solution.py:48
  20.6 269.2 %all-gather.5.cloned.1.call-start = ((), (), s32[]{:S(2)}) async-start(), calls=%async_computation.3 | async-start | bytes 6684672 | tf_op jit(solution)/shard_map/all_gather | solution.py:120
  56.6 79.2 %copy-start.2 = (bf16[256,4096,1]{1,0,2:T(8,128)(2,1)S(1)}, bf16[256,4096,1]{1,0,2:T(8,128)(2,1)}, u32[]{:S(2)}) copy-start(bf16[256,4096,1]{1,0,2:T(8,128)(2,1)} %get-tuple-element.21) | copy-start | bytes 6291460
  144.5 7.7 %copy-start.3 = (bf16[256,256]{1,0:T(8,128)(2,1)S(1)}, bf16[256,256]{1,0:T(8,128)(2,1)}, u32[]{:S(2)}) copy-start(bf16[256,256]{1,0:T(8,128)(2,1)} %param.9) | copy-start | bytes 393220
  144.9 12.6 %collective-permute-start = (bf16[256,2,2,128]{3,0,2,1:T(8,128)(2,1)S(1)}, bf16[256,2,2,128]{3,0,2,1:T(8,128)(2,1)S(1)}, u32[]{:S(2)}, u32[]{:S(2)}) collective-permute-start(bf16[256,2,2,128]{3,0,2,1:T(8,128)(2,1)S(1)} %copy.67), channel_id=1, source_target_pairs={{0,64},{16,80},{32,96},{48,112},{64,128},{80,144},{96,160},{112,17... | collective-permute-start | bytes 786440 | tf_op jit(solution)/shard_map/ppermute | solution.py:14
  147.7 10.5 %collective-permute-start.1 = (bf16[256,2,2,128]{3,0,2,1:T(8,128)(2,1)S(1)}, bf16[256,2,2,128]{3,0,2,1:T(8,128)(2,1)S(1)}, u32[]{:S(2)}, u32[]{:S(2)}) collective-permute-start(bf16[256,2,2,128]{3,0,2,1:T(8,128)(2,1)S(1)} %copy.67), channel_id=1, source_target_pairs={{0,48},{16,64},{32,80},{48,96},{64,112},{80,128},{96,144},{112,160... | collective-permute-start | bytes 786440 | tf_op jit(solution)/shard_map/ppermute | solution.py:14
  149.7 9.2 %collective-permute-start.2 = (bf16[256,2,2,128]{3,0,2,1:T(8,128)(2,1)S(1)}, bf16[256,2,2,128]{3,0,2,1:T(8,128)(2,1)S(1)}, u32[]{:S(2)}, u32[]{:S(2)}) collective-permute-start(bf16[256,2,2,128]{3,0,2,1:T(8,128)(2,1)S(1)} %copy.67), channel_id=1, source_target_pairs={{0,32},{16,48},{32,64},{48,80},{64,96},{80,112},{96,128},{112,144}... | collective-permute-start | bytes 786440 | tf_op jit(solution)/shard_map/ppermute | solution.py:14
  152.3 9.8 %collective-permute-start.3 = (bf16[256,2,2,128]{3,0,2,1:T(8,128)(2,1)S(1)}, bf16[256,2,2,128]{3,0,2,1:T(8,128)(2,1)S(1)}, u32[]{:S(2)}, u32[]{:S(2)}) collective-permute-start(bf16[256,2,2,128]{3,0,2,1:T(8,128)(2,1)S(1)} %copy.67), channel_id=1, source_target_pairs={{0,16},{16,32},{32,48},{48,64},{64,80},{80,96},{96,112},{112,128},... | collective-permute-start | bytes 786440 | tf_op jit(solution)/shard_map/ppermute | solution.py:14
  166.1 2.6 copy-start.1
  169.9 11.1 %collective-permute-start.7 = (bf16[256,2,2,128]{0,3,2,1:T(8,128)(2,1)S(1)}, bf16[256,2,2,128]{0,3,2,1:T(8,128)(2,1)S(1)}, u32[]{:S(2)}, u32[]{:S(2)}) collective-permute-start(bf16[256,2,2,128]{0,3,2,1:T(8,128)(2,1)S(1)} %get-tuple-element.24), channel_id=1, source_target_pairs={{64,0},{80,16},{96,32},{112,48},{128,64},{144,80},{160,96},{176,11... | collective-permute-start | bytes 786440 | tf_op jit(solution)/shard_map/ppermute | solution.py:14
  171.2 20.7 %collective-permute-start.6 = (bf16[256,2,2,128]{0,3,2,1:T(8,128)(2,1)S(1)}, bf16[256,2,2,128]{0,3,2,1:T(8,128)(2,1)S(1)}, u32[]{:S(2)}, u32[]{:S(2)}) collective-permute-start(bf16[256,2,2,128]{0,3,2,1:T(8,128)(2,1)S(1)} %get-tuple-element.25), channel_id=1, source_target_pairs={{48,0},{64,16},{80,32},{96,48},{112,64},{128,80},{144,96},{160,112... | collective-permute-start | bytes 786440 | tf_op jit(solution)/shard_map/ppermute | solution.py:14
  172.5 19.4 %collective-permute-start.5 = (bf16[256,2,2,128]{0,3,2,1:T(8,128)(2,1)S(1)}, bf16[256,2,2,128]{0,3,2,1:T(8,128)(2,1)S(1)}, u32[]{:S(2)}, u32[]{:S(2)}) collective-permute-start(bf16[256,2,2,128]{0,3,2,1:T(8,128)(2,1)S(1)} %get-tuple-element.26), channel_id=1, source_target_pairs={{32,0},{48,16},{64,32},{80,48},{96,64},{112,80},{128,96},{144,112}... | collective-permute-start | bytes 786440 | tf_op jit(solution)/shard_map/ppermute | solution.py:14
  173.8 18.1 %collective-permute-start.4 = (bf16[256,2,2,128]{0,3,2,1:T(8,128)(2,1)S(1)}, bf16[256,2,2,128]{0,3,2,1:T(8,128)(2,1)S(1)}, u32[]{:S(2)}, u32[]{:S(2)}) collective-permute-start(bf16[256,2,2,128]{0,3,2,1:T(8,128)(2,1)S(1)} %get-tuple-element.23), channel_id=1, source_target_pairs={{16,0},{32,16},{48,32},{64,48},{80,64},{96,80},{112,96},{128,112},... | collective-permute-start | bytes 786440 | tf_op jit(solution)/shard_map/ppermute | solution.py:14
  203.9 52.9 %all-to-all-start.1 = ((bf16[256,16,256]{2,0,1:T(8,128)(2,1)}), bf16[256,16,256]{2,0,1:T(8,128)(2,1)S(1)}, u32[]{:S(2)}, u32[]{:S(2)}) async-start(bf16[256,16,256]{2,0,1:T(8,128)(2,1)} %bitcast.77), calls=%async_computation.1 | async-start | bytes 4194304 | tf_op jit(solution)/shard_map/all_to_all | solution.py:115
Sparse Core Ops, SparseCore 0:
  11.1 124.6 all-gather.2
  193.1 96.6 all-gather.4

commit v2 on v1

--- a/solution.py
+++ b/solution.py
@@ -28,6 +28,20 @@
     return jnp.concatenate([text, image], axis=1)
 
 
+def dp_ring(size):
+    if size % 4:
+        return list(range(size))
+    chips = size // 2
+    order = [2 * x for x in range(chips // 2)] + [2 * x + 1 for x in reversed(range(chips // 2))]
+    return [2 * chip + core for chip in order for core in range(2)]
+
+
+def ring_blocks(rows, ring, axis):
+    shape = rows.shape
+    blocks = rows.reshape(shape[:axis] + (len(ring), shape[axis] // len(ring)) + shape[axis + 1 :])
+    return jnp.take(blocks, jnp.array(ring, jnp.int32), axis=axis).reshape(shape)
+
+
 def on_device(tokens, weights, block_modality, doc_ids, grad_out):
     local_rows = tokens.shape[0]
     width_rows = weights.shape[0]
@@ -43,15 +57,23 @@
     token_image = jnp.repeat(block_modality, BLOCK) == 1
     my_image = lax.dynamic_slice_in_dim(token_image, my_index * local_rows, local_rows, 0)
 
+    ring = dp_ring(dp_devices)
+    inverse = [ring.index(k) for k in range(dp_devices)]
     flat_weights = weights.reshape(width_rows, 2, 3 * head_width)
-    whole_weights = lax.all_gather(flat_weights, "dp", axis=0, tiled=True)
+    whole_weights = lax.all_gather(
+        flat_weights, "dp", axis=0, tiled=True, axis_index_groups=[ring]
+    )
     columns = lax.all_to_all(tokens, "dp", split_axis=1, concat_axis=0, tiled=True)
-    whole_weights, columns = lax.optimization_barrier((whole_weights, columns))
+    ring_columns = split_by_modality_major(
+        ring_blocks(columns, ring, 0), ring_blocks(token_image, ring, 0)
+    )
+    ring_tokens = split_by_modality(ring_blocks(tokens, ring, 1), my_image)
+    whole_weights, ring_columns, ring_tokens = lax.optimization_barrier(
+        (whole_weights, ring_columns, ring_tokens)
+    )
     stacked_weights = whole_weights.reshape(-1, 3 * head_width)
 
-    summed = jnp.dot(
-        split_by_modality(tokens, my_image), stacked_weights, preferred_element_type=jnp.float32
-    )
+    summed = jnp.dot(ring_tokens, stacked_weights, preferred_element_type=jnp.float32)
     qkv = summed.astype(jnp.bfloat16).reshape(local_rows, 3, head_count, HD)
     queries = qkv[:, 0]
     key_values = qkv[:, 1:]
@@ -112,19 +134,25 @@
         (((1,), (1,)), ((), ())),
         preferred_element_type=jnp.float32,
     ).astype(jnp.bfloat16)
+    parts = ring_blocks(parts, inverse, 1)
     group_parts = lax.all_to_all(
         parts.reshape(local_rows, mp_devices, -1), "mp", split_axis=1, concat_axis=1, tiled=True
     )
     grad_tokens = jnp.sum(group_parts.astype(jnp.float32), axis=1).astype(jnp.bfloat16)
 
-    gathered = lax.all_gather(dqkv, "dp", axis=0, tiled=True)
+    gathered = lax.all_gather(dqkv, "dp", axis=0, tiled=True, axis_index_groups=[ring])
     weight_sum = lax.dot_general(
-        columns,
-        split_by_modality_major(gathered, token_image),
+        ring_columns,
+        gathered,
         (((0,), (0,)), ((), ())),
         preferred_element_type=jnp.float32,
     )
-    grad_weights = weight_sum.astype(jnp.bfloat16).reshape(width_rows, 2, 3, head_width)
+    grad_weights = (
+        weight_sum.astype(jnp.bfloat16)
+        .reshape(2, width_rows, 3 * head_width)
+        .transpose(1, 0, 2)
+        .reshape(width_rows, 2, 3, head_width)
+    )
     return (attended, grad_tokens, grad_weights)
 
 

time: 318 us -> 311 us (0.978)
  waiting for transfers between devices: 199 us -> 106 us
  local copies, waits for them, and re-layouts: 19.8 us -> 103 us
  other arithmetic: 12.6 us -> 8.25 us
    all_gather x2, waiting for transfers between devices: 107 us -> 36.5 us  [the longest x1 36.5 us: on_device(): lax.all_gather(flat_weights, 'dp', axis=0, tiled=True, axis_index_groups=...]
    reshape x1 -> x5, local copies, waits for them, and re-layouts: 1.55 us -> 35.7 us  [the longest x1 26.2 us: on_device(): stacked_weights = whole_weights.reshape(-1, 3 * head_width)]
    all_to_all x1, waiting for transfers between devices: 33.3 us -> 0.77 us  [on_device(): lax.all_to_all(tokens, 'dp', split_axis=1, concat_axis=0, tiled=True)]
    another operation x0 -> x1, local copies, waits for them, and re-layouts: none -> 27.2 us  [split_by_modality(): jnp.stack([text, image], axis=2).reshape(rows.shape[0], 2 * rows.shape[1])]
    unnamed x21 -> x25, local copies, waits for them, and re-layouts: 11.2 us -> 24.4 us
    gather x0 -> x5, local copies, waits for them, and re-layouts: none -> 11.8 us  [ring_blocks(): jnp.take(blocks, jnp.array(ring, jnp.int32), axis=axis).reshape(shape)]
    ppermute x8, waiting for transfers between devices: 16.8 us -> 24 us  [shifted(): return lax.ppermute(block, axis, route)]
    select_n x2, other arithmetic: 7.33 us -> 2.23 us  [split_by_modality_major(): text = jnp.where(is_image[:, None], zeros, rows)]
  transfers between devices with their start and end apart: 12 -> 12, of which waited for: 7 -> 8; matrix products, arithmetic and copies ran while one was open for 9% -> 30% of each run, Pallas kernels for 0% -> 0%
where the time goes in v2:
time: 311 us; the launch traced here: 306 us
  waiting for transfers between devices  106 us (34%)
  local copies, waits for them, and re-layouts  103 us (33%)
  matrix products  39.7 us (13%)
  starting transfers between devices  34.8 us (11%)
  between operations  14.4 us (5%)
  other arithmetic  8.25 us (3%)
    all_to_all x1, waiting for transfers between devices, on_device(): lax.all_to_all(parts.reshape(local_rows, mp_devices, -1), 'mp', split_axi...  44.4 us
    all_gather x1, waiting for transfers between devices, on_device(): lax.all_gather(flat_weights, 'dp', axis=0, tiled=True, axis_index_groups=...  36.5 us
    another operation x1, local copies, waits for them, and re-layouts, split_by_modality(): jnp.stack([text, image], axis=2).reshape(rows.shape[0], 2 * rows.shape[1])  27.2 us
    reshape x1, local copies, waits for them, and re-layouts, on_device(): stacked_weights = whole_weights.reshape(-1, 3 * head_width)  26.2 us
    unnamed x25, local copies, waits for them, and re-layouts  24.4 us
    ppermute x8, waiting for transfers between devices, shifted(): return lax.ppermute(block, axis, route)  24 us
    ppermute x8, starting transfers between devices, shifted(): return lax.ppermute(block, axis, route)  20.1 us
    dot_general x1, matrix products, on_device(): lax.dot_general(split_by_modality_major(dqkv, my_image), whole_weights.re...  13.2 us
  transfers between devices with their start and end apart: 12, of which 8 were waited for; matrix products, arithmetic and copies ran while one was open for 30% of the time, Pallas kernels for 0%

profile of v2, /device:TPU:97, one launch (start us, length us, event | category | flops | bytes accessed | tf_op | source)
XLA Modules:
  0.0 306.1 jit_solution(8922575909115064053)
XLA Ops:
  7.2 2.2 copy.68
  11.3 3.3 %copy.70 = bf16[256,4096]{0,1:T(8,128)(2,1)S(1)} copy(bf16[256,4096]{1,0:T(8,128)(2,1)} %param.11) | data formatting | bytes 4194304 | tf_op args[0]
  14.6 2.4 copy.71
  16.9 7.7 %all-to-all-start = ((bf16[256,16,256]{2,0,1:T(8,128)(2,1)}), bf16[256,16,256]{2,0,1:T(8,128)(2,1)}, u32[]{:S(2)}, u32[]{:S(2)}) async-start(bf16[256,16,256]{2,0,1:T(8,128)(2,1)} %copy.71), calls=%async_computation | async-start | bytes 4194304 | tf_op jit(solution)/shard_map/all_to_all | solution.py:66
  24.8 4.1 %gather_fusion.2 = bf16[16,256,256]{2,1,0:T(8,128)(2,1)} fusion(bf16[256,16,256]{2,0,1:T(8,128)(2,1)} %copy.71, s32[1024]{0:T(1024)S(1)} %pad_clamp_fusion.1), kind=kCustom, calls=%fused_computation.clone | custom fusion | bytes 4194368 | tf_op jit(solution)/shard_map/jit(_take)/gather | solution.py:42
  28.9 2.8 copy.73
  32.8 27.2 %copy.74 = bf16[256,4096,2]{0,2,1:T(2,128)(2,1)} copy(bf16[256,4096,2]{0,1,2:T(8,128)(2,1)S(1)} %pad_maximum_fusion.1) | data formatting | bytes 8388608 | tf_op jit(solution)/shard_map/stack | solution.py:21
  60.0 7.2 %reshape.209 = bf16[256,8192]{0,1:T(8,128)(2,1)} reshape(bf16[256,4096,2]{0,2,1:T(2,128)(2,1)} %copy.74) | data formatting | bytes 8388608 | tf_op jit(solution)/shard_map/reshape | solution.py:21
  68.9 2.3 gather_fusion.1
  71.2 2.1 bitcast_select_fusion.2
  73.4 2.3 pad_maximum_fusion
  75.6 36.5 %all-gather.3.cloned.1.call-done = bf16[4096,2,768]{2,1,0:T(2,128)(2,1)} async-done(((bf16[256,2,768]{2,1,0:T(2,128)(2,1)}), bf16[4096,2,768]{2,1,0:T(2,128)(2,1)}) %all-gather.3.cloned.1.call-update) | async-done | bytes 12582928 | tf_op jit(solution)/shard_map/all_gather | solution.py:63
  112.1 26.2 %reshape.210 = bf16[8192,768]{1,0:T(8,128)(2,1)} reshape(bf16[4096,2,768]{2,1,0:T(2,128)(2,1)} %all-gather.3.cloned.1.call-done) | data formatting | bytes 25165824 | tf_op jit(solution)/shard_map/reshape | solution.py:74
  138.3 9.3 %convolution_convert_fusion.2 = bf16[256,768]{1,0:T(8,128)(2,1)S(1)} fusion(bf16[256,8192]{0,1:T(8,128)(2,1)} %reshape.209, bf16[8192,768]{1,0:T(8,128)(2,1)} %reshape.210), kind=kOutput, calls=%fused_computation.32 | convolution fusion | flops 3221422080 | bytes 17170432 | tf_op jit(solution)/shard_map/dot_general | solution.py:76
  149.4 3.2 %collective-permute-start.1 = (bf16[256,2,2,128]{3,0,2,1:T(8,128)(2,1)S(1)}, bf16[256,2,2,128]{3,0,2,1:T(8,128)(2,1)S(1)}, u32[]{:S(2)}, u32[]{:S(2)}) collective-permute-start(bf16[256,2,2,128]{3,0,2,1:T(8,128)(2,1)S(1)} %copy.91), channel_id=1, source_target_pairs={{0,48},{16,64},{32,80},{48,96},{64,112},{80,128},{96,144},{112,160... | collective-permute-start | bytes 786440 | tf_op jit(solution)/shard_map/ppermute | solution.py:14
  152.6 4.8 %collective-permute-start.2 = (bf16[256,2,2,128]{3,0,2,1:T(8,128)(2,1)S(1)}, bf16[256,2,2,128]{3,0,2,1:T(8,128)(2,1)S(1)}, u32[]{:S(2)}, u32[]{:S(2)}) collective-permute-start(bf16[256,2,2,128]{3,0,2,1:T(8,128)(2,1)S(1)} %copy.91), channel_id=1, source_target_pairs={{0,32},{16,48},{32,64},{48,80},{64,96},{80,112},{96,128},{112,144}... | collective-permute-start | bytes 786440 | tf_op jit(solution)/shard_map/ppermute | solution.py:14
  157.8 4.9 %collective-permute-start.3 = (bf16[256,2,2,128]{3,0,2,1:T(8,128)(2,1)S(1)}, bf16[256,2,2,128]{3,0,2,1:T(8,128)(2,1)S(1)}, u32[]{:S(2)}, u32[]{:S(2)}) collective-permute-start(bf16[256,2,2,128]{3,0,2,1:T(8,128)(2,1)S(1)} %copy.91), channel_id=1, source_target_pairs={{0,16},{16,32},{32,48},{48,64},{64,80},{80,96},{96,112},{112,128},... | collective-permute-start | bytes 786440 | tf_op jit(solution)/shard_map/ppermute | solution.py:14
  167.9 2.5 fusion.26
  170.4 2.2 multiply_reduce_fusion
  174.2 1.9 collective-permute-start.4
  181.7 3.3 %collective-permute-done.4 = bf16[256,2,2,128]{0,3,2,1:T(8,128)(2,1)S(1)} collective-permute-done((bf16[256,2,2,128]{0,3,2,1:T(8,128)(2,1)S(1)}, bf16[256,2,2,128]{0,3,2,1:T(8,128)(2,1)S(1)}, u32[]{:S(2)}, u32[]{:S(2)}) %collective-permute-start.4) | collective-permute-done | bytes 262176 | tf_op jit(solution)/shard_map/ppermute | solution.py:14
  185.1 5.9 %collective-permute-done.5 = bf16[256,2,2,128]{0,3,2,1:T(8,128)(2,1)S(1)} collective-permute-done((bf16[256,2,2,128]{0,3,2,1:T(8,128)(2,1)S(1)}, bf16[256,2,2,128]{0,3,2,1:T(8,128)(2,1)S(1)}, u32[]{:S(2)}, u32[]{:S(2)}) %collective-permute-start.5) | collective-permute-done | bytes 262176 | tf_op jit(solution)/shard_map/ppermute | solution.py:14
  190.9 9.6 %collective-permute-done.6 = bf16[256,2,2,128]{0,3,2,1:T(8,128)(2,1)S(1)} collective-permute-done((bf16[256,2,2,128]{0,3,2,1:T(8,128)(2,1)S(1)}, bf16[256,2,2,128]{0,3,2,1:T(8,128)(2,1)S(1)}, u32[]{:S(2)}, u32[]{:S(2)}) %collective-permute-start.6) | collective-permute-done | bytes 262176 | tf_op jit(solution)/shard_map/ppermute | solution.py:14
  200.6 3.9 %collective-permute-done.7 = bf16[256,2,2,128]{0,3,2,1:T(8,128)(2,1)S(1)} collective-permute-done((bf16[256,2,2,128]{0,3,2,1:T(8,128)(2,1)S(1)}, bf16[256,2,2,128]{0,3,2,1:T(8,128)(2,1)S(1)}, u32[]{:S(2)}, u32[]{:S(2)}) %collective-permute-start.7) | collective-permute-done | bytes 262176 | tf_op jit(solution)/shard_map/ppermute | solution.py:14
  205.5 13.1 %copy.96 = bf16[512,8,2,768]{3,1,2,0:T(8,128)(2,1)} copy(bf16[512,8,2,768]{3,2,1,0:T(2,128)(2,1)} %bitcast.85) | data formatting | bytes 25165824
  218.7 13.2 %convolution_convert_fusion = bf16[256,4096]{1,0:T(8,128)(2,1)S(1)} fusion(bf16[4096,1536]{1,0:T(8,128)(2,1)} %bitcast.86, bf16[256,768]{0,1:T(8,128)(2,1)S(1)} %get-tuple-element.34, bf16[256,768]{0,1:T(8,128)(2,1)S(1)} %get-tuple-element.33), kind=kOutput, calls=%fused_computation.5 | convolution fusion | flops 3223846912 | bytes 15466496 | tf_op jit(solution)/shard_map/dot_general | solution.py:131
  232.1 2.0 gather_fusion.3
  234.1 6.8 %all-to-all-start.1 = ((bf16[256,16,256]{2,0,1:T(8,128)(2,1)}), bf16[256,16,256]{2,0,1:T(8,128)(2,1)S(1)}, u32[]{:S(2)}, u32[]{:S(2)}) async-start(bf16[256,16,256]{2,0,1:T(8,128)(2,1)} %bitcast.87), calls=%async_computation.1 | async-start | bytes 4194304 | tf_op jit(solution)/shard_map/all_to_all | solution.py:138
  240.9 2.6 convolution_convert_fusion.3
  244.3 44.4 %all-to-all-done.1 = bf16[256,16,256]{2,0,1:T(8,128)(2,1)S(1)} async-done(((bf16[256,16,256]{2,0,1:T(8,128)(2,1)}), bf16[256,16,256]{2,0,1:T(8,128)(2,1)S(1)}, u32[]{:S(2)}, u32[]{:S(2)}) %all-to-all-start.1) | async-done | bytes 2097184 | tf_op jit(solution)/shard_map/all_to_all | solution.py:138
  289.6 7.5 %convolution_convert_fusion.1 = bf16[512,768]{1,0:T(8,128)(2,1)S(1)} fusion(bf16[4096,512]{1,0:T(8,128)(2,1)} %pad_maximum_fusion, bf16[4096,768]{0,1:T(8,128)(2,1)} %all-gather.5.cloned.1.call-done), kind=kOutput, calls=%fused_computation.28 | convolution fusion | flops 3221618688 | bytes 11272192 | tf_op jit(solution)/shard_map/dot_general | solution.py:144
  297.4 1.8 copy.86
  (67 shorter events, 22.3 us)
Async XLA Ops:
  7.2 105.0 %all-gather.3.cloned.1.call-start = ((), (), s32[]{:S(2)}) async-start(), calls=%async_computation.2 | async-start | bytes 13369344 | tf_op jit(solution)/shard_map/all_gather | solution.py:63
  16.9 7.8 %copy-start.6 = (s32[32]{0:T(128)S(1)}, s32[32]{0:T(128)}, u32[]{:S(2)}) copy-start(s32[32]{0:T(128)} %param.13) | copy-start | bytes 388
  16.9 7.8 %copy-start.5 = (s32[16]{0:T(128)S(1)}, s32[16]{0:T(128)}, u32[]{:S(2)}) copy-start(s32[16]{0:T(128)} %constant.77.clone) | copy-start | bytes 196
  16.9 52.0 %all-to-all-start = ((bf16[256,16,256]{2,0,1:T(8,128)(2,1)}), bf16[256,16,256]{2,0,1:T(8,128)(2,1)}, u32[]{:S(2)}, u32[]{:S(2)}) async-start(bf16[256,16,256]{2,0,1:T(8,128)(2,1)} %copy.71), calls=%async_computation | async-start | bytes 4194304 | tf_op jit(solution)/shard_map/all_to_all | solution.py:66
  24.7 264.9 %all-gather.5.cloned.1.call-start = ((), (), s32[]{:S(2)}) async-start(), calls=%async_computation.3 | async-start | bytes 6684672 | tf_op jit(solution)/shard_map/all_gather | solution.py:143
  60.0 8.0 %copy-start.3 = (s32[4096]{0:T(1024)S(1)}, s32[4096]{0:T(1024)}, u32[]{:S(2)}) copy-start(s32[4096]{0:T(1024)} %param.14) | copy-start | bytes 49156
  147.6 10.1 %copy-start.2 = (bf16[256,256]{1,0:T(8,128)(2,1)S(1)}, bf16[256,256]{1,0:T(8,128)(2,1)}, u32[]{:S(2)}) copy-start(bf16[256,256]{1,0:T(8,128)(2,1)} %param.15) | copy-start | bytes 393220
  147.9 14.9 %collective-permute-start = (bf16[256,2,2,128]{3,0,2,1:T(8,128)(2,1)S(1)}, bf16[256,2,2,128]{3,0,2,1:T(8,128)(2,1)S(1)}, u32[]{:S(2)}, u32[]{:S(2)}) collective-permute-start(bf16[256,2,2,128]{3,0,2,1:T(8,128)(2,1)S(1)} %copy.91), channel_id=1, source_target_pairs={{0,64},{16,80},{32,96},{48,112},{64,128},{80,144},{96,160},{112,17... | collective-permute-start | bytes 786440 | tf_op jit(solution)/shard_map/ppermute | solution.py:14
  149.4 14.2 %collective-permute-start.1 = (bf16[256,2,2,128]{3,0,2,1:T(8,128)(2,1)S(1)}, bf16[256,2,2,128]{3,0,2,1:T(8,128)(2,1)S(1)}, u32[]{:S(2)}, u32[]{:S(2)}) collective-permute-start(bf16[256,2,2,128]{3,0,2,1:T(8,128)(2,1)S(1)} %copy.91), channel_id=1, source_target_pairs={{0,48},{16,64},{32,80},{48,96},{64,112},{80,128},{96,144},{112,160... | collective-permute-start | bytes 786440 | tf_op jit(solution)/shard_map/ppermute | solution.py:14
  152.6 11.8 %collective-permute-start.2 = (bf16[256,2,2,128]{3,0,2,1:T(8,128)(2,1)S(1)}, bf16[256,2,2,128]{3,0,2,1:T(8,128)(2,1)S(1)}, u32[]{:S(2)}, u32[]{:S(2)}) collective-permute-start(bf16[256,2,2,128]{3,0,2,1:T(8,128)(2,1)S(1)} %copy.91), channel_id=1, source_target_pairs={{0,32},{16,48},{32,64},{48,80},{64,96},{80,112},{96,128},{112,144}... | collective-permute-start | bytes 786440 | tf_op jit(solution)/shard_map/ppermute | solution.py:14
  157.8 8.6 %collective-permute-start.3 = (bf16[256,2,2,128]{3,0,2,1:T(8,128)(2,1)S(1)}, bf16[256,2,2,128]{3,0,2,1:T(8,128)(2,1)S(1)}, u32[]{:S(2)}, u32[]{:S(2)}) collective-permute-start(bf16[256,2,2,128]{3,0,2,1:T(8,128)(2,1)S(1)} %copy.91), channel_id=1, source_target_pairs={{0,16},{16,32},{32,48},{48,64},{64,80},{80,96},{96,112},{112,128},... | collective-permute-start | bytes 786440 | tf_op jit(solution)/shard_map/ppermute | solution.py:14
  170.4 2.6 copy-start.1
  174.2 10.8 %collective-permute-start.4 = (bf16[256,2,2,128]{0,3,2,1:T(8,128)(2,1)S(1)}, bf16[256,2,2,128]{0,3,2,1:T(8,128)(2,1)S(1)}, u32[]{:S(2)}, u32[]{:S(2)}) collective-permute-start(bf16[256,2,2,128]{0,3,2,1:T(8,128)(2,1)S(1)} %get-tuple-element.29), channel_id=1, source_target_pairs={{16,0},{32,16},{48,32},{64,48},{80,64},{96,80},{112,96},{128,112},... | collective-permute-start | bytes 786440 | tf_op jit(solution)/shard_map/ppermute | solution.py:14
  176.2 14.8 %collective-permute-start.5 = (bf16[256,2,2,128]{0,3,2,1:T(8,128)(2,1)S(1)}, bf16[256,2,2,128]{0,3,2,1:T(8,128)(2,1)S(1)}, u32[]{:S(2)}, u32[]{:S(2)}) collective-permute-start(bf16[256,2,2,128]{0,3,2,1:T(8,128)(2,1)S(1)} %get-tuple-element.32), channel_id=1, source_target_pairs={{32,0},{48,16},{64,32},{80,48},{96,64},{112,80},{128,96},{144,112}... | collective-permute-start | bytes 786440 | tf_op jit(solution)/shard_map/ppermute | solution.py:14
  177.5 23.1 %collective-permute-start.6 = (bf16[256,2,2,128]{0,3,2,1:T(8,128)(2,1)S(1)}, bf16[256,2,2,128]{0,3,2,1:T(8,128)(2,1)S(1)}, u32[]{:S(2)}, u32[]{:S(2)}) collective-permute-start(bf16[256,2,2,128]{0,3,2,1:T(8,128)(2,1)S(1)} %get-tuple-element.31), channel_id=1, source_target_pairs={{48,0},{64,16},{80,32},{96,48},{112,64},{128,80},{144,96},{160,112... | collective-permute-start | bytes 786440 | tf_op jit(solution)/shard_map/ppermute | solution.py:14
  178.8 25.7 %collective-permute-start.7 = (bf16[256,2,2,128]{0,3,2,1:T(8,128)(2,1)S(1)}, bf16[256,2,2,128]{0,3,2,1:T(8,128)(2,1)S(1)}, u32[]{:S(2)}, u32[]{:S(2)}) collective-permute-start(bf16[256,2,2,128]{0,3,2,1:T(8,128)(2,1)S(1)} %get-tuple-element.30), channel_id=1, source_target_pairs={{64,0},{80,16},{96,32},{112,48},{128,64},{144,80},{160,96},{176,11... | collective-permute-start | bytes 786440 | tf_op jit(solution)/shard_map/ppermute | solution.py:14
  181.7 23.7 %copy-start.4 = (s32[16]{0:T(128)S(1)}, s32[16]{0:T(128)}, u32[]{:S(2)}) copy-start(s32[16]{0:T(128)} %constant.110) | copy-start | bytes 196
  205.5 13.1 %copy-start = (bf16[256,3,2,128]{0,3,2,1:T(8,128)(2,1)S(1)}, bf16[256,3,2,128]{0,3,2,1:T(8,128)(2,1)}, u32[]{:S(2)}) copy-start(bf16[256,3,2,128]{0,3,2,1:T(8,128)(2,1)} %pad_maximum_fusion.3) | copy-start | bytes 1179652
  234.1 54.6 %all-to-all-start.1 = ((bf16[256,16,256]{2,0,1:T(8,128)(2,1)}), bf16[256,16,256]{2,0,1:T(8,128)(2,1)S(1)}, u32[]{:S(2)}, u32[]{:S(2)}) async-start(bf16[256,16,256]{2,0,1:T(8,128)(2,1)} %bitcast.87), calls=%async_computation.1 | async-start | bytes 4194304 | tf_op jit(solution)/shard_map/all_to_all | solution.py:138
Sparse Core Ops, SparseCore 0:
  11.4 100.6 all-gather.2
  205.6 75.0 all-gather.4

commit v3 on v2

--- a/solution.py
+++ b/solution.py
@@ -59,19 +59,30 @@
 
     ring = dp_ring(dp_devices)
     inverse = [ring.index(k) for k in range(dp_devices)]
-    flat_weights = weights.reshape(width_rows, 2, 3 * head_width)
-    whole_weights = lax.all_gather(
+    flat_weights = (
+        weights.reshape(width_rows, 2, 3 * head_width)
+        .transpose(1, 0, 2)
+        .reshape(2 * width_rows, 3 * head_width)
+    )
+    stacked_weights = lax.all_gather(
         flat_weights, "dp", axis=0, tiled=True, axis_index_groups=[ring]
     )
     columns = lax.all_to_all(tokens, "dp", split_axis=1, concat_axis=0, tiled=True)
     ring_columns = split_by_modality_major(
         ring_blocks(columns, ring, 0), ring_blocks(token_image, ring, 0)
     )
-    ring_tokens = split_by_modality(ring_blocks(tokens, ring, 1), my_image)
-    whole_weights, ring_columns, ring_tokens = lax.optimization_barrier(
-        (whole_weights, ring_columns, ring_tokens)
+    ring_tokens = ring_blocks(tokens, ring, 1).reshape(local_rows, dp_devices, 1, width_rows)
+    ring_tokens = jnp.concatenate(
+        [
+            jnp.where(my_image[:, None, None, None], jnp.zeros_like(ring_tokens), ring_tokens),
+            jnp.where(my_image[:, None, None, None], ring_tokens, jnp.zeros_like(ring_tokens)),
+        ],
+        axis=2,
+    ).reshape(local_rows, -1)
+    stacked_weights, ring_columns, ring_tokens = lax.optimization_barrier(
+        (stacked_weights, ring_columns, ring_tokens)
     )
-    stacked_weights = whole_weights.reshape(-1, 3 * head_width)
+    block_weights = stacked_weights.reshape(dp_devices, 2, width_rows, 3 * head_width)
 
     summed = jnp.dot(ring_tokens, stacked_weights, preferred_element_type=jnp.float32)
     qkv = summed.astype(jnp.bfloat16).reshape(local_rows, 3, head_count, HD)
@@ -128,13 +139,19 @@
         .reshape(local_rows, 3 * head_width)
     )
 
+    zeros = jnp.zeros_like(dqkv)
     parts = lax.dot_general(
-        split_by_modality_major(dqkv, my_image),
-        whole_weights.reshape(whole_weights.shape[0], -1),
-        (((1,), (1,)), ((), ())),
+        jnp.where(my_image[:, None], zeros, dqkv),
+        block_weights[:, 0],
+        (((1,), (2,)), ((), ())),
         preferred_element_type=jnp.float32,
-    ).astype(jnp.bfloat16)
-    parts = ring_blocks(parts, inverse, 1)
+    ) + lax.dot_general(
+        jnp.where(my_image[:, None], dqkv, zeros),
+        block_weights[:, 1],
+        (((1,), (2,)), ((), ())),
+        preferred_element_type=jnp.float32,
+    )
+    parts = ring_blocks(parts.astype(jnp.bfloat16).reshape(local_rows, -1), inverse, 1)
     group_parts = lax.all_to_all(
         parts.reshape(local_rows, mp_devices, -1), "mp", split_axis=1, concat_axis=1, tiled=True
     )

time: 311 us -> 274 us (0.88)
  local copies, waits for them, and re-layouts: 103 us -> 30.5 us
  waiting for transfers between devices: 106 us -> 145 us
  matrix products: 39.7 us -> 35.9 us
    reshape x4 -> x0, local copies, waits for them, and re-layouts: 35.4 us -> none  [the longest x1 26.2 us: on_device(): stacked_weights = whole_weights.reshape(-1, 3 * head_width)]
    all_to_all x1, waiting for transfers between devices: 0.77 us -> 31.4 us  [on_device(): lax.all_to_all(tokens, 'dp', split_axis=1, concat_axis=0, tiled=True)]
    another operation x1 -> x0, local copies, waits for them, and re-layouts: 27.2 us -> none  [split_by_modality(): jnp.stack([text, image], axis=2).reshape(rows.shape[0], 2 * rows.shape[1])]
    all_gather x1, waiting for transfers between devices: 0.01 us -> 19.7 us  [on_device(): lax.all_gather(dqkv, 'dp', axis=0, tiled=True, axis_index_groups=[ring])]
    unnamed x25 -> x22, local copies, waits for them, and re-layouts: 24.4 us -> 11.2 us
    ppermute x8, waiting for transfers between devices: 24 us -> 15.9 us  [shifted(): return lax.ppermute(block, axis, route)]
    concatenate x0 -> x1, local copies, waits for them, and re-layouts: none -> 6.36 us  [on_device(): jnp.concatenate([jnp.where(my_image[:, None, None, None], jnp.zeros_like(...]
    gather x5 -> x4, local copies, waits for them, and re-layouts: 11.8 us -> 7.38 us  [ring_blocks(): jnp.take(blocks, jnp.array(ring, jnp.int32), axis=axis).reshape(shape)]
  transfers between devices with their start and end apart: 12 -> 12, of which waited for: 8 -> 7; matrix products, arithmetic and copies ran while one was open for 30% -> 17% of each run, Pallas kernels for 0% -> 0%
where the time goes in v3:
time: 274 us; the launch traced here: 272 us
  waiting for transfers between devices  145 us (53%)
  matrix products  35.9 us (13%)
  starting transfers between devices  34.7 us (13%)
  local copies, waits for them, and re-layouts  30.5 us (11%)
  between operations  14.4 us (5%)
  other arithmetic  11.2 us (4%)
    all_to_all x1, waiting for transfers between devices, on_device(): lax.all_to_all(parts.reshape(local_rows, mp_devices, -1), 'mp', split_axi...  41.8 us
    all_gather x1, waiting for transfers between devices, on_device(): lax.all_gather(flat_weights, 'dp', axis=0, tiled=True, axis_index_groups=...  36.4 us
    all_to_all x1, waiting for transfers between devices, on_device(): lax.all_to_all(tokens, 'dp', split_axis=1, concat_axis=0, tiled=True)  31.4 us
    ppermute x8, starting transfers between devices, shifted(): return lax.ppermute(block, axis, route)  20.1 us
    all_gather x1, waiting for transfers between devices, on_device(): lax.all_gather(dqkv, 'dp', axis=0, tiled=True, axis_index_groups=[ring])  19.7 us
    ppermute x8, waiting for transfers between devices, shifted(): return lax.ppermute(block, axis, route)  15.9 us
    unnamed x22, local copies, waits for them, and re-layouts  11.2 us
    dot_general x1, matrix products, on_device(): jnp.dot(ring_tokens, stacked_weights, preferred_element_type=jnp.float32)  9.29 us
  transfers between devices with their start and end apart: 12, of which 7 were waited for; matrix products, arithmetic and copies ran while one was open for 17% of the time, Pallas kernels for 0%

profile of v3, /device:TPU:97, one launch (start us, length us, event | category | flops | bytes accessed | tf_op | source)
XLA Modules:
  0.0 272.0 jit_solution(16255635195877370614)
XLA Ops:
  7.2 2.2 copy.40
  10.6 3.3 %copy.42 = bf16[256,4096]{0,1:T(8,128)(2,1)S(1)} copy(bf16[256,4096]{1,0:T(8,128)(2,1)} %param.11) | data formatting | bytes 4194304 | tf_op args[0]
  13.9 2.5 copy.43
  16.4 7.7 %all-to-all-start = ((bf16[256,16,256]{2,0,1:T(8,128)(2,1)}), bf16[256,16,256]{2,0,1:T(8,128)(2,1)}, u32[]{:S(2)}, u32[]{:S(2)}) async-start(bf16[256,16,256]{2,0,1:T(8,128)(2,1)} %copy.43), calls=%async_computation | async-start | bytes 4194304 | tf_op jit(solution)/shard_map/all_to_all | solution.py:70
  24.4 2.5 gather_fusion.2
  28.1 2.3 pad_maximum_fusion.1
  30.4 6.4 %copy.45 = bf16[256,16,2,256]{0,3,2,1:T(8,128)(2,1)} copy(bf16[256,16,2,256]{3,0,1,2:T(8,128)(2,1)} %pad_maximum_fusion.1) | data formatting | bytes 8388608 | tf_op jit(solution)/shard_map/concatenate | solution.py:75
  36.9 31.4 %all-to-all-done = bf16[256,16,256]{2,0,1:T(8,128)(2,1)} async-done(((bf16[256,16,256]{2,0,1:T(8,128)(2,1)}), bf16[256,16,256]{2,0,1:T(8,128)(2,1)}, u32[]{:S(2)}, u32[]{:S(2)}) %all-to-all-start) | async-done | bytes 2097184 | tf_op jit(solution)/shard_map/all_to_all | solution.py:70
  68.3 2.3 gather_fusion.1
  70.5 2.1 bitcast_select_fusion.2
  72.7 2.4 pad_maximum_fusion
  75.1 36.4 %all-gather.3.cloned.1.call-done = bf16[8192,768]{1,0:T(8,128)(2,1)} async-done(((bf16[512,768]{1,0:T(8,128)(2,1)}), bf16[8192,768]{1,0:T(8,128)(2,1)}) %all-gather.3.cloned.1.call-update) | async-done | bytes 12582928 | tf_op jit(solution)/shard_map/all_gather | solution.py:67
  111.5 9.3 %convolution_convert_fusion.1 = bf16[256,768]{1,0:T(8,128)(2,1)S(1)} fusion(bf16[256,8192]{0,1:T(8,128)(2,1)} %bitcast.108, bf16[8192,768]{1,0:T(8,128)(2,1)} %all-gather.3.cloned.1.call-done), kind=kOutput, calls=%fused_computation.37 | convolution fusion | flops 3221422080 | bytes 17170432 | tf_op jit(solution)/shard_map/dot_general | solution.py:87
  122.6 3.2 %collective-permute-start.1 = (bf16[256,2,2,128]{3,0,2,1:T(8,128)(2,1)S(1)}, bf16[256,2,2,128]{3,0,2,1:T(8,128)(2,1)S(1)}, u32[]{:S(2)}, u32[]{:S(2)}) collective-permute-start(bf16[256,2,2,128]{3,0,2,1:T(8,128)(2,1)S(1)} %copy.69), channel_id=1, source_target_pairs={{0,48},{16,64},{32,80},{48,96},{64,112},{80,128},{96,144},{112,160... | collective-permute-start | bytes 786440 | tf_op jit(solution)/shard_map/ppermute | solution.py:14
  125.8 4.8 %collective-permute-start.2 = (bf16[256,2,2,128]{3,0,2,1:T(8,128)(2,1)S(1)}, bf16[256,2,2,128]{3,0,2,1:T(8,128)(2,1)S(1)}, u32[]{:S(2)}, u32[]{:S(2)}) collective-permute-start(bf16[256,2,2,128]{3,0,2,1:T(8,128)(2,1)S(1)} %copy.69), channel_id=1, source_target_pairs={{0,32},{16,48},{32,64},{48,80},{64,96},{80,112},{96,128},{112,144}... | collective-permute-start | bytes 786440 | tf_op jit(solution)/shard_map/ppermute | solution.py:14
  131.0 4.7 %collective-permute-start.3 = (bf16[256,2,2,128]{3,0,2,1:T(8,128)(2,1)S(1)}, bf16[256,2,2,128]{3,0,2,1:T(8,128)(2,1)S(1)}, u32[]{:S(2)}, u32[]{:S(2)}) collective-permute-start(bf16[256,2,2,128]{3,0,2,1:T(8,128)(2,1)S(1)} %copy.69), channel_id=1, source_target_pairs={{0,16},{16,32},{32,48},{48,64},{64,80},{80,96},{96,112},{112,128},... | collective-permute-start | bytes 786440 | tf_op jit(solution)/shard_map/ppermute | solution.py:14
  138.1 1.5 collective-permute-done.3
  141.1 2.5 fusion.24
  143.6 2.2 multiply_reduce_fusion
  151.3 2.1 collective-permute-start.4
  153.4 1.7 fusion.12
  155.1 3.4 %collective-permute-done.7 = bf16[256,2,2,128]{0,3,2,1:T(8,128)(2,1)S(1)} collective-permute-done((bf16[256,2,2,128]{0,3,2,1:T(8,128)(2,1)S(1)}, bf16[256,2,2,128]{0,3,2,1:T(8,128)(2,1)S(1)}, u32[]{:S(2)}, u32[]{:S(2)}) %collective-permute-start.7) | collective-permute-done | bytes 262176 | tf_op jit(solution)/shard_map/ppermute | solution.py:14
  158.5 10.9 %collective-permute-done.6 = bf16[256,2,2,128]{0,3,2,1:T(8,128)(2,1)S(1)} collective-permute-done((bf16[256,2,2,128]{0,3,2,1:T(8,128)(2,1)S(1)}, bf16[256,2,2,128]{0,3,2,1:T(8,128)(2,1)S(1)}, u32[]{:S(2)}, u32[]{:S(2)}) %collective-permute-start.6) | collective-permute-done | bytes 262176 | tf_op jit(solution)/shard_map/ppermute | solution.py:14
  171.5 4.6 %fusion.1 = f32[256,16,256]{2,0,1:T(8,128)S(1)} fusion(bf16[256,768,1]{0,1,2:T(8,128)(2,1)S(1)} %bitcast.117, bf16[16,2,256,768]{3,2,1,0:T(8,128)(2,1)} %bitcast.106), kind=kOutput, calls=%fused_computation.6 | convolution fusion | flops 1610612736 | bytes 10878976 | tf_op jit(solution)/shard_map/dot_general | solution.py:148
  176.2 4.6 %add_convert_fusion = bf16[256,16,256]{2,0,1:T(8,128)(2,1)S(1)} fusion(f32[256,16,256]{2,0,1:T(8,128)S(1)} %fusion.1, bf16[256,768,1]{0,1,2:T(8,128)(2,1)S(1)} %bitcast.115, bf16[16,2,256,768]{3,2,1,0:T(8,128)(2,1)} %bitcast.107), kind=kOutput, calls=%fused_computation.11 | convolution fusion | flops 1612709888 | bytes 12976128 | tf_op jit(solution)/shard_map/dot_general | solution.py:143
  180.8 2.0 gather_fusion.3
  182.9 6.8 %all-to-all-start.1 = ((bf16[256,16,256]{2,0,1:T(8,128)(2,1)}), bf16[256,16,256]{2,0,1:T(8,128)(2,1)S(1)}, u32[]{:S(2)}, u32[]{:S(2)}) async-start(bf16[256,16,256]{2,0,1:T(8,128)(2,1)} %bitcast.109), calls=%async_computation.1 | async-start | bytes 4194304 | tf_op jit(solution)/shard_map/all_to_all | solution.py:155
  189.6 2.7 convolution_convert_fusion.2
  193.1 41.8 %all-to-all-done.1 = bf16[256,16,256]{2,0,1:T(8,128)(2,1)S(1)} async-done(((bf16[256,16,256]{2,0,1:T(8,128)(2,1)}), bf16[256,16,256]{2,0,1:T(8,128)(2,1)S(1)}, u32[]{:S(2)}, u32[]{:S(2)}) %all-to-all-start.1) | async-done | bytes 2097184 | tf_op jit(solution)/shard_map/all_to_all | solution.py:155
  235.8 19.7 %all-gather.5.cloned.1.call-done = bf16[4096,768]{0,1:T(8,128)(2,1)} async-done(((bf16[256,768]{0,1:T(8,128)(2,1)}), bf16[4096,768]{0,1:T(8,128)(2,1)}) %all-gather.5.cloned.1.call-update) | async-done | bytes 6291472 | tf_op jit(solution)/shard_map/all_gather | solution.py:160
  255.6 7.5 %convolution_convert_fusion = bf16[512,768]{1,0:T(8,128)(2,1)S(1)} fusion(bf16[4096,512]{1,0:T(8,128)(2,1)} %pad_maximum_fusion, bf16[4096,768]{0,1:T(8,128)(2,1)} %all-gather.5.cloned.1.call-done), kind=kOutput, calls=%fused_computation.33 | convolution fusion | flops 3221618688 | bytes 11272192 | tf_op jit(solution)/shard_map/dot_general | solution.py:161
  263.4 1.8 copy.60
  (61 shorter events, 18.2 us)
Async XLA Ops:
  7.2 104.3 %all-gather.3.cloned.1.call-start = ((), (), s32[]{:S(2)}) async-start(), calls=%async_computation.2 | async-start | bytes 13369344 | tf_op jit(solution)/shard_map/all_gather | solution.py:67
  16.4 7.8 %copy-start.5 = (s32[32]{0:T(128)S(1)}, s32[32]{0:T(128)}, u32[]{:S(2)}) copy-start(s32[32]{0:T(128)} %param.13) | copy-start | bytes 388
  16.4 8.0 %copy-start.4 = (s32[16]{0:T(128)S(1)}, s32[16]{0:T(128)}, u32[]{:S(2)}) copy-start(s32[16]{0:T(128)} %constant.77.clone) | copy-start | bytes 196
  16.4 51.9 %all-to-all-start = ((bf16[256,16,256]{2,0,1:T(8,128)(2,1)}), bf16[256,16,256]{2,0,1:T(8,128)(2,1)}, u32[]{:S(2)}, u32[]{:S(2)}) async-start(bf16[256,16,256]{2,0,1:T(8,128)(2,1)} %copy.43), calls=%async_computation | async-start | bytes 4194304 | tf_op jit(solution)/shard_map/all_to_all | solution.py:70
  24.1 231.4 %all-gather.5.cloned.1.call-start = ((), (), s32[]{:S(2)}) async-start(), calls=%async_computation.3 | async-start | bytes 6684672 | tf_op jit(solution)/shard_map/all_gather | solution.py:160
  30.4 6.4 %copy-start.2 = (s32[4096]{0:T(1024)S(1)}, s32[4096]{0:T(1024)}, u32[]{:S(2)}) copy-start(s32[4096]{0:T(1024)} %param.14) | copy-start | bytes 49156
  120.8 10.1 %copy-start.1 = (bf16[256,256]{1,0:T(8,128)(2,1)S(1)}, bf16[256,256]{1,0:T(8,128)(2,1)}, u32[]{:S(2)}) copy-start(bf16[256,256]{1,0:T(8,128)(2,1)} %param.15) | copy-start | bytes 393220
  121.1 14.7 %collective-permute-start = (bf16[256,2,2,128]{3,0,2,1:T(8,128)(2,1)S(1)}, bf16[256,2,2,128]{3,0,2,1:T(8,128)(2,1)S(1)}, u32[]{:S(2)}, u32[]{:S(2)}) collective-permute-start(bf16[256,2,2,128]{3,0,2,1:T(8,128)(2,1)S(1)} %copy.69), channel_id=1, source_target_pairs={{0,64},{16,80},{32,96},{48,112},{64,128},{80,144},{96,160},{112,17... | collective-permute-start | bytes 786440 | tf_op jit(solution)/shard_map/ppermute | solution.py:14
  122.6 14.1 %collective-permute-start.1 = (bf16[256,2,2,128]{3,0,2,1:T(8,128)(2,1)S(1)}, bf16[256,2,2,128]{3,0,2,1:T(8,128)(2,1)S(1)}, u32[]{:S(2)}, u32[]{:S(2)}) collective-permute-start(bf16[256,2,2,128]{3,0,2,1:T(8,128)(2,1)S(1)} %copy.69), channel_id=1, source_target_pairs={{0,48},{16,64},{32,80},{48,96},{64,112},{80,128},{96,144},{112,160... | collective-permute-start | bytes 786440 | tf_op jit(solution)/shard_map/ppermute | solution.py:14
  125.8 11.6 %collective-permute-start.2 = (bf16[256,2,2,128]{3,0,2,1:T(8,128)(2,1)S(1)}, bf16[256,2,2,128]{3,0,2,1:T(8,128)(2,1)S(1)}, u32[]{:S(2)}, u32[]{:S(2)}) collective-permute-start(bf16[256,2,2,128]{3,0,2,1:T(8,128)(2,1)S(1)} %copy.69), channel_id=1, source_target_pairs={{0,32},{16,48},{32,64},{48,80},{64,96},{80,112},{96,128},{112,144}... | collective-permute-start | bytes 786440 | tf_op jit(solution)/shard_map/ppermute | solution.py:14
  131.0 8.6 %collective-permute-start.3 = (bf16[256,2,2,128]{3,0,2,1:T(8,128)(2,1)S(1)}, bf16[256,2,2,128]{3,0,2,1:T(8,128)(2,1)S(1)}, u32[]{:S(2)}, u32[]{:S(2)}) collective-permute-start(bf16[256,2,2,128]{3,0,2,1:T(8,128)(2,1)S(1)} %copy.69), channel_id=1, source_target_pairs={{0,16},{16,32},{32,48},{48,64},{64,80},{80,96},{96,112},{112,128},... | collective-permute-start | bytes 786440 | tf_op jit(solution)/shard_map/ppermute | solution.py:14
  143.6 2.6 copy-start
  147.4 11.1 %collective-permute-start.7 = (bf16[256,2,2,128]{0,3,2,1:T(8,128)(2,1)S(1)}, bf16[256,2,2,128]{0,3,2,1:T(8,128)(2,1)S(1)}, u32[]{:S(2)}, u32[]{:S(2)}) collective-permute-start(bf16[256,2,2,128]{0,3,2,1:T(8,128)(2,1)S(1)} %get-tuple-element.26), channel_id=1, source_target_pairs={{64,0},{80,16},{96,32},{112,48},{128,64},{144,80},{160,96},{176,11... | collective-permute-start | bytes 786440 | tf_op jit(solution)/shard_map/ppermute | solution.py:14
  148.7 20.7 %collective-permute-start.6 = (bf16[256,2,2,128]{0,3,2,1:T(8,128)(2,1)S(1)}, bf16[256,2,2,128]{0,3,2,1:T(8,128)(2,1)S(1)}, u32[]{:S(2)}, u32[]{:S(2)}) collective-permute-start(bf16[256,2,2,128]{0,3,2,1:T(8,128)(2,1)S(1)} %get-tuple-element.27), channel_id=1, source_target_pairs={{48,0},{64,16},{80,32},{96,48},{112,64},{128,80},{144,96},{160,112... | collective-permute-start | bytes 786440 | tf_op jit(solution)/shard_map/ppermute | solution.py:14
  150.0 19.4 %collective-permute-start.5 = (bf16[256,2,2,128]{0,3,2,1:T(8,128)(2,1)S(1)}, bf16[256,2,2,128]{0,3,2,1:T(8,128)(2,1)S(1)}, u32[]{:S(2)}, u32[]{:S(2)}) collective-permute-start(bf16[256,2,2,128]{0,3,2,1:T(8,128)(2,1)S(1)} %get-tuple-element.28), channel_id=1, source_target_pairs={{32,0},{48,16},{64,32},{80,48},{96,64},{112,80},{128,96},{144,112}... | collective-permute-start | bytes 786440 | tf_op jit(solution)/shard_map/ppermute | solution.py:14
  151.3 18.1 %collective-permute-start.4 = (bf16[256,2,2,128]{0,3,2,1:T(8,128)(2,1)S(1)}, bf16[256,2,2,128]{0,3,2,1:T(8,128)(2,1)S(1)}, u32[]{:S(2)}, u32[]{:S(2)}) collective-permute-start(bf16[256,2,2,128]{0,3,2,1:T(8,128)(2,1)S(1)} %get-tuple-element.25), channel_id=1, source_target_pairs={{16,0},{32,16},{48,32},{64,48},{80,64},{96,80},{112,96},{128,112},... | collective-permute-start | bytes 786440 | tf_op jit(solution)/shard_map/ppermute | solution.py:14
  155.1 15.4 %copy-start.3 = (s32[16]{0:T(128)S(1)}, s32[16]{0:T(128)}, u32[]{:S(2)}) copy-start(s32[16]{0:T(128)} %constant.110) | copy-start | bytes 196
  182.9 52.0 %all-to-all-start.1 = ((bf16[256,16,256]{2,0,1:T(8,128)(2,1)}), bf16[256,16,256]{2,0,1:T(8,128)(2,1)S(1)}, u32[]{:S(2)}, u32[]{:S(2)}) async-start(bf16[256,16,256]{2,0,1:T(8,128)(2,1)} %bitcast.109), calls=%async_computation.1 | async-start | bytes 4194304 | tf_op jit(solution)/shard_map/all_to_all | solution.py:155
Sparse Core Ops, SparseCore 0:
  10.8 100.6 all-gather.2
  170.6 84.9 all-gather.4

commit v4 on v3

--- a/solution.py
+++ b/solution.py
@@ -84,13 +84,19 @@
     )
     block_weights = stacked_weights.reshape(dp_devices, 2, width_rows, 3 * head_width)
 
-    summed = jnp.dot(ring_tokens, stacked_weights, preferred_element_type=jnp.float32)
-    qkv = summed.astype(jnp.bfloat16).reshape(local_rows, 3, head_count, HD)
-    queries = qkv[:, 0]
-    key_values = qkv[:, 1:]
+    key_values = (
+        jnp.dot(ring_tokens, stacked_weights[:, head_width:], preferred_element_type=jnp.float32)
+        .astype(jnp.bfloat16)
+        .reshape(local_rows, 2, head_count, HD)
+    )
     received = []
     for distance in range(SPAN, 0, -1):
         received.append(shifted(key_values, "dp", distance))
+    queries = (
+        jnp.dot(ring_tokens, stacked_weights[:, :head_width], preferred_element_type=jnp.float32)
+        .astype(jnp.bfloat16)
+        .reshape(local_rows, head_count, HD)
+    )
     window = jnp.concatenate(received + [key_values], 0)
     key_rows = window[:, 0]
     value_rows = window[:, 1]

time: 274 us -> 271 us (0.989)
  local copies, waits for them, and re-layouts: 30.5 us -> 27.7 us
    dot_general x1 -> x2, matrix products: 9.29 us -> 12.2 us  [the longest x1 7 us: on_device(): jnp.dot(ring_tokens, stacked_weights[:, head_width:], preferred_element_t...]
    unnamed x22 -> x27, local copies, waits for them, and re-layouts: 11.2 us -> 9.27 us
  transfers between devices with their start and end apart: 12 -> 12, of which waited for: 7 -> 6; matrix products, arithmetic and copies ran while one was open for 17% -> 18% of each run, Pallas kernels for 0% -> 0%
where the time goes in v4:
time: 271 us; the launch traced here: 269 us
  waiting for transfers between devices  143 us (53%)
  matrix products  37.6 us (14%)
  starting transfers between devices  35 us (13%)
  local copies, waits for them, and re-layouts  27.7 us (10%)
  between operations  14.5 us (5%)
  other arithmetic  11.2 us (4%)
    all_to_all x1, waiting for transfers between devices, on_device(): lax.all_to_all(parts.reshape(local_rows, mp_devices, -1), 'mp', split_axi...  42.3 us
    all_gather x1, waiting for transfers between devices, on_device(): lax.all_gather(flat_weights, 'dp', axis=0, tiled=True, axis_index_groups=...  36.4 us
    all_to_all x1, waiting for transfers between devices, on_device(): lax.all_to_all(tokens, 'dp', split_axis=1, concat_axis=0, tiled=True)  30.9 us
    ppermute x8, starting transfers between devices, shifted(): return lax.ppermute(block, axis, route)  20.3 us
    all_gather x1, waiting for transfers between devices, on_device(): lax.all_gather(dqkv, 'dp', axis=0, tiled=True, axis_index_groups=[ring])  19.3 us
    ppermute x8, waiting for transfers between devices, shifted(): return lax.ppermute(block, axis, route)  13.7 us
    unnamed x27, local copies, waits for them, and re-layouts  9.27 us
    all_to_all x1, starting transfers between devices, on_device(): lax.all_to_all(tokens, 'dp', split_axis=1, concat_axis=0, tiled=True)  7.75 us
  transfers between devices with their start and end apart: 12, of which 6 were waited for; matrix products, arithmetic and copies ran while one was open for 18% of the time, Pallas kernels for 0%

profile of v4, /device:TPU:97, one launch (start us, length us, event | category | flops | bytes accessed | tf_op | source)
XLA Modules:
  0.0 268.6 jit_solution(8229567507646361081)
XLA Ops:
  7.2 2.2 copy.46
  10.6 3.3 %copy.48 = bf16[256,4096]{0,1:T(8,128)(2,1)S(1)} copy(bf16[256,4096]{1,0:T(8,128)(2,1)} %param.11) | data formatting | bytes 4194304 | tf_op args[0]
  13.9 2.5 copy.49
  16.4 7.7 %all-to-all-start = ((bf16[256,16,256]{2,0,1:T(8,128)(2,1)}), bf16[256,16,256]{2,0,1:T(8,128)(2,1)}, u32[]{:S(2)}, u32[]{:S(2)}) async-start(bf16[256,16,256]{2,0,1:T(8,128)(2,1)} %copy.49), calls=%async_computation | async-start | bytes 4194304 | tf_op jit(solution)/shard_map/all_to_all | solution.py:70
  24.4 2.5 gather_fusion.2
  28.1 2.3 pad_maximum_fusion.1
  30.4 6.4 %copy.51 = bf16[256,16,2,256]{0,3,2,1:T(8,128)(2,1)} copy(bf16[256,16,2,256]{3,0,1,2:T(8,128)(2,1)} %pad_maximum_fusion.1) | data formatting | bytes 8388608 | tf_op jit(solution)/shard_map/concatenate | solution.py:75
  37.3 30.9 %all-to-all-done = bf16[256,16,256]{2,0,1:T(8,128)(2,1)} async-done(((bf16[256,16,256]{2,0,1:T(8,128)(2,1)}), bf16[256,16,256]{2,0,1:T(8,128)(2,1)}, u32[]{:S(2)}, u32[]{:S(2)}) %all-to-all-start) | async-done | bytes 2097184 | tf_op jit(solution)/shard_map/all_to_all | solution.py:70
  68.2 2.3 gather_fusion.1
  70.5 2.1 bitcast_select_fusion.2
  72.7 2.4 pad_maximum_fusion
  75.0 36.4 %all-gather.3.cloned.1.call-done = bf16[8192,768]{1,0:T(8,128)(2,1)} async-done(((bf16[512,768]{1,0:T(8,128)(2,1)}), bf16[8192,768]{1,0:T(8,128)(2,1)}) %all-gather.3.cloned.1.call-update) | async-done | bytes 12582928 | tf_op jit(solution)/shard_map/all_gather | solution.py:67
  111.5 7.0 %fusion.16 = bf16[256,512]{1,0:T(8,128)(2,1)S(1)} fusion(bf16[256,8192]{0,1:T(8,128)(2,1)} %bitcast.101, bf16[8192,768]{1,0:T(8,128)(2,1)} %all-gather.3.cloned.1.call-done), kind=kOutput, calls=%fused_computation.41 | convolution fusion | flops 2147614720 | bytes 12845056 | tf_op jit(solution)/shard_map/dot_general | solution.py:88
  118.6 1.4 collective-permute-start
  120.1 3.2 %collective-permute-start.1 = (bf16[256,2,2,128]{3,0,2,1:T(8,128)(2,1)S(1)}, bf16[256,2,2,128]{3,0,2,1:T(8,128)(2,1)S(1)}, u32[]{:S(2)}, u32[]{:S(2)}) collective-permute-start(bf16[256,2,2,128]{3,0,2,1:T(8,128)(2,1)S(1)} %copy.52), channel_id=1, source_target_pairs={{0,48},{16,64},{32,80},{48,96},{64,112},{80,128},{96,144},{112,160... | collective-permute-start | bytes 786440 | tf_op jit(solution)/shard_map/ppermute | solution.py:14
  123.3 4.8 %collective-permute-start.2 = (bf16[256,2,2,128]{3,0,2,1:T(8,128)(2,1)S(1)}, bf16[256,2,2,128]{3,0,2,1:T(8,128)(2,1)S(1)}, u32[]{:S(2)}, u32[]{:S(2)}) collective-permute-start(bf16[256,2,2,128]{3,0,2,1:T(8,128)(2,1)S(1)} %copy.52), channel_id=1, source_target_pairs={{0,32},{16,48},{32,64},{48,80},{64,96},{80,112},{96,128},{112,144}... | collective-permute-start | bytes 786440 | tf_op jit(solution)/shard_map/ppermute | solution.py:14
  128.1 4.7 %collective-permute-start.3 = (bf16[256,2,2,128]{3,0,2,1:T(8,128)(2,1)S(1)}, bf16[256,2,2,128]{3,0,2,1:T(8,128)(2,1)S(1)}, u32[]{:S(2)}, u32[]{:S(2)}) collective-permute-start(bf16[256,2,2,128]{3,0,2,1:T(8,128)(2,1)S(1)} %copy.52), channel_id=1, source_target_pairs={{0,16},{16,32},{32,48},{48,64},{64,80},{80,96},{96,112},{112,128},... | collective-permute-start | bytes 786440 | tf_op jit(solution)/shard_map/ppermute | solution.py:14
  132.8 5.2 %fusion.20 = bf16[256,256]{0,1:T(8,128)(2,1)S(1)} fusion(bf16[256,8192]{0,1:T(8,128)(2,1)} %bitcast.102, bf16[8192,768]{1,0:T(8,128)(2,1)} %all-gather.3.cloned.1.call-done), kind=kOutput, calls=%fused_computation.44 | convolution fusion | flops 1073807360 | bytes 8519680 | tf_op jit(solution)/shard_map/dot_general | solution.py:96
  139.3 2.6 fusion.34
  141.9 2.2 multiply_reduce_fusion
  149.7 2.1 collective-permute-start.4
  152.4 2.7 %collective-permute-done.7 = bf16[256,2,2,128]{0,3,2,1:T(8,128)(2,1)S(1)} collective-permute-done((bf16[256,2,2,128]{0,3,2,1:T(8,128)(2,1)S(1)}, bf16[256,2,2,128]{0,3,2,1:T(8,128)(2,1)S(1)}, u32[]{:S(2)}, u32[]{:S(2)}) %collective-permute-start.7) | collective-permute-done | bytes 262176 | tf_op jit(solution)/shard_map/ppermute | solution.py:14
  155.1 10.9 %collective-permute-done.6 = bf16[256,2,2,128]{0,3,2,1:T(8,128)(2,1)S(1)} collective-permute-done((bf16[256,2,2,128]{0,3,2,1:T(8,128)(2,1)S(1)}, bf16[256,2,2,128]{0,3,2,1:T(8,128)(2,1)S(1)}, u32[]{:S(2)}, u32[]{:S(2)}) %collective-permute-start.6) | collective-permute-done | bytes 262176 | tf_op jit(solution)/shard_map/ppermute | solution.py:14
  168.1 4.6 %fusion.3 = f32[256,16,256]{2,0,1:T(8,128)S(1)} fusion(bf16[256,768,1]{0,1,2:T(8,128)(2,1)S(1)} %bitcast.111, bf16[16,2,256,768]{3,2,1,0:T(8,128)(2,1)} %bitcast.104), kind=kOutput, calls=%fused_computation.8 | convolution fusion | flops 1610612736 | bytes 10878976 | tf_op jit(solution)/shard_map/dot_general | solution.py:154
  172.8 4.6 %add_convert_fusion = bf16[256,16,256]{2,0,1:T(8,128)(2,1)S(1)} fusion(f32[256,16,256]{2,0,1:T(8,128)S(1)} %fusion.3, bf16[256,768,1]{0,1,2:T(8,128)(2,1)S(1)} %bitcast.109, bf16[16,2,256,768]{3,2,1,0:T(8,128)(2,1)} %bitcast.105), kind=kOutput, calls=%fused_computation.13 | convolution fusion | flops 1612709888 | bytes 12976128 | tf_op jit(solution)/shard_map/dot_general | solution.py:149
  177.4 2.0 gather_fusion.3
  179.4 6.9 %all-to-all-start.1 = ((bf16[256,16,256]{2,0,1:T(8,128)(2,1)}), bf16[256,16,256]{2,0,1:T(8,128)(2,1)S(1)}, u32[]{:S(2)}, u32[]{:S(2)}) async-start(bf16[256,16,256]{2,0,1:T(8,128)(2,1)} %bitcast.99), calls=%async_computation.1 | async-start | bytes 4194304 | tf_op jit(solution)/shard_map/all_to_all | solution.py:161
  186.4 2.4 convolution_convert_fusion.1
  189.6 42.3 %all-to-all-done.1 = bf16[256,16,256]{2,0,1:T(8,128)(2,1)S(1)} async-done(((bf16[256,16,256]{2,0,1:T(8,128)(2,1)}), bf16[256,16,256]{2,0,1:T(8,128)(2,1)S(1)}, u32[]{:S(2)}, u32[]{:S(2)}) %all-to-all-start.1) | async-done | bytes 2097184 | tf_op jit(solution)/shard_map/all_to_all | solution.py:161
  232.9 19.3 %all-gather.5.cloned.1.call-done = bf16[4096,768]{0,1:T(8,128)(2,1)} async-done(((bf16[256,768]{0,1:T(8,128)(2,1)}), bf16[4096,768]{0,1:T(8,128)(2,1)}) %all-gather.5.cloned.1.call-update) | async-done | bytes 6291472 | tf_op jit(solution)/shard_map/all_gather | solution.py:166
  252.1 7.5 %convolution_convert_fusion = bf16[512,768]{1,0:T(8,128)(2,1)S(1)} fusion(bf16[4096,512]{1,0:T(8,128)(2,1)} %pad_maximum_fusion, bf16[4096,768]{0,1:T(8,128)(2,1)} %all-gather.5.cloned.1.call-done), kind=kOutput, calls=%fused_computation.37 | convolution fusion | flops 3221618688 | bytes 11272192 | tf_op jit(solution)/shard_map/dot_general | solution.py:167
  259.9 1.8 copy.69
  (66 shorter events, 14.6 us)
Async XLA Ops:
  7.2 104.3 %all-gather.3.cloned.1.call-start = ((), (), s32[]{:S(2)}) async-start(), calls=%async_computation.2 | async-start | bytes 13369344 | tf_op jit(solution)/shard_map/all_gather | solution.py:67
  16.4 7.8 %copy-start.8 = (s32[32]{0:T(128)S(1)}, s32[32]{0:T(128)}, u32[]{:S(2)}) copy-start(s32[32]{0:T(128)} %param.13) | copy-start | bytes 388
  16.4 8.0 %copy-start.7 = (s32[16]{0:T(128)S(1)}, s32[16]{0:T(128)}, u32[]{:S(2)}) copy-start(s32[16]{0:T(128)} %constant.77.clone) | copy-start | bytes 196
  16.4 51.9 %all-to-all-start = ((bf16[256,16,256]{2,0,1:T(8,128)(2,1)}), bf16[256,16,256]{2,0,1:T(8,128)(2,1)}, u32[]{:S(2)}, u32[]{:S(2)}) async-start(bf16[256,16,256]{2,0,1:T(8,128)(2,1)} %copy.49), calls=%async_computation | async-start | bytes 4194304 | tf_op jit(solution)/shard_map/all_to_all | solution.py:70
  24.1 228.0 %all-gather.5.cloned.1.call-start = ((), (), s32[]{:S(2)}) async-start(), calls=%async_computation.3 | async-start | bytes 6684672 | tf_op jit(solution)/shard_map/all_gather | solution.py:166
  30.3 6.4 %copy-start.5 = (s32[4096]{0:T(1024)S(1)}, s32[4096]{0:T(1024)}, u32[]{:S(2)}) copy-start(s32[4096]{0:T(1024)} %param.14) | copy-start | bytes 49156
  30.4 6.5 %copy-start.4 = (bf16[256,256]{1,0:T(8,128)(2,1)S(1)}, bf16[256,256]{1,0:T(8,128)(2,1)}, u32[]{:S(2)}) copy-start(bf16[256,256]{1,0:T(8,128)(2,1)} %param.15) | copy-start | bytes 393220
  118.6 19.4 %collective-permute-start = (bf16[256,2,2,128]{3,0,2,1:T(8,128)(2,1)S(1)}, bf16[256,2,2,128]{3,0,2,1:T(8,128)(2,1)S(1)}, u32[]{:S(2)}, u32[]{:S(2)}) collective-permute-start(bf16[256,2,2,128]{3,0,2,1:T(8,128)(2,1)S(1)} %copy.52), channel_id=1, source_target_pairs={{0,64},{16,80},{32,96},{48,112},{64,128},{80,144},{96,160},{112,17... | collective-permute-start | bytes 786440 | tf_op jit(solution)/shard_map/ppermute | solution.py:14
  120.1 18.0 %collective-permute-start.1 = (bf16[256,2,2,128]{3,0,2,1:T(8,128)(2,1)S(1)}, bf16[256,2,2,128]{3,0,2,1:T(8,128)(2,1)S(1)}, u32[]{:S(2)}, u32[]{:S(2)}) collective-permute-start(bf16[256,2,2,128]{3,0,2,1:T(8,128)(2,1)S(1)} %copy.52), channel_id=1, source_target_pairs={{0,48},{16,64},{32,80},{48,96},{64,112},{80,128},{96,144},{112,160... | collective-permute-start | bytes 786440 | tf_op jit(solution)/shard_map/ppermute | solution.py:14
  123.3 14.8 %collective-permute-start.2 = (bf16[256,2,2,128]{3,0,2,1:T(8,128)(2,1)S(1)}, bf16[256,2,2,128]{3,0,2,1:T(8,128)(2,1)S(1)}, u32[]{:S(2)}, u32[]{:S(2)}) collective-permute-start(bf16[256,2,2,128]{3,0,2,1:T(8,128)(2,1)S(1)} %copy.52), channel_id=1, source_target_pairs={{0,32},{16,48},{32,64},{48,80},{64,96},{80,112},{96,128},{112,144}... | collective-permute-start | bytes 786440 | tf_op jit(solution)/shard_map/ppermute | solution.py:14
  128.1 10.1 %collective-permute-start.3 = (bf16[256,2,2,128]{3,0,2,1:T(8,128)(2,1)S(1)}, bf16[256,2,2,128]{3,0,2,1:T(8,128)(2,1)S(1)}, u32[]{:S(2)}, u32[]{:S(2)}) collective-permute-start(bf16[256,2,2,128]{3,0,2,1:T(8,128)(2,1)S(1)} %copy.52), channel_id=1, source_target_pairs={{0,16},{16,32},{32,48},{48,64},{64,80},{80,96},{96,112},{112,128},... | collective-permute-start | bytes 786440 | tf_op jit(solution)/shard_map/ppermute | solution.py:14
  138.3 1.0 copy-start.1
  141.9 2.6 copy-start
  145.3 6.5 %copy-start.2 = (bf16[1280,2,2,128]{3,0,2,1:T(8,128)(2,1)S(1)}, bf16[1280,2,2,128]{3,0,2,1:T(8,128)(2,1)}, u32[]{:S(2)}) copy-start(bf16[1280,2,2,128]{3,0,2,1:T(8,128)(2,1)} %copy-done.1) | copy-start | bytes 3932164
  145.6 9.5 %collective-permute-start.7 = (bf16[256,2,2,128]{0,3,2,1:T(8,128)(2,1)S(1)}, bf16[256,2,2,128]{0,3,2,1:T(8,128)(2,1)S(1)}, u32[]{:S(2)}, u32[]{:S(2)}) collective-permute-start(bf16[256,2,2,128]{0,3,2,1:T(8,128)(2,1)S(1)} %get-tuple-element.26), channel_id=1, source_target_pairs={{64,0},{80,16},{96,32},{112,48},{128,64},{144,80},{160,96},{176,11... | collective-permute-start | bytes 786440 | tf_op jit(solution)/shard_map/ppermute | solution.py:14
  147.1 19.0 %collective-permute-start.6 = (bf16[256,2,2,128]{0,3,2,1:T(8,128)(2,1)S(1)}, bf16[256,2,2,128]{0,3,2,1:T(8,128)(2,1)S(1)}, u32[]{:S(2)}, u32[]{:S(2)}) collective-permute-start(bf16[256,2,2,128]{0,3,2,1:T(8,128)(2,1)S(1)} %get-tuple-element.27), channel_id=1, source_target_pairs={{48,0},{64,16},{80,32},{96,48},{112,64},{128,80},{144,96},{160,112... | collective-permute-start | bytes 786440 | tf_op jit(solution)/shard_map/ppermute | solution.py:14
  148.4 17.7 %collective-permute-start.5 = (bf16[256,2,2,128]{0,3,2,1:T(8,128)(2,1)S(1)}, bf16[256,2,2,128]{0,3,2,1:T(8,128)(2,1)S(1)}, u32[]{:S(2)}, u32[]{:S(2)}) collective-permute-start(bf16[256,2,2,128]{0,3,2,1:T(8,128)(2,1)S(1)} %get-tuple-element.28), channel_id=1, source_target_pairs={{32,0},{48,16},{64,32},{80,48},{96,64},{112,80},{128,96},{144,112}... | collective-permute-start | bytes 786440 | tf_op jit(solution)/shard_map/ppermute | solution.py:14
  149.7 16.4 %collective-permute-start.4 = (bf16[256,2,2,128]{0,3,2,1:T(8,128)(2,1)S(1)}, bf16[256,2,2,128]{0,3,2,1:T(8,128)(2,1)S(1)}, u32[]{:S(2)}, u32[]{:S(2)}) collective-permute-start(bf16[256,2,2,128]{0,3,2,1:T(8,128)(2,1)S(1)} %get-tuple-element.25), channel_id=1, source_target_pairs={{16,0},{32,16},{48,32},{64,48},{80,64},{96,80},{112,96},{128,112},... | collective-permute-start | bytes 786440 | tf_op jit(solution)/shard_map/ppermute | solution.py:14
  152.4 14.7 %copy-start.6 = (s32[16]{0:T(128)S(1)}, s32[16]{0:T(128)}, u32[]{:S(2)}) copy-start(s32[16]{0:T(128)} %constant.110) | copy-start | bytes 196
  179.4 6.9 %copy-start.3 = (bf16[1280,2,2,128]{3,0,2,1:T(8,128)(2,1)S(1)}, bf16[1280,2,2,128]{3,0,2,1:T(8,128)(2,1)}, u32[]{:S(2)}) copy-start(bf16[1280,2,2,128]{3,0,2,1:T(8,128)(2,1)} %copy-done.1) | copy-start | bytes 3932164
  179.4 52.5 %all-to-all-start.1 = ((bf16[256,16,256]{2,0,1:T(8,128)(2,1)}), bf16[256,16,256]{2,0,1:T(8,128)(2,1)S(1)}, u32[]{:S(2)}, u32[]{:S(2)}) async-start(bf16[256,16,256]{2,0,1:T(8,128)(2,1)} %bitcast.99), calls=%async_computation.1 | async-start | bytes 4194304 | tf_op jit(solution)/shard_map/all_to_all | solution.py:161
Sparse Core Ops, SparseCore 0:
  10.8 100.6 all-gather.2
  167.2 84.8 all-gather.4

commit v5 on v4

--- a/solution.py
+++ b/solution.py
@@ -157,11 +157,11 @@
         (((1,), (2,)), ((), ())),
         preferred_element_type=jnp.float32,
     )
-    parts = ring_blocks(parts.astype(jnp.bfloat16).reshape(local_rows, -1), inverse, 1)
-    group_parts = lax.all_to_all(
-        parts.reshape(local_rows, mp_devices, -1), "mp", split_axis=1, concat_axis=1, tiled=True
-    )
-    grad_tokens = jnp.sum(group_parts.astype(jnp.float32), axis=1).astype(jnp.bfloat16)
+    parts = jnp.take(
+        parts.astype(jnp.bfloat16).transpose(1, 0, 2), jnp.array(inverse, jnp.int32), axis=0
+    ).reshape(mp_devices, local_rows, -1)
+    group_parts = lax.all_to_all(parts, "mp", split_axis=0, concat_axis=0, tiled=True)
+    grad_tokens = jnp.sum(group_parts.astype(jnp.float32), axis=0).astype(jnp.bfloat16)
 
     gathered = lax.all_gather(dqkv, "dp", axis=0, tiled=True, axis_index_groups=[ring])
     weight_sum = lax.dot_general(

time: 271 us -> 271 us (level)
    gather x4 -> x3, local copies, waits for them, and re-layouts: 7.38 us -> 5.37 us  [ring_blocks(): jnp.take(blocks, jnp.array(ring, jnp.int32), axis=axis).reshape(shape)]
where the time goes in v5:
time: 271 us; the launch traced here: 269 us
  waiting for transfers between devices  143 us (53%)
  matrix products  37.6 us (14%)
  starting transfers between devices  35 us (13%)
  local copies, waits for them, and re-layouts  27.7 us (10%)
  between operations  14.5 us (5%)
  other arithmetic  11.2 us (4%)
    all_to_all x1, waiting for transfers between devices, on_device(): lax.all_to_all(parts, 'mp', split_axis=0, concat_axis=0, tiled=True)  42.3 us
    all_gather x1, waiting for transfers between devices, on_device(): lax.all_gather(flat_weights, 'dp', axis=0, tiled=True, axis_index_groups=...  36.4 us
    all_to_all x1, waiting for transfers between devices, on_device(): lax.all_to_all(tokens, 'dp', split_axis=1, concat_axis=0, tiled=True)  30.9 us
    ppermute x8, starting transfers between devices, shifted(): return lax.ppermute(block, axis, route)  20.3 us
    all_gather x1, waiting for transfers between devices, on_device(): lax.all_gather(dqkv, 'dp', axis=0, tiled=True, axis_index_groups=[ring])  19.3 us
    ppermute x8, waiting for transfers between devices, shifted(): return lax.ppermute(block, axis, route)  13.7 us
    unnamed x27, local copies, waits for them, and re-layouts  9.27 us
    all_to_all x1, starting transfers between devices, on_device(): lax.all_to_all(tokens, 'dp', split_axis=1, concat_axis=0, tiled=True)  7.75 us
  transfers between devices with their start and end apart: 12, of which 6 were waited for; matrix products, arithmetic and copies ran while one was open for 18% of the time, Pallas kernels for 0%

profile of v5, /device:TPU:97, one launch (start us, length us, event | category | flops | bytes accessed | tf_op | source)
XLA Modules:
  0.0 268.6 jit_solution(8229567507646361081)
XLA Ops:
  7.2 2.2 copy.46
  10.6 3.3 %copy.48 = bf16[256,4096]{0,1:T(8,128)(2,1)S(1)} copy(bf16[256,4096]{1,0:T(8,128)(2,1)} %param.11) | data formatting | bytes 4194304 | tf_op args[0]
  13.9 2.5 copy.49
  16.4 7.7 %all-to-all-start = ((bf16[256,16,256]{2,0,1:T(8,128)(2,1)}), bf16[256,16,256]{2,0,1:T(8,128)(2,1)}, u32[]{:S(2)}, u32[]{:S(2)}) async-start(bf16[256,16,256]{2,0,1:T(8,128)(2,1)} %copy.49), calls=%async_computation | async-start | bytes 4194304 | tf_op jit(solution)/shard_map/all_to_all | solution.py:70
  24.4 2.5 gather_fusion.1
  28.1 2.3 pad_maximum_fusion.1
  30.4 6.4 %copy.51 = bf16[256,16,2,256]{0,3,2,1:T(8,128)(2,1)} copy(bf16[256,16,2,256]{3,0,1,2:T(8,128)(2,1)} %pad_maximum_fusion.1) | data formatting | bytes 8388608 | tf_op jit(solution)/shard_map/concatenate | solution.py:75
  37.3 30.9 %all-to-all-done = bf16[256,16,256]{2,0,1:T(8,128)(2,1)} async-done(((bf16[256,16,256]{2,0,1:T(8,128)(2,1)}), bf16[256,16,256]{2,0,1:T(8,128)(2,1)}, u32[]{:S(2)}, u32[]{:S(2)}) %all-to-all-start) | async-done | bytes 2097184 | tf_op jit(solution)/shard_map/all_to_all | solution.py:70
  68.2 2.3 gather_fusion.2
  70.5 2.1 bitcast_select_fusion.3
  72.7 2.4 pad_maximum_fusion
  75.0 36.4 %all-gather.3.cloned.1.call-done = bf16[8192,768]{1,0:T(8,128)(2,1)} async-done(((bf16[512,768]{1,0:T(8,128)(2,1)}), bf16[8192,768]{1,0:T(8,128)(2,1)}) %all-gather.3.cloned.1.call-update) | async-done | bytes 12582928 | tf_op jit(solution)/shard_map/all_gather | solution.py:67
  111.5 7.0 %fusion.15 = bf16[256,512]{1,0:T(8,128)(2,1)S(1)} fusion(bf16[256,8192]{0,1:T(8,128)(2,1)} %bitcast.95, bf16[8192,768]{1,0:T(8,128)(2,1)} %all-gather.3.cloned.1.call-done), kind=kOutput, calls=%fused_computation.40 | convolution fusion | flops 2147614720 | bytes 12845056 | tf_op jit(solution)/shard_map/dot_general | solution.py:88
  118.6 1.4 collective-permute-start
  120.1 3.2 %collective-permute-start.1 = (bf16[256,2,2,128]{3,0,2,1:T(8,128)(2,1)S(1)}, bf16[256,2,2,128]{3,0,2,1:T(8,128)(2,1)S(1)}, u32[]{:S(2)}, u32[]{:S(2)}) collective-permute-start(bf16[256,2,2,128]{3,0,2,1:T(8,128)(2,1)S(1)} %copy.52), channel_id=1, source_target_pairs={{0,48},{16,64},{32,80},{48,96},{64,112},{80,128},{96,144},{112,160... | collective-permute-start | bytes 786440 | tf_op jit(solution)/shard_map/ppermute | solution.py:14
  123.3 4.8 %collective-permute-start.2 = (bf16[256,2,2,128]{3,0,2,1:T(8,128)(2,1)S(1)}, bf16[256,2,2,128]{3,0,2,1:T(8,128)(2,1)S(1)}, u32[]{:S(2)}, u32[]{:S(2)}) collective-permute-start(bf16[256,2,2,128]{3,0,2,1:T(8,128)(2,1)S(1)} %copy.52), channel_id=1, source_target_pairs={{0,32},{16,48},{32,64},{48,80},{64,96},{80,112},{96,128},{112,144}... | collective-permute-start | bytes 786440 | tf_op jit(solution)/shard_map/ppermute | solution.py:14
  128.1 4.7 %collective-permute-start.3 = (bf16[256,2,2,128]{3,0,2,1:T(8,128)(2,1)S(1)}, bf16[256,2,2,128]{3,0,2,1:T(8,128)(2,1)S(1)}, u32[]{:S(2)}, u32[]{:S(2)}) collective-permute-start(bf16[256,2,2,128]{3,0,2,1:T(8,128)(2,1)S(1)} %copy.52), channel_id=1, source_target_pairs={{0,16},{16,32},{32,48},{48,64},{64,80},{80,96},{96,112},{112,128},... | collective-permute-start | bytes 786440 | tf_op jit(solution)/shard_map/ppermute | solution.py:14
  132.8 5.2 %fusion.19 = bf16[256,256]{0,1:T(8,128)(2,1)S(1)} fusion(bf16[256,8192]{0,1:T(8,128)(2,1)} %bitcast.96, bf16[8192,768]{1,0:T(8,128)(2,1)} %all-gather.3.cloned.1.call-done), kind=kOutput, calls=%fused_computation.43 | convolution fusion | flops 1073807360 | bytes 8519680 | tf_op jit(solution)/shard_map/dot_general | solution.py:96
  139.3 2.6 fusion.33
  141.9 2.2 multiply_reduce_fusion
  149.7 2.1 collective-permute-start.4
  152.4 2.7 %collective-permute-done.7 = bf16[256,2,2,128]{0,3,2,1:T(8,128)(2,1)S(1)} collective-permute-done((bf16[256,2,2,128]{0,3,2,1:T(8,128)(2,1)S(1)}, bf16[256,2,2,128]{0,3,2,1:T(8,128)(2,1)S(1)}, u32[]{:S(2)}, u32[]{:S(2)}) %collective-permute-start.7) | collective-permute-done | bytes 262176 | tf_op jit(solution)/shard_map/ppermute | solution.py:14
  155.1 10.9 %collective-permute-done.6 = bf16[256,2,2,128]{0,3,2,1:T(8,128)(2,1)S(1)} collective-permute-done((bf16[256,2,2,128]{0,3,2,1:T(8,128)(2,1)S(1)}, bf16[256,2,2,128]{0,3,2,1:T(8,128)(2,1)S(1)}, u32[]{:S(2)}, u32[]{:S(2)}) %collective-permute-start.6) | collective-permute-done | bytes 262176 | tf_op jit(solution)/shard_map/ppermute | solution.py:14
  168.1 4.6 %fusion.3 = f32[256,16,256]{2,0,1:T(8,128)S(1)} fusion(bf16[256,768,1]{0,1,2:T(8,128)(2,1)S(1)} %bitcast.105, bf16[16,2,256,768]{3,2,1,0:T(8,128)(2,1)} %bitcast.98), kind=kOutput, calls=%fused_computation.8 | convolution fusion | flops 1610612736 | bytes 10878976 | tf_op jit(solution)/shard_map/dot_general | solution.py:154
  172.8 4.6 %fusion.13 = bf16[16,256,256]{2,1,0:T(8,128)(2,1)S(1)} fusion(f32[256,16,256]{2,0,1:T(8,128)S(1)} %fusion.3, bf16[256,768,1]{0,1,2:T(8,128)(2,1)S(1)} %bitcast.103, bf16[16,2,256,768]{3,2,1,0:T(8,128)(2,1)} %bitcast.99), kind=kOutput, calls=%fused_computation.31 | convolution fusion | flops 1612709888 | bytes 12976128 | tf_op jit(solution)/shard_map/dot_general | solution.py:149
  177.4 2.0 gather_fusion.3
  179.4 6.9 %all-to-all-start.1 = ((bf16[16,256,256]{2,1,0:T(8,128)(2,1)}), bf16[16,256,256]{2,1,0:T(8,128)(2,1)S(1)}, u32[]{:S(2)}, u32[]{:S(2)}) async-start(bf16[16,256,256]{2,1,0:T(8,128)(2,1)} %gather_fusion.3), calls=%async_computation.1 | async-start | bytes 4194304 | tf_op jit(solution)/shard_map/all_to_all | solution.py:163
  186.4 2.4 convolution_convert_fusion.1
  189.6 42.3 %all-to-all-done.1 = bf16[16,256,256]{2,1,0:T(8,128)(2,1)S(1)} async-done(((bf16[16,256,256]{2,1,0:T(8,128)(2,1)}), bf16[16,256,256]{2,1,0:T(8,128)(2,1)S(1)}, u32[]{:S(2)}, u32[]{:S(2)}) %all-to-all-start.1) | async-done | bytes 2097184 | tf_op jit(solution)/shard_map/all_to_all | solution.py:163
  232.9 19.3 %all-gather.5.cloned.1.call-done = bf16[4096,768]{0,1:T(8,128)(2,1)} async-done(((bf16[256,768]{0,1:T(8,128)(2,1)}), bf16[4096,768]{0,1:T(8,128)(2,1)}) %all-gather.5.cloned.1.call-update) | async-done | bytes 6291472 | tf_op jit(solution)/shard_map/all_gather | solution.py:166
  252.1 7.5 %convolution_convert_fusion = bf16[512,768]{1,0:T(8,128)(2,1)S(1)} fusion(bf16[4096,512]{1,0:T(8,128)(2,1)} %pad_maximum_fusion, bf16[4096,768]{0,1:T(8,128)(2,1)} %all-gather.5.cloned.1.call-done), kind=kOutput, calls=%fused_computation.36 | convolution fusion | flops 3221618688 | bytes 11272192 | tf_op jit(solution)/shard_map/dot_general | solution.py:167
  259.9 1.8 copy.69
  (66 shorter events, 14.6 us)
Async XLA Ops:
  7.2 104.3 %all-gather.3.cloned.1.call-start = ((), (), s32[]{:S(2)}) async-start(), calls=%async_computation.2 | async-start | bytes 13369344 | tf_op jit(solution)/shard_map/all_gather | solution.py:67
  16.4 7.8 %copy-start.8 = (s32[32]{0:T(128)S(1)}, s32[32]{0:T(128)}, u32[]{:S(2)}) copy-start(s32[32]{0:T(128)} %param.13) | copy-start | bytes 388
  16.4 8.0 %copy-start.7 = (s32[16]{0:T(128)S(1)}, s32[16]{0:T(128)}, u32[]{:S(2)}) copy-start(s32[16]{0:T(128)} %constant.77.clone) | copy-start | bytes 196
  16.4 51.9 %all-to-all-start = ((bf16[256,16,256]{2,0,1:T(8,128)(2,1)}), bf16[256,16,256]{2,0,1:T(8,128)(2,1)}, u32[]{:S(2)}, u32[]{:S(2)}) async-start(bf16[256,16,256]{2,0,1:T(8,128)(2,1)} %copy.49), calls=%async_computation | async-start | bytes 4194304 | tf_op jit(solution)/shard_map/all_to_all | solution.py:70
  24.1 228.0 %all-gather.5.cloned.1.call-start = ((), (), s32[]{:S(2)}) async-start(), calls=%async_computation.3 | async-start | bytes 6684672 | tf_op jit(solution)/shard_map/all_gather | solution.py:166
  30.3 6.4 %copy-start.5 = (s32[4096]{0:T(1024)S(1)}, s32[4096]{0:T(1024)}, u32[]{:S(2)}) copy-start(s32[4096]{0:T(1024)} %param.14) | copy-start | bytes 49156
  30.4 6.5 %copy-start.4 = (bf16[256,256]{1,0:T(8,128)(2,1)S(1)}, bf16[256,256]{1,0:T(8,128)(2,1)}, u32[]{:S(2)}) copy-start(bf16[256,256]{1,0:T(8,128)(2,1)} %param.15) | copy-start | bytes 393220
  118.6 19.4 %collective-permute-start = (bf16[256,2,2,128]{3,0,2,1:T(8,128)(2,1)S(1)}, bf16[256,2,2,128]{3,0,2,1:T(8,128)(2,1)S(1)}, u32[]{:S(2)}, u32[]{:S(2)}) collective-permute-start(bf16[256,2,2,128]{3,0,2,1:T(8,128)(2,1)S(1)} %copy.52), channel_id=1, source_target_pairs={{0,64},{16,80},{32,96},{48,112},{64,128},{80,144},{96,160},{112,17... | collective-permute-start | bytes 786440 | tf_op jit(solution)/shard_map/ppermute | solution.py:14
  120.1 18.0 %collective-permute-start.1 = (bf16[256,2,2,128]{3,0,2,1:T(8,128)(2,1)S(1)}, bf16[256,2,2,128]{3,0,2,1:T(8,128)(2,1)S(1)}, u32[]{:S(2)}, u32[]{:S(2)}) collective-permute-start(bf16[256,2,2,128]{3,0,2,1:T(8,128)(2,1)S(1)} %copy.52), channel_id=1, source_target_pairs={{0,48},{16,64},{32,80},{48,96},{64,112},{80,128},{96,144},{112,160... | collective-permute-start | bytes 786440 | tf_op jit(solution)/shard_map/ppermute | solution.py:14
  123.3 14.8 %collective-permute-start.2 = (bf16[256,2,2,128]{3,0,2,1:T(8,128)(2,1)S(1)}, bf16[256,2,2,128]{3,0,2,1:T(8,128)(2,1)S(1)}, u32[]{:S(2)}, u32[]{:S(2)}) collective-permute-start(bf16[256,2,2,128]{3,0,2,1:T(8,128)(2,1)S(1)} %copy.52), channel_id=1, source_target_pairs={{0,32},{16,48},{32,64},{48,80},{64,96},{80,112},{96,128},{112,144}... | collective-permute-start | bytes 786440 | tf_op jit(solution)/shard_map/ppermute | solution.py:14
  128.1 10.1 %collective-permute-start.3 = (bf16[256,2,2,128]{3,0,2,1:T(8,128)(2,1)S(1)}, bf16[256,2,2,128]{3,0,2,1:T(8,128)(2,1)S(1)}, u32[]{:S(2)}, u32[]{:S(2)}) collective-permute-start(bf16[256,2,2,128]{3,0,2,1:T(8,128)(2,1)S(1)} %copy.52), channel_id=1, source_target_pairs={{0,16},{16,32},{32,48},{48,64},{64,80},{80,96},{96,112},{112,128},... | collective-permute-start | bytes 786440 | tf_op jit(solution)/shard_map/ppermute | solution.py:14
  138.3 1.0 copy-start.1
  141.9 2.6 copy-start
  145.3 6.5 %copy-start.2 = (bf16[1280,2,2,128]{3,0,2,1:T(8,128)(2,1)S(1)}, bf16[1280,2,2,128]{3,0,2,1:T(8,128)(2,1)}, u32[]{:S(2)}) copy-start(bf16[1280,2,2,128]{3,0,2,1:T(8,128)(2,1)} %copy-done.1) | copy-start | bytes 3932164
  145.6 9.5 %collective-permute-start.7 = (bf16[256,2,2,128]{0,3,2,1:T(8,128)(2,1)S(1)}, bf16[256,2,2,128]{0,3,2,1:T(8,128)(2,1)S(1)}, u32[]{:S(2)}, u32[]{:S(2)}) collective-permute-start(bf16[256,2,2,128]{0,3,2,1:T(8,128)(2,1)S(1)} %get-tuple-element.26), channel_id=1, source_target_pairs={{64,0},{80,16},{96,32},{112,48},{128,64},{144,80},{160,96},{176,11... | collective-permute-start | bytes 786440 | tf_op jit(solution)/shard_map/ppermute | solution.py:14
  147.1 19.0 %collective-permute-start.6 = (bf16[256,2,2,128]{0,3,2,1:T(8,128)(2,1)S(1)}, bf16[256,2,2,128]{0,3,2,1:T(8,128)(2,1)S(1)}, u32[]{:S(2)}, u32[]{:S(2)}) collective-permute-start(bf16[256,2,2,128]{0,3,2,1:T(8,128)(2,1)S(1)} %get-tuple-element.27), channel_id=1, source_target_pairs={{48,0},{64,16},{80,32},{96,48},{112,64},{128,80},{144,96},{160,112... | collective-permute-start | bytes 786440 | tf_op jit(solution)/shard_map/ppermute | solution.py:14
  148.4 17.7 %collective-permute-start.5 = (bf16[256,2,2,128]{0,3,2,1:T(8,128)(2,1)S(1)}, bf16[256,2,2,128]{0,3,2,1:T(8,128)(2,1)S(1)}, u32[]{:S(2)}, u32[]{:S(2)}) collective-permute-start(bf16[256,2,2,128]{0,3,2,1:T(8,128)(2,1)S(1)} %get-tuple-element.28), channel_id=1, source_target_pairs={{32,0},{48,16},{64,32},{80,48},{96,64},{112,80},{128,96},{144,112}... | collective-permute-start | bytes 786440 | tf_op jit(solution)/shard_map/ppermute | solution.py:14
  149.7 16.4 %collective-permute-start.4 = (bf16[256,2,2,128]{0,3,2,1:T(8,128)(2,1)S(1)}, bf16[256,2,2,128]{0,3,2,1:T(8,128)(2,1)S(1)}, u32[]{:S(2)}, u32[]{:S(2)}) collective-permute-start(bf16[256,2,2,128]{0,3,2,1:T(8,128)(2,1)S(1)} %get-tuple-element.25), channel_id=1, source_target_pairs={{16,0},{32,16},{48,32},{64,48},{80,64},{96,80},{112,96},{128,112},... | collective-permute-start | bytes 786440 | tf_op jit(solution)/shard_map/ppermute | solution.py:14
  152.4 14.7 %copy-start.6 = (s32[16]{0:T(128)S(1)}, s32[16]{0:T(128)}, u32[]{:S(2)}) copy-start(s32[16]{0:T(128)} %constant.110) | copy-start | bytes 196
  179.4 6.9 %copy-start.3 = (bf16[1280,2,2,128]{3,0,2,1:T(8,128)(2,1)S(1)}, bf16[1280,2,2,128]{3,0,2,1:T(8,128)(2,1)}, u32[]{:S(2)}) copy-start(bf16[1280,2,2,128]{3,0,2,1:T(8,128)(2,1)} %copy-done.1) | copy-start | bytes 3932164
  179.4 52.5 %all-to-all-start.1 = ((bf16[16,256,256]{2,1,0:T(8,128)(2,1)}), bf16[16,256,256]{2,1,0:T(8,128)(2,1)S(1)}, u32[]{:S(2)}, u32[]{:S(2)}) async-start(bf16[16,256,256]{2,1,0:T(8,128)(2,1)} %gather_fusion.3), calls=%async_computation.1 | async-start | bytes 4194304 | tf_op jit(solution)/shard_map/all_to_all | solution.py:163
Sparse Core Ops, SparseCore 0:
  10.8 100.6 all-gather.2
  167.2 84.8 all-gather.4

commit v6 on v5

--- a/solution.py
+++ b/solution.py
@@ -89,14 +89,15 @@
         .astype(jnp.bfloat16)
         .reshape(local_rows, 2, head_count, HD)
     )
-    received = []
-    for distance in range(SPAN, 0, -1):
-        received.append(shifted(key_values, "dp", distance))
     queries = (
         jnp.dot(ring_tokens, stacked_weights[:, :head_width], preferred_element_type=jnp.float32)
         .astype(jnp.bfloat16)
         .reshape(local_rows, head_count, HD)
     )
+    sent_values, queries = lax.optimization_barrier((key_values, queries))
+    received = []
+    for distance in range(SPAN, 0, -1):
+        received.append(shifted(sent_values, "dp", distance))
     window = jnp.concatenate(received + [key_values], 0)
     key_rows = window[:, 0]
     value_rows = window[:, 1]

time: 271 us -> 275 us (1.015)
    unnamed x27 -> x23, local copies, waits for them, and re-layouts: 9.27 us -> 11.1 us
  transfers between devices with their start and end apart: 12 -> 12, of which waited for: 6 -> 7; matrix products, arithmetic and copies ran while one was open for 18% -> 17% of each run, Pallas kernels for 0% -> 0%
where the time goes in v6:
time: 275 us; the launch traced here: 274 us
  waiting for transfers between devices  145 us (53%)
  matrix products  37.9 us (14%)
  starting transfers between devices  34.7 us (13%)
  local copies, waits for them, and re-layouts  30.3 us (11%)
  between operations  14.4 us (5%)
  other arithmetic  11.2 us (4%)
    all_to_all x1, waiting for transfers between devices, on_device(): lax.all_to_all(parts, 'mp', split_axis=0, concat_axis=0, tiled=True)  41.8 us
    all_gather x1, waiting for transfers between devices, on_device(): lax.all_gather(flat_weights, 'dp', axis=0, tiled=True, axis_index_groups=...  36.4 us
    all_to_all x1, waiting for transfers between devices, on_device(): lax.all_to_all(tokens, 'dp', split_axis=1, concat_axis=0, tiled=True)  31.4 us
    ppermute x8, starting transfers between devices, shifted(): return lax.ppermute(block, axis, route)  20.1 us
    all_gather x1, waiting for transfers between devices, on_device(): lax.all_gather(dqkv, 'dp', axis=0, tiled=True, axis_index_groups=[ring])  19.7 us
    ppermute x8, waiting for transfers between devices, shifted(): return lax.ppermute(block, axis, route)  16 us
    unnamed x23, local copies, waits for them, and re-layouts  11.1 us
    all_to_all x1, starting transfers between devices, on_device(): lax.all_to_all(tokens, 'dp', split_axis=1, concat_axis=0, tiled=True)  7.75 us
  transfers between devices with their start and end apart: 12, of which 7 were waited for; matrix products, arithmetic and copies ran while one was open for 17% of the time, Pallas kernels for 0%

profile of v6, /device:TPU:97, one launch (start us, length us, event | category | flops | bytes accessed | tf_op | source)
XLA Modules:
  0.0 273.8 jit_solution(18026385252446908178)
XLA Ops:
  7.2 2.2 copy.46
  10.6 3.3 %copy.48 = bf16[256,4096]{0,1:T(8,128)(2,1)S(1)} copy(bf16[256,4096]{1,0:T(8,128)(2,1)} %param.11) | data formatting | bytes 4194304 | tf_op args[0]
  13.9 2.4 copy.49
  16.4 7.7 %all-to-all-start = ((bf16[256,16,256]{2,0,1:T(8,128)(2,1)}), bf16[256,16,256]{2,0,1:T(8,128)(2,1)}, u32[]{:S(2)}, u32[]{:S(2)}) async-start(bf16[256,16,256]{2,0,1:T(8,128)(2,1)} %copy.49), calls=%async_computation | async-start | bytes 4194304 | tf_op jit(solution)/shard_map/all_to_all | solution.py:70
  24.4 2.5 gather_fusion.1
  28.1 2.3 pad_maximum_fusion.1
  30.4 6.4 %copy.51 = bf16[256,16,2,256]{0,3,2,1:T(8,128)(2,1)} copy(bf16[256,16,2,256]{3,0,1,2:T(8,128)(2,1)} %pad_maximum_fusion.1) | data formatting | bytes 8388608 | tf_op jit(solution)/shard_map/concatenate | solution.py:75
  36.9 31.4 %all-to-all-done = bf16[256,16,256]{2,0,1:T(8,128)(2,1)} async-done(((bf16[256,16,256]{2,0,1:T(8,128)(2,1)}), bf16[256,16,256]{2,0,1:T(8,128)(2,1)}, u32[]{:S(2)}, u32[]{:S(2)}) %all-to-all-start) | async-done | bytes 2097184 | tf_op jit(solution)/shard_map/all_to_all | solution.py:70
  68.3 2.3 gather_fusion.2
  70.5 2.1 bitcast_select_fusion.3
  72.7 2.4 pad_maximum_fusion
  75.1 36.4 %all-gather.3.cloned.1.call-done = bf16[8192,768]{1,0:T(8,128)(2,1)} async-done(((bf16[512,768]{1,0:T(8,128)(2,1)}), bf16[8192,768]{1,0:T(8,128)(2,1)}) %all-gather.3.cloned.1.call-update) | async-done | bytes 12582928 | tf_op jit(solution)/shard_map/all_gather | solution.py:67
  111.5 7.1 %fusion.15 = bf16[256,512]{1,0:T(8,128)(2,1)S(1)} fusion(bf16[256,8192]{0,1:T(8,128)(2,1)} %bitcast.95, bf16[8192,768]{1,0:T(8,128)(2,1)} %all-gather.3.cloned.1.call-done), kind=kOutput, calls=%fused_computation.40 | convolution fusion | flops 2147614720 | bytes 12845056 | tf_op jit(solution)/shard_map/dot_general | solution.py:88
  118.7 4.1 %fusion.19 = bf16[256,256]{0,1:T(8,128)(2,1)S(1)} fusion(bf16[256,8192]{0,1:T(8,128)(2,1)S(1)} %bitcast.96, bf16[8192,768]{1,0:T(8,128)(2,1)} %all-gather.3.cloned.1.call-done), kind=kOutput, calls=%fused_computation.43 | convolution fusion | flops 1073807360 | bytes 8519680 | tf_op jit(solution)/shard_map/dot_general | solution.py:93
  124.3 3.2 %collective-permute-start.1 = (bf16[256,2,2,128]{3,0,2,1:T(8,128)(2,1)S(1)}, bf16[256,2,2,128]{3,0,2,1:T(8,128)(2,1)S(1)}, u32[]{:S(2)}, u32[]{:S(2)}) collective-permute-start(bf16[256,2,2,128]{3,0,2,1:T(8,128)(2,1)S(1)} %copy.52), channel_id=1, source_target_pairs={{0,48},{16,64},{32,80},{48,96},{64,112},{80,128},{96,144},{112,160... | collective-permute-start | bytes 786440 | tf_op jit(solution)/shard_map/ppermute | solution.py:14
  127.5 4.8 %collective-permute-start.2 = (bf16[256,2,2,128]{3,0,2,1:T(8,128)(2,1)S(1)}, bf16[256,2,2,128]{3,0,2,1:T(8,128)(2,1)S(1)}, u32[]{:S(2)}, u32[]{:S(2)}) collective-permute-start(bf16[256,2,2,128]{3,0,2,1:T(8,128)(2,1)S(1)} %copy.52), channel_id=1, source_target_pairs={{0,32},{16,48},{32,64},{48,80},{64,96},{80,112},{96,128},{112,144}... | collective-permute-start | bytes 786440 | tf_op jit(solution)/shard_map/ppermute | solution.py:14
  132.7 4.7 %collective-permute-start.3 = (bf16[256,2,2,128]{3,0,2,1:T(8,128)(2,1)S(1)}, bf16[256,2,2,128]{3,0,2,1:T(8,128)(2,1)S(1)}, u32[]{:S(2)}, u32[]{:S(2)}) collective-permute-start(bf16[256,2,2,128]{3,0,2,1:T(8,128)(2,1)S(1)} %copy.52), channel_id=1, source_target_pairs={{0,16},{16,32},{32,48},{48,64},{64,80},{80,96},{96,112},{112,128},... | collective-permute-start | bytes 786440 | tf_op jit(solution)/shard_map/ppermute | solution.py:14
  142.9 2.6 fusion.33
  145.4 2.2 multiply_reduce_fusion
  153.3 1.9 collective-permute-start.4
  155.2 1.7 fusion.18
  156.9 3.4 %collective-permute-done.7 = bf16[256,2,2,128]{0,3,2,1:T(8,128)(2,1)S(1)} collective-permute-done((bf16[256,2,2,128]{0,3,2,1:T(8,128)(2,1)S(1)}, bf16[256,2,2,128]{0,3,2,1:T(8,128)(2,1)S(1)}, u32[]{:S(2)}, u32[]{:S(2)}) %collective-permute-start.7) | collective-permute-done | bytes 262176 | tf_op jit(solution)/shard_map/ppermute | solution.py:14
  160.3 10.9 %collective-permute-done.6 = bf16[256,2,2,128]{0,3,2,1:T(8,128)(2,1)S(1)} collective-permute-done((bf16[256,2,2,128]{0,3,2,1:T(8,128)(2,1)S(1)}, bf16[256,2,2,128]{0,3,2,1:T(8,128)(2,1)S(1)}, u32[]{:S(2)}, u32[]{:S(2)}) %collective-permute-start.6) | collective-permute-done | bytes 262176 | tf_op jit(solution)/shard_map/ppermute | solution.py:14
  173.3 4.6 %fusion.3 = f32[256,16,256]{2,0,1:T(8,128)S(1)} fusion(bf16[256,768,1]{0,1,2:T(8,128)(2,1)S(1)} %bitcast.105, bf16[16,2,256,768]{3,2,1,0:T(8,128)(2,1)} %bitcast.98), kind=kOutput, calls=%fused_computation.8 | convolution fusion | flops 1610612736 | bytes 10878976 | tf_op jit(solution)/shard_map/dot_general | solution.py:155
  177.9 4.6 %fusion.13 = bf16[16,256,256]{2,1,0:T(8,128)(2,1)S(1)} fusion(f32[256,16,256]{2,0,1:T(8,128)S(1)} %fusion.3, bf16[256,768,1]{0,1,2:T(8,128)(2,1)S(1)} %bitcast.103, bf16[16,2,256,768]{3,2,1,0:T(8,128)(2,1)} %bitcast.99), kind=kOutput, calls=%fused_computation.31 | convolution fusion | flops 1612709888 | bytes 12976128 | tf_op jit(solution)/shard_map/dot_general | solution.py:150
  182.6 2.0 gather_fusion.3
  184.6 6.8 %all-to-all-start.1 = ((bf16[16,256,256]{2,1,0:T(8,128)(2,1)}), bf16[16,256,256]{2,1,0:T(8,128)(2,1)S(1)}, u32[]{:S(2)}, u32[]{:S(2)}) async-start(bf16[16,256,256]{2,1,0:T(8,128)(2,1)} %gather_fusion.3), calls=%async_computation.1 | async-start | bytes 4194304 | tf_op jit(solution)/shard_map/all_to_all | solution.py:164
  191.4 2.7 convolution_convert_fusion.1
  194.8 41.8 %all-to-all-done.1 = bf16[16,256,256]{2,1,0:T(8,128)(2,1)S(1)} async-done(((bf16[16,256,256]{2,1,0:T(8,128)(2,1)}), bf16[16,256,256]{2,1,0:T(8,128)(2,1)S(1)}, u32[]{:S(2)}, u32[]{:S(2)}) %all-to-all-start.1) | async-done | bytes 2097184 | tf_op jit(solution)/shard_map/all_to_all | solution.py:164
  237.6 19.7 %all-gather.5.cloned.1.call-done = bf16[4096,768]{0,1:T(8,128)(2,1)} async-done(((bf16[256,768]{0,1:T(8,128)(2,1)}), bf16[4096,768]{0,1:T(8,128)(2,1)}) %all-gather.5.cloned.1.call-update) | async-done | bytes 6291472 | tf_op jit(solution)/shard_map/all_gather | solution.py:167
  257.3 7.5 %convolution_convert_fusion = bf16[512,768]{1,0:T(8,128)(2,1)S(1)} fusion(bf16[4096,512]{1,0:T(8,128)(2,1)} %pad_maximum_fusion, bf16[4096,768]{0,1:T(8,128)(2,1)} %all-gather.5.cloned.1.call-done), kind=kOutput, calls=%fused_computation.36 | convolution fusion | flops 3221618688 | bytes 11272192 | tf_op jit(solution)/shard_map/dot_general | solution.py:168
  265.1 1.8 copy.69
  (62 shorter events, 19.7 us)
Async XLA Ops:
  7.2 104.3 %all-gather.3.cloned.1.call-start = ((), (), s32[]{:S(2)}) async-start(), calls=%async_computation.2 | async-start | bytes 13369344 | tf_op jit(solution)/shard_map/all_gather | solution.py:67
  16.4 7.8 %copy-start.6 = (s32[32]{0:T(128)S(1)}, s32[32]{0:T(128)}, u32[]{:S(2)}) copy-start(s32[32]{0:T(128)} %param.13) | copy-start | bytes 388
  16.4 8.0 %copy-start.5 = (s32[16]{0:T(128)S(1)}, s32[16]{0:T(128)}, u32[]{:S(2)}) copy-start(s32[16]{0:T(128)} %constant.77.clone) | copy-start | bytes 196
  16.4 51.9 %all-to-all-start = ((bf16[256,16,256]{2,0,1:T(8,128)(2,1)}), bf16[256,16,256]{2,0,1:T(8,128)(2,1)}, u32[]{:S(2)}, u32[]{:S(2)}) async-start(bf16[256,16,256]{2,0,1:T(8,128)(2,1)} %copy.49), calls=%async_computation | async-start | bytes 4194304 | tf_op jit(solution)/shard_map/all_to_all | solution.py:70
  24.1 233.2 %all-gather.5.cloned.1.call-start = ((), (), s32[]{:S(2)}) async-start(), calls=%async_computation.3 | async-start | bytes 6684672 | tf_op jit(solution)/shard_map/all_gather | solution.py:167
  30.4 6.4 %copy-start.3 = (s32[4096]{0:T(1024)S(1)}, s32[4096]{0:T(1024)}, u32[]{:S(2)}) copy-start(s32[4096]{0:T(1024)} %param.14) | copy-start | bytes 49156
  111.5 7.1 %copy-start = (bf16[256,16,2,256]{0,3,2,1:T(8,128)(2,1)S(1)}, bf16[256,16,2,256]{0,3,2,1:T(8,128)(2,1)}, u32[]{:S(2)}) copy-start(bf16[256,16,2,256]{0,3,2,1:T(8,128)(2,1)} %copy.51) | copy-start | bytes 12582916
  118.6 14.0 %copy-start.2 = (bf16[256,256]{1,0:T(8,128)(2,1)S(1)}, bf16[256,256]{1,0:T(8,128)(2,1)}, u32[]{:S(2)}) copy-start(bf16[256,256]{1,0:T(8,128)(2,1)} %param.15) | copy-start | bytes 393220
  122.9 14.6 %collective-permute-start = (bf16[256,2,2,128]{3,0,2,1:T(8,128)(2,1)S(1)}, bf16[256,2,2,128]{3,0,2,1:T(8,128)(2,1)S(1)}, u32[]{:S(2)}, u32[]{:S(2)}) collective-permute-start(bf16[256,2,2,128]{3,0,2,1:T(8,128)(2,1)S(1)} %copy.52), channel_id=1, source_target_pairs={{0,64},{16,80},{32,96},{48,112},{64,128},{80,144},{96,160},{112,17... | collective-permute-start | bytes 786440 | tf_op jit(solution)/shard_map/ppermute | solution.py:14
  124.3 13.9 %collective-permute-start.1 = (bf16[256,2,2,128]{3,0,2,1:T(8,128)(2,1)S(1)}, bf16[256,2,2,128]{3,0,2,1:T(8,128)(2,1)S(1)}, u32[]{:S(2)}, u32[]{:S(2)}) collective-permute-start(bf16[256,2,2,128]{3,0,2,1:T(8,128)(2,1)S(1)} %copy.52), channel_id=1, source_target_pairs={{0,48},{16,64},{32,80},{48,96},{64,112},{80,128},{96,144},{112,160... | collective-permute-start | bytes 786440 | tf_op jit(solution)/shard_map/ppermute | solution.py:14
  127.5 11.5 %collective-permute-start.2 = (bf16[256,2,2,128]{3,0,2,1:T(8,128)(2,1)S(1)}, bf16[256,2,2,128]{3,0,2,1:T(8,128)(2,1)S(1)}, u32[]{:S(2)}, u32[]{:S(2)}) collective-permute-start(bf16[256,2,2,128]{3,0,2,1:T(8,128)(2,1)S(1)} %copy.52), channel_id=1, source_target_pairs={{0,32},{16,48},{32,64},{48,80},{64,96},{80,112},{96,128},{112,144}... | collective-permute-start | bytes 786440 | tf_op jit(solution)/shard_map/ppermute | solution.py:14
  132.7 8.6 %collective-permute-start.3 = (bf16[256,2,2,128]{3,0,2,1:T(8,128)(2,1)S(1)}, bf16[256,2,2,128]{3,0,2,1:T(8,128)(2,1)S(1)}, u32[]{:S(2)}, u32[]{:S(2)}) collective-permute-start(bf16[256,2,2,128]{3,0,2,1:T(8,128)(2,1)S(1)} %copy.52), channel_id=1, source_target_pairs={{0,16},{16,32},{32,48},{48,64},{64,80},{80,96},{96,112},{112,128},... | collective-permute-start | bytes 786440 | tf_op jit(solution)/shard_map/ppermute | solution.py:14
  145.4 2.6 copy-start.1
  149.2 11.1 %collective-permute-start.7 = (bf16[256,2,2,128]{0,3,2,1:T(8,128)(2,1)S(1)}, bf16[256,2,2,128]{0,3,2,1:T(8,128)(2,1)S(1)}, u32[]{:S(2)}, u32[]{:S(2)}) collective-permute-start(bf16[256,2,2,128]{0,3,2,1:T(8,128)(2,1)S(1)} %get-tuple-element.30), channel_id=1, source_target_pairs={{64,0},{80,16},{96,32},{112,48},{128,64},{144,80},{160,96},{176,11... | collective-permute-start | bytes 786440 | tf_op jit(solution)/shard_map/ppermute | solution.py:14
  150.5 20.7 %collective-permute-start.6 = (bf16[256,2,2,128]{0,3,2,1:T(8,128)(2,1)S(1)}, bf16[256,2,2,128]{0,3,2,1:T(8,128)(2,1)S(1)}, u32[]{:S(2)}, u32[]{:S(2)}) collective-permute-start(bf16[256,2,2,128]{0,3,2,1:T(8,128)(2,1)S(1)} %get-tuple-element.31), channel_id=1, source_target_pairs={{48,0},{64,16},{80,32},{96,48},{112,64},{128,80},{144,96},{160,112... | collective-permute-start | bytes 786440 | tf_op jit(solution)/shard_map/ppermute | solution.py:14
  151.8 19.4 %collective-permute-start.5 = (bf16[256,2,2,128]{0,3,2,1:T(8,128)(2,1)S(1)}, bf16[256,2,2,128]{0,3,2,1:T(8,128)(2,1)S(1)}, u32[]{:S(2)}, u32[]{:S(2)}) collective-permute-start(bf16[256,2,2,128]{0,3,2,1:T(8,128)(2,1)S(1)} %get-tuple-element.32), channel_id=1, source_target_pairs={{32,0},{48,16},{64,32},{80,48},{96,64},{112,80},{128,96},{144,112}... | collective-permute-start | bytes 786440 | tf_op jit(solution)/shard_map/ppermute | solution.py:14
  153.3 17.9 %collective-permute-start.4 = (bf16[256,2,2,128]{0,3,2,1:T(8,128)(2,1)S(1)}, bf16[256,2,2,128]{0,3,2,1:T(8,128)(2,1)S(1)}, u32[]{:S(2)}, u32[]{:S(2)}) collective-permute-start(bf16[256,2,2,128]{0,3,2,1:T(8,128)(2,1)S(1)} %get-tuple-element.29), channel_id=1, source_target_pairs={{16,0},{32,16},{48,32},{64,48},{80,64},{96,80},{112,96},{128,112},... | collective-permute-start | bytes 786440 | tf_op jit(solution)/shard_map/ppermute | solution.py:14
  156.9 15.4 %copy-start.4 = (s32[16]{0:T(128)S(1)}, s32[16]{0:T(128)}, u32[]{:S(2)}) copy-start(s32[16]{0:T(128)} %constant.110) | copy-start | bytes 196
  184.6 52.0 %all-to-all-start.1 = ((bf16[16,256,256]{2,1,0:T(8,128)(2,1)}), bf16[16,256,256]{2,1,0:T(8,128)(2,1)S(1)}, u32[]{:S(2)}, u32[]{:S(2)}) async-start(bf16[16,256,256]{2,1,0:T(8,128)(2,1)} %gather_fusion.3), calls=%async_computation.1 | async-start | bytes 4194304 | tf_op jit(solution)/shard_map/all_to_all | solution.py:164
Sparse Core Ops, SparseCore 0:
  10.8 100.6 all-gather.2
  172.4 84.9 all-gather.4

commit v7 on v5

--- a/solution.py
+++ b/solution.py
@@ -145,17 +145,14 @@
         .reshape(local_rows, 3 * head_width)
     )
 
-    zeros = jnp.zeros_like(dqkv)
-    parts = lax.dot_general(
-        jnp.where(my_image[:, None], zeros, dqkv),
-        block_weights[:, 0],
-        (((1,), (2,)), ((), ())),
-        preferred_element_type=jnp.float32,
-    ) + lax.dot_general(
-        jnp.where(my_image[:, None], dqkv, zeros),
-        block_weights[:, 1],
-        (((1,), (2,)), ((), ())),
-        preferred_element_type=jnp.float32,
+    parts = jnp.where(
+        my_image[:, None, None],
+        lax.dot_general(
+            dqkv, block_weights[:, 1], (((1,), (2,)), ((), ())), preferred_element_type=jnp.float32
+        ),
+        lax.dot_general(
+            dqkv, block_weights[:, 0], (((1,), (2,)), ((), ())), preferred_element_type=jnp.float32
+        ),
     )
     parts = jnp.take(
         parts.astype(jnp.bfloat16).transpose(1, 0, 2), jnp.array(inverse, jnp.int32), axis=0

time: 271 us -> 271 us (level)
    unnamed x27 -> x29, local copies, waits for them, and re-layouts: 9.27 us -> 9.28 us
where the time goes in v7:
time: 271 us; the launch traced here: 268 us
  waiting for transfers between devices  143 us (53%)
  matrix products  38.1 us (14%)
  starting transfers between devices  35 us (13%)
  local copies, waits for them, and re-layouts  27.7 us (10%)
  between operations  14.5 us (5%)
  other arithmetic  10.1 us (4%)
    all_to_all x1, waiting for transfers between devices, on_device(): lax.all_to_all(parts, 'mp', split_axis=0, concat_axis=0, tiled=True)  42.3 us
    all_gather x1, waiting for transfers between devices, on_device(): lax.all_gather(flat_weights, 'dp', axis=0, tiled=True, axis_index_groups=...  36.4 us
    all_to_all x1, waiting for transfers between devices, on_device(): lax.all_to_all(tokens, 'dp', split_axis=1, concat_axis=0, tiled=True)  30.9 us
    ppermute x8, starting transfers between devices, shifted(): return lax.ppermute(block, axis, route)  20.3 us
    all_gather x1, waiting for transfers between devices, on_device(): lax.all_gather(dqkv, 'dp', axis=0, tiled=True, axis_index_groups=[ring])  19.4 us
    ppermute x8, waiting for transfers between devices, shifted(): return lax.ppermute(block, axis, route)  13.7 us
    unnamed x29, local copies, waits for them, and re-layouts  9.28 us
    all_to_all x1, starting transfers between devices, on_device(): lax.all_to_all(tokens, 'dp', split_axis=1, concat_axis=0, tiled=True)  7.75 us
  transfers between devices with their start and end apart: 12, of which 6 were waited for; matrix products, arithmetic and copies ran while one was open for 18% of the time, Pallas kernels for 0%

profile of v7, /device:TPU:97, one launch (start us, length us, event | category | flops | bytes accessed | tf_op | source)
XLA Modules:
  0.0 268.1 jit_solution(16642393631974717457)
XLA Ops:
  7.2 2.2 copy.46
  10.6 3.3 %copy.48 = bf16[256,4096]{0,1:T(8,128)(2,1)S(1)} copy(bf16[256,4096]{1,0:T(8,128)(2,1)} %param.11) | data formatting | bytes 4194304 | tf_op args[0]
  13.9 2.5 copy.49
  16.4 7.7 %all-to-all-start = ((bf16[256,16,256]{2,0,1:T(8,128)(2,1)}), bf16[256,16,256]{2,0,1:T(8,128)(2,1)}, u32[]{:S(2)}, u32[]{:S(2)}) async-start(bf16[256,16,256]{2,0,1:T(8,128)(2,1)} %copy.49), calls=%async_computation | async-start | bytes 4194304 | tf_op jit(solution)/shard_map/all_to_all | solution.py:70
  24.4 2.5 gather_fusion.1
  28.1 2.3 pad_maximum_fusion.1
  30.4 6.4 %copy.51 = bf16[256,16,2,256]{0,3,2,1:T(8,128)(2,1)} copy(bf16[256,16,2,256]{3,0,1,2:T(8,128)(2,1)} %pad_maximum_fusion.1) | data formatting | bytes 8388608 | tf_op jit(solution)/shard_map/concatenate | solution.py:75
  37.3 30.9 %all-to-all-done = bf16[256,16,256]{2,0,1:T(8,128)(2,1)} async-done(((bf16[256,16,256]{2,0,1:T(8,128)(2,1)}), bf16[256,16,256]{2,0,1:T(8,128)(2,1)}, u32[]{:S(2)}, u32[]{:S(2)}) %all-to-all-start) | async-done | bytes 2097184 | tf_op jit(solution)/shard_map/all_to_all | solution.py:70
  68.2 2.3 gather_fusion.2
  70.5 2.1 bitcast_select_fusion.3
  72.7 2.4 pad_maximum_fusion
  75.0 36.4 %all-gather.3.cloned.1.call-done = bf16[8192,768]{1,0:T(8,128)(2,1)} async-done(((bf16[512,768]{1,0:T(8,128)(2,1)}), bf16[8192,768]{1,0:T(8,128)(2,1)}) %all-gather.3.cloned.1.call-update) | async-done | bytes 12582928 | tf_op jit(solution)/shard_map/all_gather | solution.py:67
  111.5 7.0 %fusion.15 = bf16[256,512]{1,0:T(8,128)(2,1)S(1)} fusion(bf16[256,8192]{0,1:T(8,128)(2,1)} %bitcast.92, bf16[8192,768]{1,0:T(8,128)(2,1)} %all-gather.3.cloned.1.call-done), kind=kOutput, calls=%fused_computation.40 | convolution fusion | flops 2147614720 | bytes 12845056 | tf_op jit(solution)/shard_map/dot_general | solution.py:88
  118.6 1.4 collective-permute-start
  120.1 3.2 %collective-permute-start.1 = (bf16[256,2,2,128]{3,0,2,1:T(8,128)(2,1)S(1)}, bf16[256,2,2,128]{3,0,2,1:T(8,128)(2,1)S(1)}, u32[]{:S(2)}, u32[]{:S(2)}) collective-permute-start(bf16[256,2,2,128]{3,0,2,1:T(8,128)(2,1)S(1)} %copy.52), channel_id=1, source_target_pairs={{0,48},{16,64},{32,80},{48,96},{64,112},{80,128},{96,144},{112,160... | collective-permute-start | bytes 786440 | tf_op jit(solution)/shard_map/ppermute | solution.py:14
  123.3 4.8 %collective-permute-start.2 = (bf16[256,2,2,128]{3,0,2,1:T(8,128)(2,1)S(1)}, bf16[256,2,2,128]{3,0,2,1:T(8,128)(2,1)S(1)}, u32[]{:S(2)}, u32[]{:S(2)}) collective-permute-start(bf16[256,2,2,128]{3,0,2,1:T(8,128)(2,1)S(1)} %copy.52), channel_id=1, source_target_pairs={{0,32},{16,48},{32,64},{48,80},{64,96},{80,112},{96,128},{112,144}... | collective-permute-start | bytes 786440 | tf_op jit(solution)/shard_map/ppermute | solution.py:14
  128.1 4.7 %collective-permute-start.3 = (bf16[256,2,2,128]{3,0,2,1:T(8,128)(2,1)S(1)}, bf16[256,2,2,128]{3,0,2,1:T(8,128)(2,1)S(1)}, u32[]{:S(2)}, u32[]{:S(2)}) collective-permute-start(bf16[256,2,2,128]{3,0,2,1:T(8,128)(2,1)S(1)} %copy.52), channel_id=1, source_target_pairs={{0,16},{16,32},{32,48},{48,64},{64,80},{80,96},{96,112},{112,128},... | collective-permute-start | bytes 786440 | tf_op jit(solution)/shard_map/ppermute | solution.py:14
  132.8 5.2 %fusion.19 = bf16[256,256]{0,1:T(8,128)(2,1)S(1)} fusion(bf16[256,8192]{0,1:T(8,128)(2,1)} %bitcast.93, bf16[8192,768]{1,0:T(8,128)(2,1)} %all-gather.3.cloned.1.call-done), kind=kOutput, calls=%fused_computation.43 | convolution fusion | flops 1073807360 | bytes 8519680 | tf_op jit(solution)/shard_map/dot_general | solution.py:96
  139.3 2.6 fusion.33
  141.9 2.2 multiply_reduce_fusion
  149.7 2.1 collective-permute-start.4
  152.4 2.7 %collective-permute-done.7 = bf16[256,2,2,128]{0,3,2,1:T(8,128)(2,1)S(1)} collective-permute-done((bf16[256,2,2,128]{0,3,2,1:T(8,128)(2,1)S(1)}, bf16[256,2,2,128]{0,3,2,1:T(8,128)(2,1)S(1)}, u32[]{:S(2)}, u32[]{:S(2)}) %collective-permute-start.7) | collective-permute-done | bytes 262176 | tf_op jit(solution)/shard_map/ppermute | solution.py:14
  155.1 10.9 %collective-permute-done.6 = bf16[256,2,2,128]{0,3,2,1:T(8,128)(2,1)S(1)} collective-permute-done((bf16[256,2,2,128]{0,3,2,1:T(8,128)(2,1)S(1)}, bf16[256,2,2,128]{0,3,2,1:T(8,128)(2,1)S(1)}, u32[]{:S(2)}, u32[]{:S(2)}) %collective-permute-start.6) | collective-permute-done | bytes 262176 | tf_op jit(solution)/shard_map/ppermute | solution.py:14
  167.1 4.8 %fusion.3 = bf16[256,16,256]{2,0,1:T(8,128)(2,1)S(1)} fusion(bf16[256,768,1]{0,1,2:T(8,128)(2,1)} %bitcast.98, bf16[16,2,256,768]{3,2,1,0:T(8,128)(2,1)} %bitcast.108), kind=kOutput, calls=%fused_computation.8 | convolution fusion | flops 1610612736 | bytes 8781824 | tf_op jit(solution)/shard_map/dot_general | solution.py:153
  171.9 5.0 %fusion.13 = bf16[16,256,256]{2,1,0:T(8,128)(2,1)S(1)} fusion(bf16[256,16,256]{2,0,1:T(8,128)(2,1)S(1)} %fusion.3, pred[256]{0:T(512)(128)(4,1)S(1)} %dynamic_slice.9, bf16[256,768,1]{0,1,2:T(8,128)(2,1)S(1)} %bitcast.99, bf16[16,2,256,768]{3,2,1,0:T(8,128)(2,1)} %bitcast.109), kind=kOutput, calls=%fused_computation.31 | convolution fusion | flops 1611661312 | bytes 10879232 | tf_op jit(solution)/shard_map/dot_general | solution.py:150
  176.9 2.0 gather_fusion.3
  178.9 6.9 %all-to-all-start.1 = ((bf16[16,256,256]{2,1,0:T(8,128)(2,1)}), bf16[16,256,256]{2,1,0:T(8,128)(2,1)S(1)}, u32[]{:S(2)}, u32[]{:S(2)}) async-start(bf16[16,256,256]{2,1,0:T(8,128)(2,1)} %gather_fusion.3), calls=%async_computation.1 | async-start | bytes 4194304 | tf_op jit(solution)/shard_map/all_to_all | solution.py:160
  185.8 2.4 convolution_convert_fusion.1
  189.1 42.3 %all-to-all-done.1 = bf16[16,256,256]{2,1,0:T(8,128)(2,1)S(1)} async-done(((bf16[16,256,256]{2,1,0:T(8,128)(2,1)}), bf16[16,256,256]{2,1,0:T(8,128)(2,1)S(1)}, u32[]{:S(2)}, u32[]{:S(2)}) %all-to-all-start.1) | async-done | bytes 2097184 | tf_op jit(solution)/shard_map/all_to_all | solution.py:160
  232.4 19.4 %all-gather.5.cloned.1.call-done = bf16[4096,768]{0,1:T(8,128)(2,1)} async-done(((bf16[256,768]{0,1:T(8,128)(2,1)}), bf16[4096,768]{0,1:T(8,128)(2,1)}) %all-gather.5.cloned.1.call-update) | async-done | bytes 6291472 | tf_op jit(solution)/shard_map/all_gather | solution.py:163
  251.7 7.5 %convolution_convert_fusion = bf16[512,768]{1,0:T(8,128)(2,1)S(1)} fusion(bf16[4096,512]{1,0:T(8,128)(2,1)} %pad_maximum_fusion, bf16[4096,768]{0,1:T(8,128)(2,1)} %all-gather.5.cloned.1.call-done), kind=kOutput, calls=%fused_computation.36 | convolution fusion | flops 3221618688 | bytes 11272192 | tf_op jit(solution)/shard_map/dot_general | solution.py:164
  259.5 1.8 copy.69
  (67 shorter events, 13.6 us)
Async XLA Ops:
  7.2 104.3 %all-gather.3.cloned.1.call-start = ((), (), s32[]{:S(2)}) async-start(), calls=%async_computation.2 | async-start | bytes 13369344 | tf_op jit(solution)/shard_map/all_gather | solution.py:67
  16.4 7.8 %copy-start.9 = (s32[32]{0:T(128)S(1)}, s32[32]{0:T(128)}, u32[]{:S(2)}) copy-start(s32[32]{0:T(128)} %param.13) | copy-start | bytes 388
  16.4 8.0 %copy-start.8 = (s32[16]{0:T(128)S(1)}, s32[16]{0:T(128)}, u32[]{:S(2)}) copy-start(s32[16]{0:T(128)} %constant.76.clone) | copy-start | bytes 196
  16.4 51.9 %all-to-all-start = ((bf16[256,16,256]{2,0,1:T(8,128)(2,1)}), bf16[256,16,256]{2,0,1:T(8,128)(2,1)}, u32[]{:S(2)}, u32[]{:S(2)}) async-start(bf16[256,16,256]{2,0,1:T(8,128)(2,1)} %copy.49), calls=%async_computation | async-start | bytes 4194304 | tf_op jit(solution)/shard_map/all_to_all | solution.py:70
  24.1 227.6 %all-gather.5.cloned.1.call-start = ((), (), s32[]{:S(2)}) async-start(), calls=%async_computation.3 | async-start | bytes 6684672 | tf_op jit(solution)/shard_map/all_gather | solution.py:163
  30.3 6.4 %copy-start.6 = (s32[4096]{0:T(1024)S(1)}, s32[4096]{0:T(1024)}, u32[]{:S(2)}) copy-start(s32[4096]{0:T(1024)} %param.14) | copy-start | bytes 49156
  30.4 6.5 %copy-start.5 = (bf16[256,256]{1,0:T(8,128)(2,1)S(1)}, bf16[256,256]{1,0:T(8,128)(2,1)}, u32[]{:S(2)}) copy-start(bf16[256,256]{1,0:T(8,128)(2,1)} %param.15) | copy-start | bytes 393220
  118.6 19.4 %collective-permute-start = (bf16[256,2,2,128]{3,0,2,1:T(8,128)(2,1)S(1)}, bf16[256,2,2,128]{3,0,2,1:T(8,128)(2,1)S(1)}, u32[]{:S(2)}, u32[]{:S(2)}) collective-permute-start(bf16[256,2,2,128]{3,0,2,1:T(8,128)(2,1)S(1)} %copy.52), channel_id=1, source_target_pairs={{0,64},{16,80},{32,96},{48,112},{64,128},{80,144},{96,160},{112,17... | collective-permute-start | bytes 786440 | tf_op jit(solution)/shard_map/ppermute | solution.py:14
  120.1 18.0 %collective-permute-start.1 = (bf16[256,2,2,128]{3,0,2,1:T(8,128)(2,1)S(1)}, bf16[256,2,2,128]{3,0,2,1:T(8,128)(2,1)S(1)}, u32[]{:S(2)}, u32[]{:S(2)}) collective-permute-start(bf16[256,2,2,128]{3,0,2,1:T(8,128)(2,1)S(1)} %copy.52), channel_id=1, source_target_pairs={{0,48},{16,64},{32,80},{48,96},{64,112},{80,128},{96,144},{112,160... | collective-permute-start | bytes 786440 | tf_op jit(solution)/shard_map/ppermute | solution.py:14
  123.3 14.8 %collective-permute-start.2 = (bf16[256,2,2,128]{3,0,2,1:T(8,128)(2,1)S(1)}, bf16[256,2,2,128]{3,0,2,1:T(8,128)(2,1)S(1)}, u32[]{:S(2)}, u32[]{:S(2)}) collective-permute-start(bf16[256,2,2,128]{3,0,2,1:T(8,128)(2,1)S(1)} %copy.52), channel_id=1, source_target_pairs={{0,32},{16,48},{32,64},{48,80},{64,96},{80,112},{96,128},{112,144}... | collective-permute-start | bytes 786440 | tf_op jit(solution)/shard_map/ppermute | solution.py:14
  128.1 10.1 %collective-permute-start.3 = (bf16[256,2,2,128]{3,0,2,1:T(8,128)(2,1)S(1)}, bf16[256,2,2,128]{3,0,2,1:T(8,128)(2,1)S(1)}, u32[]{:S(2)}, u32[]{:S(2)}) collective-permute-start(bf16[256,2,2,128]{3,0,2,1:T(8,128)(2,1)S(1)} %copy.52), channel_id=1, source_target_pairs={{0,16},{16,32},{32,48},{48,64},{64,80},{80,96},{96,112},{112,128},... | collective-permute-start | bytes 786440 | tf_op jit(solution)/shard_map/ppermute | solution.py:14
  138.3 1.0 copy-start.2
  141.9 2.6 copy-start
  145.3 6.5 %copy-start.3 = (bf16[1280,2,2,128]{3,0,2,1:T(8,128)(2,1)S(1)}, bf16[1280,2,2,128]{3,0,2,1:T(8,128)(2,1)}, u32[]{:S(2)}) copy-start(bf16[1280,2,2,128]{3,0,2,1:T(8,128)(2,1)} %copy-done.2) | copy-start | bytes 3932164
  145.6 9.5 %collective-permute-start.7 = (bf16[256,2,2,128]{0,3,2,1:T(8,128)(2,1)S(1)}, bf16[256,2,2,128]{0,3,2,1:T(8,128)(2,1)S(1)}, u32[]{:S(2)}, u32[]{:S(2)}) collective-permute-start(bf16[256,2,2,128]{0,3,2,1:T(8,128)(2,1)S(1)} %get-tuple-element.24), channel_id=1, source_target_pairs={{64,0},{80,16},{96,32},{112,48},{128,64},{144,80},{160,96},{176,11... | collective-permute-start | bytes 786440 | tf_op jit(solution)/shard_map/ppermute | solution.py:14
  147.1 19.0 %collective-permute-start.6 = (bf16[256,2,2,128]{0,3,2,1:T(8,128)(2,1)S(1)}, bf16[256,2,2,128]{0,3,2,1:T(8,128)(2,1)S(1)}, u32[]{:S(2)}, u32[]{:S(2)}) collective-permute-start(bf16[256,2,2,128]{0,3,2,1:T(8,128)(2,1)S(1)} %get-tuple-element.25), channel_id=1, source_target_pairs={{48,0},{64,16},{80,32},{96,48},{112,64},{128,80},{144,96},{160,112... | collective-permute-start | bytes 786440 | tf_op jit(solution)/shard_map/ppermute | solution.py:14
  148.4 17.7 %collective-permute-start.5 = (bf16[256,2,2,128]{0,3,2,1:T(8,128)(2,1)S(1)}, bf16[256,2,2,128]{0,3,2,1:T(8,128)(2,1)S(1)}, u32[]{:S(2)}, u32[]{:S(2)}) collective-permute-start(bf16[256,2,2,128]{0,3,2,1:T(8,128)(2,1)S(1)} %get-tuple-element.26), channel_id=1, source_target_pairs={{32,0},{48,16},{64,32},{80,48},{96,64},{112,80},{128,96},{144,112}... | collective-permute-start | bytes 786440 | tf_op jit(solution)/shard_map/ppermute | solution.py:14
  149.7 16.4 %collective-permute-start.4 = (bf16[256,2,2,128]{0,3,2,1:T(8,128)(2,1)S(1)}, bf16[256,2,2,128]{0,3,2,1:T(8,128)(2,1)S(1)}, u32[]{:S(2)}, u32[]{:S(2)}) collective-permute-start(bf16[256,2,2,128]{0,3,2,1:T(8,128)(2,1)S(1)} %get-tuple-element.23), channel_id=1, source_target_pairs={{16,0},{32,16},{48,32},{64,48},{80,64},{96,80},{112,96},{128,112},... | collective-permute-start | bytes 786440 | tf_op jit(solution)/shard_map/ppermute | solution.py:14
  152.4 14.7 %copy-start.7 = (s32[16]{0:T(128)S(1)}, s32[16]{0:T(128)}, u32[]{:S(2)}) copy-start(s32[16]{0:T(128)} %constant.109) | copy-start | bytes 196
  167.1 4.8 %copy-start.1 = (bf16[256,3,2,128]{0,3,2,1:T(8,128)(2,1)S(1)}, bf16[256,3,2,128]{0,3,2,1:T(8,128)(2,1)}, u32[]{:S(2)}) copy-start(bf16[256,3,2,128]{0,3,2,1:T(8,128)(2,1)} %maximum_convert_fusion) | copy-start | bytes 1179652
  178.9 6.9 %copy-start.4 = (bf16[1280,2,2,128]{3,0,2,1:T(8,128)(2,1)S(1)}, bf16[1280,2,2,128]{3,0,2,1:T(8,128)(2,1)}, u32[]{:S(2)}) copy-start(bf16[1280,2,2,128]{3,0,2,1:T(8,128)(2,1)} %copy-done.2) | copy-start | bytes 3932164
  178.9 52.5 %all-to-all-start.1 = ((bf16[16,256,256]{2,1,0:T(8,128)(2,1)}), bf16[16,256,256]{2,1,0:T(8,128)(2,1)S(1)}, u32[]{:S(2)}, u32[]{:S(2)}) async-start(bf16[16,256,256]{2,1,0:T(8,128)(2,1)} %gather_fusion.3), calls=%async_computation.1 | async-start | bytes 4194304 | tf_op jit(solution)/shard_map/all_to_all | solution.py:160
Sparse Core Ops, SparseCore 0:
  10.8 100.6 all-gather.2
  167.2 84.4 all-gather.4

commit v8 on v5

--- a/solution.py
+++ b/solution.py
@@ -163,11 +163,11 @@
     group_parts = lax.all_to_all(parts, "mp", split_axis=0, concat_axis=0, tiled=True)
     grad_tokens = jnp.sum(group_parts.astype(jnp.float32), axis=0).astype(jnp.bfloat16)
 
-    gathered = lax.all_gather(dqkv, "dp", axis=0, tiled=True, axis_index_groups=[ring])
+    gathered = lax.all_gather(dqkv[None], "dp", axis=0, tiled=True, axis_index_groups=[ring])
     weight_sum = lax.dot_general(
-        ring_columns,
+        ring_columns.reshape(dp_devices, local_rows, -1),
         gathered,
-        (((0,), (0,)), ((), ())),
+        (((0, 1), (0, 1)), ((), ())),
         preferred_element_type=jnp.float32,
     )
     grad_weights = (

time: 271 us -> 263 us (0.970)
  waiting for transfers between devices: 143 us -> 137 us
    all_gather x1, waiting for transfers between devices: 19.3 us -> 13.8 us  [on_device(): lax.all_gather(dqkv[None], 'dp', axis=0, tiled=True, axis_index_groups=[r...]
where the time goes in v8:
time: 263 us; the launch traced here: 262 us
  waiting for transfers between devices  137 us (52%)
  matrix products  37.7 us (14%)
  starting transfers between devices  35 us (13%)
  local copies, waits for them, and re-layouts  28.7 us (11%)
  between operations  14.5 us (6%)
  other arithmetic  9.41 us (4%)
    all_to_all x1, waiting for transfers between devices, on_device(): lax.all_to_all(parts, 'mp', split_axis=0, concat_axis=0, tiled=True)  42.2 us
    all_gather x1, waiting for transfers between devices, on_device(): lax.all_gather(flat_weights, 'dp', axis=0, tiled=True, axis_index_groups=...  36.4 us
    all_to_all x1, waiting for transfers between devices, on_device(): lax.all_to_all(tokens, 'dp', split_axis=1, concat_axis=0, tiled=True)  30.9 us
    ppermute x8, starting transfers between devices, shifted(): return lax.ppermute(block, axis, route)  20.3 us
    all_gather x1, waiting for transfers between devices, on_device(): lax.all_gather(dqkv[None], 'dp', axis=0, tiled=True, axis_index_groups=[r...  13.8 us
    ppermute x8, waiting for transfers between devices, shifted(): return lax.ppermute(block, axis, route)  13.7 us
    unnamed x27, local copies, waits for them, and re-layouts  9.27 us
    all_to_all x1, starting transfers between devices, on_device(): lax.all_to_all(tokens, 'dp', split_axis=1, concat_axis=0, tiled=True)  7.75 us
  transfers between devices with their start and end apart: 12, of which 6 were waited for; matrix products, arithmetic and copies ran while one was open for 18% of the time, Pallas kernels for 0%

profile of v8, /device:TPU:97, one launch (start us, length us, event | category | flops | bytes accessed | tf_op | source)
XLA Modules:
  0.0 262.4 jit_solution(9539630087630359603)
XLA Ops:
  7.2 2.2 copy.75
  10.6 3.3 %copy.77 = bf16[256,4096]{0,1:T(8,128)(2,1)S(1)} copy(bf16[256,4096]{1,0:T(8,128)(2,1)} %param.11) | data formatting | bytes 4194304 | tf_op args[0]
  13.9 2.5 copy.78
  16.4 7.7 %all-to-all-start = ((bf16[256,16,256]{2,0,1:T(8,128)(2,1)}), bf16[256,16,256]{2,0,1:T(8,128)(2,1)}, u32[]{:S(2)}, u32[]{:S(2)}) async-start(bf16[256,16,256]{2,0,1:T(8,128)(2,1)} %copy.78), calls=%async_computation | async-start | bytes 4194304 | tf_op jit(solution)/shard_map/all_to_all | solution.py:70
  24.4 2.5 gather_fusion.1
  28.1 2.3 pad_maximum_fusion.1
  30.4 6.4 %copy.80 = bf16[256,16,2,256]{0,3,2,1:T(8,128)(2,1)} copy(bf16[256,16,2,256]{3,0,1,2:T(8,128)(2,1)} %pad_maximum_fusion.1) | data formatting | bytes 8388608 | tf_op jit(solution)/shard_map/concatenate | solution.py:75
  37.3 30.9 %all-to-all-done = bf16[256,16,256]{2,0,1:T(8,128)(2,1)} async-done(((bf16[256,16,256]{2,0,1:T(8,128)(2,1)}), bf16[256,16,256]{2,0,1:T(8,128)(2,1)}, u32[]{:S(2)}, u32[]{:S(2)}) %all-to-all-start) | async-done | bytes 2097184 | tf_op jit(solution)/shard_map/all_to_all | solution.py:70
  68.2 2.3 gather_fusion.2
  70.5 2.1 bitcast_select_fusion.3
  72.7 2.4 pad_maximum_fusion
  75.0 36.4 %all-gather.3.cloned.1.call-done = bf16[8192,768]{1,0:T(8,128)(2,1)} async-done(((bf16[512,768]{1,0:T(8,128)(2,1)}), bf16[8192,768]{1,0:T(8,128)(2,1)}) %all-gather.3.cloned.1.call-update) | async-done | bytes 12582928 | tf_op jit(solution)/shard_map/all_gather | solution.py:67
  111.5 7.0 %fusion.15 = bf16[256,512]{1,0:T(8,128)(2,1)S(1)} fusion(bf16[256,8192]{0,1:T(8,128)(2,1)} %bitcast.99, bf16[8192,768]{1,0:T(8,128)(2,1)} %all-gather.3.cloned.1.call-done), kind=kOutput, calls=%fused_computation.40 | convolution fusion | flops 2147614720 | bytes 12845056 | tf_op jit(solution)/shard_map/dot_general | solution.py:88
  118.6 1.4 collective-permute-start
  120.1 3.2 %collective-permute-start.1 = (bf16[256,2,2,128]{3,0,2,1:T(8,128)(2,1)S(1)}, bf16[256,2,2,128]{3,0,2,1:T(8,128)(2,1)S(1)}, u32[]{:S(2)}, u32[]{:S(2)}) collective-permute-start(bf16[256,2,2,128]{3,0,2,1:T(8,128)(2,1)S(1)} %copy.81), channel_id=1, source_target_pairs={{0,48},{16,64},{32,80},{48,96},{64,112},{80,128},{96,144},{112,160... | collective-permute-start | bytes 786440 | tf_op jit(solution)/shard_map/ppermute | solution.py:14
  123.3 4.8 %collective-permute-start.2 = (bf16[256,2,2,128]{3,0,2,1:T(8,128)(2,1)S(1)}, bf16[256,2,2,128]{3,0,2,1:T(8,128)(2,1)S(1)}, u32[]{:S(2)}, u32[]{:S(2)}) collective-permute-start(bf16[256,2,2,128]{3,0,2,1:T(8,128)(2,1)S(1)} %copy.81), channel_id=1, source_target_pairs={{0,32},{16,48},{32,64},{48,80},{64,96},{80,112},{96,128},{112,144}... | collective-permute-start | bytes 786440 | tf_op jit(solution)/shard_map/ppermute | solution.py:14
  128.1 4.7 %collective-permute-start.3 = (bf16[256,2,2,128]{3,0,2,1:T(8,128)(2,1)S(1)}, bf16[256,2,2,128]{3,0,2,1:T(8,128)(2,1)S(1)}, u32[]{:S(2)}, u32[]{:S(2)}) collective-permute-start(bf16[256,2,2,128]{3,0,2,1:T(8,128)(2,1)S(1)} %copy.81), channel_id=1, source_target_pairs={{0,16},{16,32},{32,48},{48,64},{64,80},{80,96},{96,112},{112,128},... | collective-permute-start | bytes 786440 | tf_op jit(solution)/shard_map/ppermute | solution.py:14
  132.8 5.2 %fusion.19 = bf16[256,256]{0,1:T(8,128)(2,1)S(1)} fusion(bf16[256,8192]{0,1:T(8,128)(2,1)} %bitcast.100, bf16[8192,768]{1,0:T(8,128)(2,1)} %all-gather.3.cloned.1.call-done), kind=kOutput, calls=%fused_computation.43 | convolution fusion | flops 1073807360 | bytes 8519680 | tf_op jit(solution)/shard_map/dot_general | solution.py:96
  139.3 2.6 fusion.33
  141.9 2.2 multiply_reduce_fusion
  149.7 2.1 collective-permute-start.4
  152.4 2.7 %collective-permute-done.7 = bf16[256,2,2,128]{0,3,2,1:T(8,128)(2,1)S(1)} collective-permute-done((bf16[256,2,2,128]{0,3,2,1:T(8,128)(2,1)S(1)}, bf16[256,2,2,128]{0,3,2,1:T(8,128)(2,1)S(1)}, u32[]{:S(2)}, u32[]{:S(2)}) %collective-permute-start.7) | collective-permute-done | bytes 262176 | tf_op jit(solution)/shard_map/ppermute | solution.py:14
  155.1 10.9 %collective-permute-done.6 = bf16[256,2,2,128]{0,3,2,1:T(8,128)(2,1)S(1)} collective-permute-done((bf16[256,2,2,128]{0,3,2,1:T(8,128)(2,1)S(1)}, bf16[256,2,2,128]{0,3,2,1:T(8,128)(2,1)S(1)}, u32[]{:S(2)}, u32[]{:S(2)}) %collective-permute-start.6) | collective-permute-done | bytes 262176 | tf_op jit(solution)/shard_map/ppermute | solution.py:14
  167.3 4.6 %fusion.3 = f32[256,16,256]{2,0,1:T(8,128)S(1)} fusion(bf16[256,768,1]{0,1,2:T(8,128)(2,1)S(1)} %bitcast.109, bf16[16,2,256,768]{3,2,1,0:T(8,128)(2,1)} %bitcast.102), kind=kOutput, calls=%fused_computation.8 | convolution fusion | flops 1610612736 | bytes 10878976 | tf_op jit(solution)/shard_map/dot_general | solution.py:154
  172.0 4.6 %fusion.13 = bf16[16,256,256]{2,1,0:T(8,128)(2,1)S(1)} fusion(f32[256,16,256]{2,0,1:T(8,128)S(1)} %fusion.3, bf16[256,768,1]{0,1,2:T(8,128)(2,1)S(1)} %bitcast.107, bf16[16,2,256,768]{3,2,1,0:T(8,128)(2,1)} %bitcast.103), kind=kOutput, calls=%fused_computation.31 | convolution fusion | flops 1612709888 | bytes 12976128 | tf_op jit(solution)/shard_map/dot_general | solution.py:149
  176.6 2.0 gather_fusion.3
  178.7 6.9 %all-to-all-start.1 = ((bf16[16,256,256]{2,1,0:T(8,128)(2,1)}), bf16[16,256,256]{2,1,0:T(8,128)(2,1)S(1)}, u32[]{:S(2)}, u32[]{:S(2)}) async-start(bf16[16,256,256]{2,1,0:T(8,128)(2,1)} %gather_fusion.3), calls=%async_computation.1 | async-start | bytes 4194304 | tf_op jit(solution)/shard_map/all_to_all | solution.py:163
  185.6 2.6 convolution_convert_fusion
  188.9 42.2 %all-to-all-done.1 = bf16[16,256,256]{2,1,0:T(8,128)(2,1)S(1)} async-done(((bf16[16,256,256]{2,1,0:T(8,128)(2,1)}), bf16[16,256,256]{2,1,0:T(8,128)(2,1)S(1)}, u32[]{:S(2)}, u32[]{:S(2)}) %all-to-all-start.1) | async-done | bytes 2097184 | tf_op jit(solution)/shard_map/all_to_all | solution.py:163
  232.1 13.8 %all-gather.5.cloned.1.call-done = bf16[16,256,768]{2,1,0:T(8,128)(2,1)} async-done(((bf16[1,256,768]{2,1,0:T(8,128)(2,1)}), bf16[16,256,768]{2,1,0:T(8,128)(2,1)}) %all-gather.5.cloned.1.call-update) | async-done | bytes 6291472 | tf_op jit(solution)/shard_map/all_gather | solution.py:166
  245.9 7.5 %bitcast_convert_fusion = bf16[512,768]{1,0:T(8,128)(2,1)S(1)} fusion(bf16[16,256,512]{2,1,0:T(8,128)(2,1)} %bitcast.98, bf16[16,256,768]{2,1,0:T(8,128)(2,1)} %all-gather.5.cloned.1.call-done), kind=kOutput, calls=%fused_computation.36 | convolution fusion | flops 3221618688 | bytes 11272192 | tf_op jit(solution)/shard_map/dot_general | solution.py:167
  253.7 1.8 copy.100
  (67 shorter events, 13.8 us)
Async XLA Ops:
  7.2 104.3 %all-gather.3.cloned.1.call-start = ((), (), s32[]{:S(2)}) async-start(), calls=%async_computation.2 | async-start | bytes 13369344 | tf_op jit(solution)/shard_map/all_gather | solution.py:67
  16.4 7.8 %copy-start.8 = (s32[32]{0:T(128)S(1)}, s32[32]{0:T(128)}, u32[]{:S(2)}) copy-start(s32[32]{0:T(128)} %param.13) | copy-start | bytes 388
  16.4 8.0 %copy-start.7 = (s32[16]{0:T(128)S(1)}, s32[16]{0:T(128)}, u32[]{:S(2)}) copy-start(s32[16]{0:T(128)} %constant.77.clone) | copy-start | bytes 196
  16.4 51.9 %all-to-all-start = ((bf16[256,16,256]{2,0,1:T(8,128)(2,1)}), bf16[256,16,256]{2,0,1:T(8,128)(2,1)}, u32[]{:S(2)}, u32[]{:S(2)}) async-start(bf16[256,16,256]{2,0,1:T(8,128)(2,1)} %copy.78), calls=%async_computation | async-start | bytes 4194304 | tf_op jit(solution)/shard_map/all_to_all | solution.py:70
  24.1 221.8 %all-gather.5.cloned.1.call-start = ((), (), s32[]{:S(2)}) async-start(), calls=%async_computation.3 | async-start | bytes 6684672 | tf_op jit(solution)/shard_map/all_gather | solution.py:166
  30.3 6.4 %copy-start.5 = (s32[4096]{0:T(1024)S(1)}, s32[4096]{0:T(1024)}, u32[]{:S(2)}) copy-start(s32[4096]{0:T(1024)} %param.14) | copy-start | bytes 49156
  30.4 6.5 %copy-start.4 = (bf16[256,256]{1,0:T(8,128)(2,1)S(1)}, bf16[256,256]{1,0:T(8,128)(2,1)}, u32[]{:S(2)}) copy-start(bf16[256,256]{1,0:T(8,128)(2,1)} %param.15) | copy-start | bytes 393220
  118.6 19.4 %collective-permute-start = (bf16[256,2,2,128]{3,0,2,1:T(8,128)(2,1)S(1)}, bf16[256,2,2,128]{3,0,2,1:T(8,128)(2,1)S(1)}, u32[]{:S(2)}, u32[]{:S(2)}) collective-permute-start(bf16[256,2,2,128]{3,0,2,1:T(8,128)(2,1)S(1)} %copy.81), channel_id=1, source_target_pairs={{0,64},{16,80},{32,96},{48,112},{64,128},{80,144},{96,160},{112,17... | collective-permute-start | bytes 786440 | tf_op jit(solution)/shard_map/ppermute | solution.py:14
  120.1 18.0 %collective-permute-start.1 = (bf16[256,2,2,128]{3,0,2,1:T(8,128)(2,1)S(1)}, bf16[256,2,2,128]{3,0,2,1:T(8,128)(2,1)S(1)}, u32[]{:S(2)}, u32[]{:S(2)}) collective-permute-start(bf16[256,2,2,128]{3,0,2,1:T(8,128)(2,1)S(1)} %copy.81), channel_id=1, source_target_pairs={{0,48},{16,64},{32,80},{48,96},{64,112},{80,128},{96,144},{112,160... | collective-permute-start | bytes 786440 | tf_op jit(solution)/shard_map/ppermute | solution.py:14
  123.3 14.8 %collective-permute-start.2 = (bf16[256,2,2,128]{3,0,2,1:T(8,128)(2,1)S(1)}, bf16[256,2,2,128]{3,0,2,1:T(8,128)(2,1)S(1)}, u32[]{:S(2)}, u32[]{:S(2)}) collective-permute-start(bf16[256,2,2,128]{3,0,2,1:T(8,128)(2,1)S(1)} %copy.81), channel_id=1, source_target_pairs={{0,32},{16,48},{32,64},{48,80},{64,96},{80,112},{96,128},{112,144}... | collective-permute-start | bytes 786440 | tf_op jit(solution)/shard_map/ppermute | solution.py:14
  128.1 10.1 %collective-permute-start.3 = (bf16[256,2,2,128]{3,0,2,1:T(8,128)(2,1)S(1)}, bf16[256,2,2,128]{3,0,2,1:T(8,128)(2,1)S(1)}, u32[]{:S(2)}, u32[]{:S(2)}) collective-permute-start(bf16[256,2,2,128]{3,0,2,1:T(8,128)(2,1)S(1)} %copy.81), channel_id=1, source_target_pairs={{0,16},{16,32},{32,48},{48,64},{64,80},{80,96},{96,112},{112,128},... | collective-permute-start | bytes 786440 | tf_op jit(solution)/shard_map/ppermute | solution.py:14
  138.3 1.0 copy-start.1
  141.9 2.6 %copy-start = (f32[2,256,1280]{2,1,0:T(8,128)}, f32[2,256,1280]{2,1,0:T(8,128)S(1)}, u32[]{:S(2)}) copy-start(f32[2,256,1280]{2,1,0:T(8,128)S(1)} %get-tuple-element.33) | copy-start | bytes 7864324
  145.3 6.5 %copy-start.2 = (bf16[1280,2,2,128]{3,0,2,1:T(8,128)(2,1)S(1)}, bf16[1280,2,2,128]{3,0,2,1:T(8,128)(2,1)}, u32[]{:S(2)}) copy-start(bf16[1280,2,2,128]{3,0,2,1:T(8,128)(2,1)} %copy-done.1) | copy-start | bytes 3932164
  145.6 9.5 %collective-permute-start.7 = (bf16[256,2,2,128]{0,3,2,1:T(8,128)(2,1)S(1)}, bf16[256,2,2,128]{0,3,2,1:T(8,128)(2,1)S(1)}, u32[]{:S(2)}, u32[]{:S(2)}) collective-permute-start(bf16[256,2,2,128]{0,3,2,1:T(8,128)(2,1)S(1)} %get-tuple-element.29), channel_id=1, source_target_pairs={{64,0},{80,16},{96,32},{112,48},{128,64},{144,80},{160,96},{176,11... | collective-permute-start | bytes 786440 | tf_op jit(solution)/shard_map/ppermute | solution.py:14
  147.1 19.0 %collective-permute-start.6 = (bf16[256,2,2,128]{0,3,2,1:T(8,128)(2,1)S(1)}, bf16[256,2,2,128]{0,3,2,1:T(8,128)(2,1)S(1)}, u32[]{:S(2)}, u32[]{:S(2)}) collective-permute-start(bf16[256,2,2,128]{0,3,2,1:T(8,128)(2,1)S(1)} %get-tuple-element.30), channel_id=1, source_target_pairs={{48,0},{64,16},{80,32},{96,48},{112,64},{128,80},{144,96},{160,112... | collective-permute-start | bytes 786440 | tf_op jit(solution)/shard_map/ppermute | solution.py:14
  148.4 17.7 %collective-permute-start.5 = (bf16[256,2,2,128]{0,3,2,1:T(8,128)(2,1)S(1)}, bf16[256,2,2,128]{0,3,2,1:T(8,128)(2,1)S(1)}, u32[]{:S(2)}, u32[]{:S(2)}) collective-permute-start(bf16[256,2,2,128]{0,3,2,1:T(8,128)(2,1)S(1)} %get-tuple-element.31), channel_id=1, source_target_pairs={{32,0},{48,16},{64,32},{80,48},{96,64},{112,80},{128,96},{144,112}... | collective-permute-start | bytes 786440 | tf_op jit(solution)/shard_map/ppermute | solution.py:14
  149.7 16.4 %collective-permute-start.4 = (bf16[256,2,2,128]{0,3,2,1:T(8,128)(2,1)S(1)}, bf16[256,2,2,128]{0,3,2,1:T(8,128)(2,1)S(1)}, u32[]{:S(2)}, u32[]{:S(2)}) collective-permute-start(bf16[256,2,2,128]{0,3,2,1:T(8,128)(2,1)S(1)} %get-tuple-element.28), channel_id=1, source_target_pairs={{16,0},{32,16},{48,32},{64,48},{80,64},{96,80},{112,96},{128,112},... | collective-permute-start | bytes 786440 | tf_op jit(solution)/shard_map/ppermute | solution.py:14
  166.3 1.0 copy-start.6
  178.7 6.9 %copy-start.3 = (bf16[1280,2,2,128]{3,0,2,1:T(8,128)(2,1)S(1)}, bf16[1280,2,2,128]{3,0,2,1:T(8,128)(2,1)}, u32[]{:S(2)}) copy-start(bf16[1280,2,2,128]{3,0,2,1:T(8,128)(2,1)} %copy-done.1) | copy-start | bytes 3932164
  178.7 52.5 %all-to-all-start.1 = ((bf16[16,256,256]{2,1,0:T(8,128)(2,1)}), bf16[16,256,256]{2,1,0:T(8,128)(2,1)S(1)}, u32[]{:S(2)}, u32[]{:S(2)}) async-start(bf16[16,256,256]{2,1,0:T(8,128)(2,1)} %gather_fusion.3), calls=%async_computation.1 | async-start | bytes 4194304 | tf_op jit(solution)/shard_map/all_to_all | solution.py:163
Sparse Core Ops, SparseCore 0:
  10.8 100.6 all-gather.2
  167.4 78.4 all-gather.4

commit v9 on v8

--- a/solution.py
+++ b/solution.py
@@ -126,16 +126,20 @@
         jnp.einsum("hqk,khd->qhd", dscore, key_rows, preferred_element_type=jnp.float32)
         * scale_factor
     )
+    blocks = (head_count, local_rows, SPAN + 1, local_rows)
     grad_k = (
-        jnp.einsum("hqk,qhd->khd", dscore, queries, preferred_element_type=jnp.float32)
+        jnp.einsum(
+            "hqbk,qhd->bkhd", dscore.reshape(blocks), queries, preferred_element_type=jnp.float32
+        )
         * scale_factor
     )
-    grad_v = jnp.einsum("hqk,qhd->khd", probs, upstream, preferred_element_type=jnp.float32)
-    window_grads = jnp.stack([grad_k, grad_v], 1)
-    own_grads = window_grads[front_pad:]
+    grad_v = jnp.einsum(
+        "hqbk,qhd->bkhd", probs.reshape(blocks), upstream, preferred_element_type=jnp.float32
+    )
+    window_grads = jnp.stack([grad_k, grad_v], 2)
+    own_grads = window_grads[SPAN]
     for distance in range(1, SPAN + 1):
-        lower_edge = front_pad - distance * local_rows
-        sent_block = window_grads[lower_edge : lower_edge + local_rows]
+        sent_block = window_grads[SPAN - distance]
         own_grads = own_grads + shifted(sent_block.astype(jnp.bfloat16), "dp", -distance).astype(
             sent_block.dtype
         )

time: 263 us -> 272 us (1.034)
  waiting for transfers between devices: 137 us -> 140 us
  local copies, waits for them, and re-layouts: 28.7 us -> 31.5 us
    convert_element_type x0 -> x3, local copies, waits for them, and re-layouts: none -> 2.96 us  [the longest x1 1.44 us: on_device(): dscore = (probs_f * (dprob - row_delta)).astype(jnp.bfloat16)]
    all_to_all x1, waiting for transfers between devices: 42.2 us -> 45.1 us  [on_device(): lax.all_to_all(parts, 'mp', split_axis=0, concat_axis=0, tiled=True)]
    unnamed x27 -> x29, local copies, waits for them, and re-layouts: 9.27 us -> 9.29 us
  transfers between devices with their start and end apart: 12 -> 12, of which waited for: 6 -> 8; matrix products, arithmetic and copies ran while one was open for 18% -> 17% of each run, Pallas kernels for 0% -> 0%
where the time goes in v9:
time: 272 us; the launch traced here: 271 us
  waiting for transfers between devices  140 us (51%)
  matrix products  38.5 us (14%)
  starting transfers between devices  34.9 us (13%)
  local copies, waits for them, and re-layouts  31.5 us (12%)
  between operations  14.5 us (5%)
  other arithmetic  11.9 us (4%)
    all_to_all x1, waiting for transfers between devices, on_device(): lax.all_to_all(parts, 'mp', split_axis=0, concat_axis=0, tiled=True)  45.1 us
    all_gather x1, waiting for transfers between devices, on_device(): lax.all_gather(flat_weights, 'dp', axis=0, tiled=True, axis_index_groups=...  36.4 us
    all_to_all x1, waiting for transfers between devices, on_device(): lax.all_to_all(tokens, 'dp', split_axis=1, concat_axis=0, tiled=True)  31 us
    ppermute x8, starting transfers between devices, shifted(): return lax.ppermute(block, axis, route)  20.3 us
    ppermute x8, waiting for transfers between devices, shifted(): return lax.ppermute(block, axis, route)  14.5 us
    all_gather x1, waiting for transfers between devices, on_device(): lax.all_gather(dqkv[None], 'dp', axis=0, tiled=True, axis_index_groups=[r...  12.6 us
    unnamed x29, local copies, waits for them, and re-layouts  9.29 us
    all_to_all x1, starting transfers between devices, on_device(): lax.all_to_all(tokens, 'dp', split_axis=1, concat_axis=0, tiled=True)  7.75 us
  transfers between devices with their start and end apart: 12, of which 8 were waited for; matrix products, arithmetic and copies ran while one was open for 17% of the time, Pallas kernels for 0%

profile of v9, /device:TPU:97, one launch (start us, length us, event | category | flops | bytes accessed | tf_op | source)
XLA Modules:
  0.0 270.9 jit_solution(16988979114056407919)
XLA Ops:
  7.2 2.2 copy.97
  10.6 3.3 %copy.99 = bf16[256,4096]{0,1:T(8,128)(2,1)S(1)} copy(bf16[256,4096]{1,0:T(8,128)(2,1)} %param.11) | data formatting | bytes 4194304 | tf_op args[0]
  13.9 2.4 copy.100
  16.4 7.7 %all-to-all-start = ((bf16[256,16,256]{2,0,1:T(8,128)(2,1)}), bf16[256,16,256]{2,0,1:T(8,128)(2,1)}, u32[]{:S(2)}, u32[]{:S(2)}) async-start(bf16[256,16,256]{2,0,1:T(8,128)(2,1)} %copy.100), calls=%async_computation | async-start | bytes 4194304 | tf_op jit(solution)/shard_map/all_to_all | solution.py:70
  24.4 2.5 gather_fusion.1
  28.1 2.3 pad_maximum_fusion.1
  30.4 6.4 %copy.102 = bf16[256,16,2,256]{0,3,2,1:T(8,128)(2,1)} copy(bf16[256,16,2,256]{3,0,1,2:T(8,128)(2,1)} %pad_maximum_fusion.1) | data formatting | bytes 8388608 | tf_op jit(solution)/shard_map/concatenate | solution.py:75
  37.3 31.0 %all-to-all-done = bf16[256,16,256]{2,0,1:T(8,128)(2,1)} async-done(((bf16[256,16,256]{2,0,1:T(8,128)(2,1)}), bf16[256,16,256]{2,0,1:T(8,128)(2,1)}, u32[]{:S(2)}, u32[]{:S(2)}) %all-to-all-start) | async-done | bytes 2097184 | tf_op jit(solution)/shard_map/all_to_all | solution.py:70
  68.3 2.3 gather_fusion.2
  70.5 2.1 bitcast_select_fusion.3
  72.7 2.4 pad_maximum_fusion
  75.1 36.4 %all-gather.3.cloned.1.call-done = bf16[8192,768]{1,0:T(8,128)(2,1)} async-done(((bf16[512,768]{1,0:T(8,128)(2,1)}), bf16[8192,768]{1,0:T(8,128)(2,1)}) %all-gather.3.cloned.1.call-update) | async-done | bytes 12582928 | tf_op jit(solution)/shard_map/all_gather | solution.py:67
  111.5 7.0 %fusion.15 = bf16[256,512]{1,0:T(8,128)(2,1)S(1)} fusion(bf16[256,8192]{0,1:T(8,128)(2,1)} %bitcast.142, bf16[8192,768]{1,0:T(8,128)(2,1)} %all-gather.3.cloned.1.call-done), kind=kOutput, calls=%fused_computation.40 | convolution fusion | flops 2147614720 | bytes 12845056 | tf_op jit(solution)/shard_map/dot_general | solution.py:88
  120.0 3.2 %collective-permute-start.1 = (bf16[256,2,2,128]{3,0,2,1:T(8,128)(2,1)S(1)}, bf16[256,2,2,128]{3,0,2,1:T(8,128)(2,1)S(1)}, u32[]{:S(2)}, u32[]{:S(2)}) collective-permute-start(bf16[256,2,2,128]{3,0,2,1:T(8,128)(2,1)S(1)} %copy.103), channel_id=1, source_target_pairs={{0,48},{16,64},{32,80},{48,96},{64,112},{80,128},{96,144},{112,160... | collective-permute-start | bytes 786440 | tf_op jit(solution)/shard_map/ppermute | solution.py:14
  123.3 4.8 %collective-permute-start.2 = (bf16[256,2,2,128]{3,0,2,1:T(8,128)(2,1)S(1)}, bf16[256,2,2,128]{3,0,2,1:T(8,128)(2,1)S(1)}, u32[]{:S(2)}, u32[]{:S(2)}) collective-permute-start(bf16[256,2,2,128]{3,0,2,1:T(8,128)(2,1)S(1)} %copy.103), channel_id=1, source_target_pairs={{0,32},{16,48},{32,64},{48,80},{64,96},{80,112},{96,128},{112,144}... | collective-permute-start | bytes 786440 | tf_op jit(solution)/shard_map/ppermute | solution.py:14
  128.1 5.2 %fusion.19 = bf16[256,256]{0,1:T(8,128)(2,1)S(1)} fusion(bf16[256,8192]{0,1:T(8,128)(2,1)} %bitcast.143, bf16[8192,768]{1,0:T(8,128)(2,1)} %all-gather.3.cloned.1.call-done), kind=kOutput, calls=%fused_computation.43 | convolution fusion | flops 1073807360 | bytes 8519680 | tf_op jit(solution)/shard_map/dot_general | solution.py:96
  133.3 4.9 %collective-permute-start.3 = (bf16[256,2,2,128]{3,0,2,1:T(8,128)(2,1)S(1)}, bf16[256,2,2,128]{3,0,2,1:T(8,128)(2,1)S(1)}, u32[]{:S(2)}, u32[]{:S(2)}) collective-permute-start(bf16[256,2,2,128]{3,0,2,1:T(8,128)(2,1)S(1)} %copy.103), channel_id=1, source_target_pairs={{0,16},{16,32},{32,48},{48,64},{64,80},{80,96},{96,112},{112,128},... | collective-permute-start | bytes 786440 | tf_op jit(solution)/shard_map/ppermute | solution.py:14
  138.3 3.0 %collective-permute-done.3 = bf16[256,2,2,128]{3,0,2,1:T(8,128)(2,1)S(1)} collective-permute-done((bf16[256,2,2,128]{3,0,2,1:T(8,128)(2,1)S(1)}, bf16[256,2,2,128]{3,0,2,1:T(8,128)(2,1)S(1)}, u32[]{:S(2)}, u32[]{:S(2)}) %collective-permute-start.3) | collective-permute-done | bytes 262176 | tf_op jit(solution)/shard_map/ppermute | solution.py:14
  142.5 2.6 fusion.35
  145.0 2.2 multiply_reduce_fusion
  147.2 2.2 multiply_convert_fusion
  152.3 2.0 fusion.13
  159.2 1.9 collective-permute-start.4
  162.7 10.3 %collective-permute-done.6 = bf16[256,2,2,128]{0,3,2,1:T(8,128)(2,1)S(1)} collective-permute-done((bf16[256,2,2,128]{0,3,2,1:T(8,128)(2,1)S(1)}, bf16[256,2,2,128]{0,3,2,1:T(8,128)(2,1)S(1)}, u32[]{:S(2)}, u32[]{:S(2)}) %collective-permute-start.6) | collective-permute-done | bytes 262176 | tf_op jit(solution)/shard_map/ppermute | solution.py:14
  175.3 4.7 %fusion.3 = f32[256,16,256]{2,0,1:T(8,128)S(1)} fusion(bf16[256,768,1]{0,1,2:T(8,128)(2,1)S(1)} %bitcast.154, bf16[16,2,256,768]{3,2,1,0:T(8,128)(2,1)} %bitcast.145), kind=kOutput, calls=%fused_computation.8 | convolution fusion | flops 1610612736 | bytes 10878976 | tf_op jit(solution)/shard_map/dot_general | solution.py:158
  180.0 4.6 %fusion.12 = bf16[16,256,256]{2,1,0:T(8,128)(2,1)S(1)} fusion(f32[256,16,256]{2,0,1:T(8,128)S(1)} %fusion.3, bf16[256,768,1]{0,1,2:T(8,128)(2,1)S(1)} %bitcast.150, bf16[16,2,256,768]{3,2,1,0:T(8,128)(2,1)} %bitcast.146), kind=kOutput, calls=%fused_computation.28 | convolution fusion | flops 1612709888 | bytes 12976128 | tf_op jit(solution)/shard_map/dot_general | solution.py:153
  184.6 2.0 gather_fusion.3
  186.6 6.8 %all-to-all-start.1 = ((bf16[16,256,256]{2,1,0:T(8,128)(2,1)}), bf16[16,256,256]{2,1,0:T(8,128)(2,1)S(1)}, u32[]{:S(2)}, u32[]{:S(2)}) async-start(bf16[16,256,256]{2,1,0:T(8,128)(2,1)} %gather_fusion.3), calls=%async_computation.1 | async-start | bytes 4194304 | tf_op jit(solution)/shard_map/all_to_all | solution.py:167
  195.8 45.1 %all-to-all-done.1 = bf16[16,256,256]{2,1,0:T(8,128)(2,1)S(1)} async-done(((bf16[16,256,256]{2,1,0:T(8,128)(2,1)}), bf16[16,256,256]{2,1,0:T(8,128)(2,1)S(1)}, u32[]{:S(2)}, u32[]{:S(2)}) %all-to-all-start.1) | async-done | bytes 2097184 | tf_op jit(solution)/shard_map/all_to_all | solution.py:167
  241.9 12.6 %all-gather.5.cloned.1.call-done = bf16[16,256,768]{2,1,0:T(8,128)(2,1)} async-done(((bf16[1,256,768]{2,1,0:T(8,128)(2,1)}), bf16[16,256,768]{2,1,0:T(8,128)(2,1)}) %all-gather.5.cloned.1.call-update) | async-done | bytes 6291472 | tf_op jit(solution)/shard_map/all_gather | solution.py:170
  254.5 7.5 %bitcast_convert_fusion = bf16[512,768]{1,0:T(8,128)(2,1)S(1)} fusion(bf16[16,256,512]{2,1,0:T(8,128)(2,1)} %bitcast.141, bf16[16,256,768]{2,1,0:T(8,128)(2,1)} %all-gather.5.cloned.1.call-done), kind=kOutput, calls=%fused_computation.33 | convolution fusion | flops 3221618688 | bytes 11272192 | tf_op jit(solution)/shard_map/dot_general | solution.py:171
  262.3 1.8 copy.130
  (71 shorter events, 21.1 us)
Async XLA Ops:
  7.2 104.3 %all-gather.3.cloned.1.call-start = ((), (), s32[]{:S(2)}) async-start(), calls=%async_computation.2 | async-start | bytes 13369344 | tf_op jit(solution)/shard_map/all_gather | solution.py:67
  16.4 7.8 %copy-start.9 = (s32[32]{0:T(128)S(1)}, s32[32]{0:T(128)}, u32[]{:S(2)}) copy-start(s32[32]{0:T(128)} %param.13) | copy-start | bytes 388
  16.4 8.0 %copy-start.8 = (s32[16]{0:T(128)S(1)}, s32[16]{0:T(128)}, u32[]{:S(2)}) copy-start(s32[16]{0:T(128)} %constant.77.clone) | copy-start | bytes 196
  16.4 51.9 %all-to-all-start = ((bf16[256,16,256]{2,0,1:T(8,128)(2,1)}), bf16[256,16,256]{2,0,1:T(8,128)(2,1)}, u32[]{:S(2)}, u32[]{:S(2)}) async-start(bf16[256,16,256]{2,0,1:T(8,128)(2,1)} %copy.100), calls=%async_computation | async-start | bytes 4194304 | tf_op jit(solution)/shard_map/all_to_all | solution.py:70
  24.1 230.4 %all-gather.5.cloned.1.call-start = ((), (), s32[]{:S(2)}) async-start(), calls=%async_computation.3 | async-start | bytes 6684672 | tf_op jit(solution)/shard_map/all_gather | solution.py:170
  30.4 6.4 %copy-start.6 = (s32[4096]{0:T(1024)S(1)}, s32[4096]{0:T(1024)}, u32[]{:S(2)}) copy-start(s32[4096]{0:T(1024)} %param.14) | copy-start | bytes 49156
  30.4 6.5 %copy-start.5 = (bf16[256,256]{1,0:T(8,128)(2,1)S(1)}, bf16[256,256]{1,0:T(8,128)(2,1)}, u32[]{:S(2)}) copy-start(bf16[256,256]{1,0:T(8,128)(2,1)} %param.15) | copy-start | bytes 393220
  118.6 19.6 %collective-permute-start = (bf16[256,2,2,128]{3,0,2,1:T(8,128)(2,1)S(1)}, bf16[256,2,2,128]{3,0,2,1:T(8,128)(2,1)S(1)}, u32[]{:S(2)}, u32[]{:S(2)}) collective-permute-start(bf16[256,2,2,128]{3,0,2,1:T(8,128)(2,1)S(1)} %copy.103), channel_id=1, source_target_pairs={{0,64},{16,80},{32,96},{48,112},{64,128},{80,144},{96,160},{112,17... | collective-permute-start | bytes 786440 | tf_op jit(solution)/shard_map/ppermute | solution.py:14
  120.0 18.2 %collective-permute-start.1 = (bf16[256,2,2,128]{3,0,2,1:T(8,128)(2,1)S(1)}, bf16[256,2,2,128]{3,0,2,1:T(8,128)(2,1)S(1)}, u32[]{:S(2)}, u32[]{:S(2)}) collective-permute-start(bf16[256,2,2,128]{3,0,2,1:T(8,128)(2,1)S(1)} %copy.103), channel_id=1, source_target_pairs={{0,48},{16,64},{32,80},{48,96},{64,112},{80,128},{96,144},{112,160... | collective-permute-start | bytes 786440 | tf_op jit(solution)/shard_map/ppermute | solution.py:14
  123.3 15.0 %collective-permute-start.2 = (bf16[256,2,2,128]{3,0,2,1:T(8,128)(2,1)S(1)}, bf16[256,2,2,128]{3,0,2,1:T(8,128)(2,1)S(1)}, u32[]{:S(2)}, u32[]{:S(2)}) collective-permute-start(bf16[256,2,2,128]{3,0,2,1:T(8,128)(2,1)S(1)} %copy.103), channel_id=1, source_target_pairs={{0,32},{16,48},{32,64},{48,80},{64,96},{80,112},{96,128},{112,144}... | collective-permute-start | bytes 786440 | tf_op jit(solution)/shard_map/ppermute | solution.py:14
  133.3 8.0 %collective-permute-start.3 = (bf16[256,2,2,128]{3,0,2,1:T(8,128)(2,1)S(1)}, bf16[256,2,2,128]{3,0,2,1:T(8,128)(2,1)S(1)}, u32[]{:S(2)}, u32[]{:S(2)}) collective-permute-start(bf16[256,2,2,128]{3,0,2,1:T(8,128)(2,1)S(1)} %copy.103), channel_id=1, source_target_pairs={{0,16},{16,32},{32,48},{48,64},{64,80},{80,96},{96,112},{112,128},... | collective-permute-start | bytes 786440 | tf_op jit(solution)/shard_map/ppermute | solution.py:14
  141.4 1.1 copy-start.2
  145.0 2.2 copy-start.1
  152.3 2.0 copy-start
  154.8 6.3 %copy-start.3 = (bf16[1280,2,2,128]{3,0,2,1:T(8,128)(2,1)S(1)}, bf16[1280,2,2,128]{3,0,2,1:T(8,128)(2,1)}, u32[]{:S(2)}) copy-start(bf16[1280,2,2,128]{3,0,2,1:T(8,128)(2,1)} %copy-done.2) | copy-start | bytes 3932164
  155.2 7.5 %collective-permute-start.7 = (bf16[256,2,2,128]{0,3,2,1:T(8,128)(2,1)S(1)}, bf16[256,2,2,128]{0,3,2,1:T(8,128)(2,1)S(1)}, u32[]{:S(2)}, u32[]{:S(2)}) collective-permute-start(bf16[256,2,2,128]{0,3,2,1:T(8,128)(2,1)S(1)} %get-tuple-element.32), channel_id=1, source_target_pairs={{64,0},{80,16},{96,32},{112,48},{128,64},{144,80},{160,96},{176,11... | collective-permute-start | bytes 786440 | tf_op jit(solution)/shard_map/ppermute | solution.py:14
  156.6 16.4 %collective-permute-start.6 = (bf16[256,2,2,128]{0,3,2,1:T(8,128)(2,1)S(1)}, bf16[256,2,2,128]{0,3,2,1:T(8,128)(2,1)S(1)}, u32[]{:S(2)}, u32[]{:S(2)}) collective-permute-start(bf16[256,2,2,128]{0,3,2,1:T(8,128)(2,1)S(1)} %get-tuple-element.33), channel_id=1, source_target_pairs={{48,0},{64,16},{80,32},{96,48},{112,64},{128,80},{144,96},{160,112... | collective-permute-start | bytes 786440 | tf_op jit(solution)/shard_map/ppermute | solution.py:14
  157.9 15.1 %collective-permute-start.5 = (bf16[256,2,2,128]{0,3,2,1:T(8,128)(2,1)S(1)}, bf16[256,2,2,128]{0,3,2,1:T(8,128)(2,1)S(1)}, u32[]{:S(2)}, u32[]{:S(2)}) collective-permute-start(bf16[256,2,2,128]{0,3,2,1:T(8,128)(2,1)S(1)} %get-tuple-element.31), channel_id=1, source_target_pairs={{32,0},{48,16},{64,32},{80,48},{96,64},{112,80},{128,96},{144,112}... | collective-permute-start | bytes 786440 | tf_op jit(solution)/shard_map/ppermute | solution.py:14
  159.2 14.0 %collective-permute-start.4 = (bf16[256,2,2,128]{0,3,2,1:T(8,128)(2,1)S(1)}, bf16[256,2,2,128]{0,3,2,1:T(8,128)(2,1)S(1)}, u32[]{:S(2)}, u32[]{:S(2)}) collective-permute-start(bf16[256,2,2,128]{0,3,2,1:T(8,128)(2,1)S(1)} %get-tuple-element.30), channel_id=1, source_target_pairs={{16,0},{32,16},{48,32},{64,48},{80,64},{96,80},{112,96},{128,112},... | collective-permute-start | bytes 786440 | tf_op jit(solution)/shard_map/ppermute | solution.py:14
  173.4 1.8 copy-start.7
  175.3 4.7 %copy-start.4 = (bf16[256,3,2,128]{0,3,2,1:T(8,128)(2,1)S(1)}, bf16[256,3,2,128]{0,3,2,1:T(8,128)(2,1)}, u32[]{:S(2)}) copy-start(bf16[256,3,2,128]{0,3,2,1:T(8,128)(2,1)} %get-tuple-element.22) | copy-start | bytes 1179652
  186.6 54.3 %all-to-all-start.1 = ((bf16[16,256,256]{2,1,0:T(8,128)(2,1)}), bf16[16,256,256]{2,1,0:T(8,128)(2,1)S(1)}, u32[]{:S(2)}, u32[]{:S(2)}) async-start(bf16[16,256,256]{2,1,0:T(8,128)(2,1)} %gather_fusion.3), calls=%async_computation.1 | async-start | bytes 4194304 | tf_op jit(solution)/shard_map/all_to_all | solution.py:167
Sparse Core Ops, SparseCore 0:
  10.8 100.6 all-gather.2
  175.3 79.1 all-gather.4
